TPU v7x, 512 devices: a whole 4x8x8 slice. The times are simulated.
512 devices in a mesh: grp: 16 (over x, z_lo), ep: 32 (over y, z_hi, core).
Axes of the slice: x: 4, y: 8, z: 8 (z_hi: 2, z_lo: 4; z = z_hi * 4 + z_lo), core: 2. Of those that a mesh axis runs over, the one named last changes fastest.
Arguments:
- slot_hidden: bfloat16 [65536, 8, 768], P(('grp', 'ep')), may hold values from -6 to 6
- expert_ids: int32 [65536, 8], P(('grp', 'ep')), may hold values from 0 to 63, all different within a row; in each aligned block of 128 rows (0 to 127, 128 to 255, ...) at most 24 rows name the same one
- gate_fixed: int32 [65536, 8], P(('grp', 'ep')), may hold values from 1 to 65535
- master: float32 [64, 768, 2048], P('ep', 'grp'), may hold values from -6 to 6
- moment_one: bfloat16 [64, 768, 2048], P('ep', 'grp'), may hold values from -3 to 3
- moment_two: bfloat16 [64, 768, 2048], P('ep', 'grp'), may hold values from 0.0099487305 to 2
- gradient: bfloat16 [64, 768, 2048], P('ep', 'grp'), may hold values from -6 to 6
Outputs:
- mixed: bfloat16 [65536, 2048], P(('grp', 'ep'))
- backup: float32 [64, 768, 2048], P('ep', 'grp')
Inputs may be any that keep to these rules, and one draw needn't show every extreme that they name: `expert_ids`: in each aligned block of 128 rows (the rows of one device) no expert is named by more than 24 rows, a bound that some block reaches; the 8 experts of a row differ.
All inputs are finite; a program needn't handle non-finite values.
Results may differ from a plain program's by a relative error of at most 0.0057.
Values may be sent and summed in bfloat16 or wider, within the bound.
No kernel may reach another device: no remote copies, remote signals or barrier semaphores. Data moves between devices by JAX's collectives and lax.ppermute only.
A program may use at most 64 MiB of HBM per device.

v0:
```python
import math

import jax
import jax.numpy as jnp
from jax import lax
from jax.sharding import Mesh
from jax.sharding import PartitionSpec as P

GRP = ("grp_0", "grp_1")
GRP_EP = ("grp_0", "grp_1", "ep")


beta_one = 0.9
beta_two = 0.95
corr_one = 1.0 - 0.9**40
corr_two = 1.0 - 0.95**40
learn_rate = 0.05
decay_rate = 0.1
adam_eps = 1e-08
gate_unit = 65536.0


def from_behind(value, axis, steps):
    count = lax.axis_size(axis)
    pairs = [(source, (source + steps) % count) for source in range(count)]
    return lax.ppermute(value, axis, pairs)


def gather_axes(shard, axes, dim):
    if not axes:
        return shard
    nearer = lax.all_gather(shard, axes[-1], axis=dim, tiled=True)
    return gather_axes(nearer, axes[:-1], dim)


def cut_along(shard, dim, peers):
    dims = shard.shape
    tiles = shard.reshape(*dims[:dim], peers, dims[dim] // peers, *dims[dim + 1 :])
    return jnp.moveaxis(tiles, dim, 0)


def cut_rows(length, count):
    unit = 8 if length >= 8 * count else 1
    return [length // unit * k // count * unit for k in range(1, count)]


def laid_out(tiles, dim):
    dims = list(tiles.shape[1:])
    dims[dim] *= tiles.shape[0]
    return jnp.moveaxis(tiles, 0, dim).reshape(dims)


def exchange_in_pieces(shard, axis, pieces, split_dim, concat_dim):
    tiles = cut_along(shard, split_dim, lax.axis_size(axis))
    split_at = max(range(1, max(2, tiles.ndim - 1)), key=lambda d: tiles.shape[d])
    gathered = []
    for piece in jnp.split(tiles, cut_rows(tiles.shape[split_at], pieces), axis=split_at):
        if piece.size:
            gathered.append(lax.all_to_all(piece, axis, split_axis=0, concat_axis=0, tiled=True))
    return laid_out(jnp.concatenate(gathered, axis=split_at), concat_dim)


def adamw_step(master, moment_one, moment_two, gradient):
    widened = gradient.astype(jnp.float32)
    first_moment = beta_one * moment_one.astype(jnp.float32) + (1.0 - beta_one) * widened
    second_moment = beta_two * moment_two.astype(jnp.float32) + (1.0 - beta_two) * widened * widened
    return (
        first_moment / corr_one / (jnp.sqrt(second_moment / corr_two) + adam_eps)
        + decay_rate * master
    )


def slot_positions(ids_block, experts, capacity):
    onehot = (ids_block[:, None] == jnp.arange(experts, dtype=jnp.int32)[None, :]).astype(jnp.int32)
    before = jnp.cumsum(onehot, axis=0) - onehot
    slot_index = jnp.sum(before * onehot, axis=1)
    return ids_block * capacity + slot_index


def body(slot_hidden, expert_ids, gate_fixed, master, moment_one, moment_two, gradient):
    groups = lax.axis_size(GRP)
    ranks = lax.axis_size("ep")
    local_experts = master.shape[0]
    experts = local_experts * ranks
    tok_count, top_count, hidden_width = slot_hidden.shape
    width = master.shape[2]
    capacity = max(2, tok_count * top_count // experts + tok_count * top_count // (2 * experts))
    scaling = 1.0 / math.sqrt(hidden_width)
    step_dir = adamw_step(master, moment_one, moment_two, gradient)
    updated = master - learn_rate * step_dir
    partner_master = from_behind(master.astype(jnp.bfloat16), GRP, groups // 2).astype(master.dtype)
    partner_rest = from_behind((moment_one, moment_two, gradient), GRP, groups // 2)
    backup = adamw_step(partner_master, partner_rest[0], partner_rest[1], partner_rest[2])
    weights = updated.astype(jnp.bfloat16)
    pairs = tok_count * top_count
    positions = slot_positions(expert_ids.reshape(pairs), experts, capacity)
    outgoing = jnp.zeros((experts * capacity, hidden_width), jnp.bfloat16)
    outgoing = outgoing.at[positions].set(slot_hidden.reshape(pairs, hidden_width))
    outgoing = outgoing.reshape(experts, capacity, hidden_width)
    arrived = lax.all_to_all(outgoing, "ep", split_axis=0, concat_axis=1, tiled=True)
    gathered = gather_axes(weights, GRP, 1)
    product = jnp.einsum("erh,ehd->erd", arrived, gathered, preferred_element_type=jnp.float32)
    results = (product * scaling).astype(jnp.bfloat16)
    returned = exchange_in_pieces(results, "ep", 2, 1, 0)
    picked = returned.reshape(experts * capacity, width)[positions]
    factors = gate_fixed.reshape(pairs).astype(jnp.float32) / gate_unit
    weighted = (picked.astype(jnp.float32) * factors[:, None]).reshape(tok_count, top_count, width)
    mixed = jnp.sum(weighted, axis=1).astype(jnp.bfloat16)
    return (mixed, backup)


def solution(mesh):
    torus = Mesh(mesh.devices.reshape(4, 4, mesh.shape["ep"]), ("grp_0", "grp_1", "ep"))
    in_specs = (
        P(GRP_EP, None, None),
        P(GRP_EP, None),
        P(GRP_EP, None),
        P("ep", GRP, None),
        P("ep", GRP, None),
        P("ep", GRP, None),
        P("ep", GRP, None),
    )
    out_specs = (P(GRP_EP, None), P("ep", GRP, None))
    return jax.shard_map(body, mesh=torus, in_specs=in_specs, out_specs=out_specs, check_vma=False)
```

profile of v0, /device:TPU:21, one launch (start us, length us, event | category | flops | bytes accessed | tf_op | source)
XLA Modules:
  0.0 392.5 jit_solution(8593457974764892059)
XLA Ops:
  7.2 0.0 copy-start
  7.2 0.0 copy-start.4
  7.2 0.0 all-gather.3.cloned.1.call-start
  7.2 3.4 fusion.27
  10.6 0.0 all-gather.3.cloned.1.call-update
  10.6 0.0 all-gather.5.cloned.1.call-start
  10.7 49.0 %all-gather.3.cloned.1.call-done = bf16[2,192,2048]{2,1,0:T(8,128)(2,1)} async-done(((bf16[2,48,2048]{2,1,0:T(8,128)(2,1)}), bf16[2,192,2048]{2,1,0:T(8,128)(2,1)}) %all-gather.3.cloned.1.call-update) | async-done | bytes 1572880 | tf_op jit(solution)/shard_map/all_gather | solution.py:32
  59.7 0.0 all-gather.5.cloned.1.call-update
  59.7 0.0 copy-done.4
  59.8 0.1 copy.20
  59.9 0.1 eq.29
  59.9 0.1 eq.25
  60.1 18.0 %reduce-window.6 = s32[64,8,128]{2,1,0:T(8,128)S(1)} reduce-window(s32[64,8,128]{2,1,0:T(8,128)S(1)} %fusion.26, s32[]{:T(128)} %constant.8.clone.1), window={size=1x1x128 pad=0_0x0_0x127_0}, to_apply=%region_0.0 | reduce-window | flops 8323072 | bytes 524292 | tf_op jit(solution)/shard_map/reduce-window
  78.1 0.1 slice.10
  78.2 0.1 copy.22
  78.4 0.1 copy.23
  78.5 0.1 copy.19
  78.6 0.1 mul.75
  78.7 0.1 broadcast_add_fusion
  78.8 0.1 fusion.25
  78.9 0.0 copy-done
  78.9 6.9 %scatter_custom_fusion = bf16[1536,768]{1,0:T(8,128)(2,1)} fusion(s32[1024]{0:T(1024)S(1)} %bitcast.48, bf16[128,8,768]{2,1,0:T(8,128)(2,1)S(1)} %copy-done, bf16[]{:T(256)} %constant.14.clone.1), kind=kCustom, calls=%fused_computation.7 | custom fusion | bytes 3932162 | tf_op jit(solution)/shard_map/scatter | solution.py:98
  85.9 70.6 %all_to_all.28 = bf16[64,24,768]{2,1,0:T(8,128)(2,1)S(1)} all-to-all(bf16[64,24,768]{2,1,0:T(8,128)(2,1)} %bitcast.41), channel_id=1, replica_groups=mesh['grp_0'=4,'grp_1'=4,'ep'=32] {'ep'}, dimensions={0} | all-to-all | bytes 4718592 | tf_op jit(solution)/shard_map/all_to_all | solution.py:100
  156.4 1.6 copy.24
  158.0 7.9 %multiply_convert_fusion = bf16[2,768,2048]{2,1,0:T(8,128)(2,1)S(1)} fusion(bf16[2,768,768]{2,1,0:T(8,128)(2,1)} %bitcast.44, bf16[2,768,2048]{2,1,0:T(8,128)(2,1)} %all-gather.5.cloned.1.call-done), kind=kOutput, calls=%fused_computation.2 | convolution fusion | flops 4838129664 | bytes 14942208 | tf_op jit(solution)/shard_map/erh,ehd->erd/dot_general | solution.py:102
  165.9 1.1 copy.30
  167.0 0.0 copy-start.1
  167.0 2.7 copy-done.1
  169.7 1.5 split.8
  171.2 6.9 %all-to-all-start.1 = ((bf16[32,2,8,2048]{3,2,1,0:T(8,128)(2,1)}), bf16[32,2,8,2048]{3,2,1,0:T(8,128)(2,1)}, u32[]{:S(2)}, u32[]{:S(2)}) async-start(bf16[32,2,8,2048]{3,2,1,0:T(8,128)(2,1)} %split.8), calls=%async_computation.1 | async-start | bytes 4194304 | tf_op jit(solution)/shard_map/all_to_all | solution.py:59
  178.1 4.8 %split.9 = bf16[32,2,16,2048]{3,2,1,0:T(8,128)(2,1)} slice(bf16[32,2,24,2048]{3,2,1,0:T(8,128)(2,1)} %bitcast.40), slice={[0:32], [0:2], [8:24], [0:2048]} | slice | bytes 8388608 | tf_op jit(solution)/shard_map/split | solution.py:57
  183.0 45.7 %all-to-all-done.1 = bf16[32,2,8,2048]{3,2,1,0:T(8,128)(2,1)} async-done(((bf16[32,2,8,2048]{3,2,1,0:T(8,128)(2,1)}), bf16[32,2,8,2048]{3,2,1,0:T(8,128)(2,1)}, u32[]{:S(2)}, u32[]{:S(2)}) %all-to-all-start.1) | async-done | bytes 2097184 | tf_op jit(solution)/shard_map/all_to_all | solution.py:59
  228.6 14.3 %all-to-all-start.2 = ((bf16[32,2,16,2048]{3,2,1,0:T(8,128)(2,1)}), bf16[32,2,16,2048]{3,2,1,0:T(8,128)(2,1)}, u32[]{:S(2)}, u32[]{:S(2)}) async-start(bf16[32,2,16,2048]{3,2,1,0:T(8,128)(2,1)} %split.9), calls=%async_computation.2 | async-start | bytes 8388608 | tf_op jit(solution)/shard_map/all_to_all | solution.py:59
  242.9 0.0 copy-done.2
  242.9 1.9 collective-permute-start
  244.9 4.9 %collective-permute-start.1 = (bf16[2,48,2048]{2,1,0:T(8,128)(2,1)}, bf16[2,48,2048]{2,1,0:T(8,128)(2,1)S(1)}, u32[]{:S(2)}, u32[]{:S(2)}) collective-permute-start(bf16[2,48,2048]{2,1,0:T(8,128)(2,1)} %param.13), channel_id=1, source_target_pairs={{0,256},{32,288},{64,320},{96,352},{128,384},{160,416},{192,448},{... | collective-permute-start | bytes 1179656 | tf_op jit(solution)/shard_map/ppermute | solution.py:26
  249.8 1.9 collective-permute-start.2
  251.7 5.0 %collective-permute-start.3 = (bf16[2,48,2048]{2,1,0:T(8,128)(2,1)}, bf16[2,48,2048]{2,1,0:T(8,128)(2,1)S(1)}, u32[]{:S(2)}, u32[]{:S(2)}) collective-permute-start(bf16[2,48,2048]{2,1,0:T(8,128)(2,1)} %get-tuple-element.2), channel_id=1, source_target_pairs={{0,256},{32,288},{64,320},{96,352},{128,384},{160,416},{192,448},{... | collective-permute-start | bytes 1179656 | tf_op jit(solution)/shard_map/ppermute | solution.py:26
  256.8 0.7 copy.26
  257.5 24.6 %collective-permute-done.3 = bf16[2,48,2048]{2,1,0:T(8,128)(2,1)S(1)} collective-permute-done((bf16[2,48,2048]{2,1,0:T(8,128)(2,1)}, bf16[2,48,2048]{2,1,0:T(8,128)(2,1)S(1)}, u32[]{:S(2)}, u32[]{:S(2)}) %collective-permute-start.3) | collective-permute-done | bytes 393248 | tf_op jit(solution)/shard_map/ppermute | solution.py:26
  282.1 0.0 collective-permute-done
  282.1 0.0 collective-permute-done.1
  282.1 0.0 collective-permute-done.2
  282.1 1.5 fusion.13
  283.6 75.7 %all-to-all-done.2 = bf16[32,2,16,2048]{3,2,1,0:T(8,128)(2,1)} async-done(((bf16[32,2,16,2048]{3,2,1,0:T(8,128)(2,1)}), bf16[32,2,16,2048]{3,2,1,0:T(8,128)(2,1)}, u32[]{:S(2)}, u32[]{:S(2)}) %all-to-all-start.2) | async-done | bytes 4194336 | tf_op jit(solution)/shard_map/all_to_all | solution.py:59
  359.3 6.7 %pad_maximum_fusion = bf16[32,2,24,2048]{3,2,1,0:T(8,128)(2,1)} fusion(bf16[32,2,16,2048]{3,2,1,0:T(8,128)(2,1)} %all-to-all-done.2, bf16[32,2,8,2048]{3,2,1,0:T(8,128)(2,1)} %all-to-all-done.1), kind=kLoop, calls=%fused_computation.5 | loop fusion | flops 12582912 | bytes 12582912 | tf_op jit(solution)/shard_map/concatenate | solution.py:60
  366.0 12.4 %gather_fusion = bf16[1024,2048]{1,0:T(8,128)(2,1)} fusion(bf16[1536,2048]{1,0:T(8,128)(2,1)} %bitcast.38, s32[1024]{0:T(1024)S(1)} %broadcast_clamp_fusion), kind=kCustom, calls=%fused_computation | custom fusion | bytes 8392704 | tf_op jit(solution)/shard_map/gather | solution.py:105
  378.4 7.3 %fusion = bf16[128,2048]{1,0:T(8,128)(2,1)} fusion(bf16[1024,2048]{1,0:T(8,128)(2,1)} %gather_fusion, f32[128,8]{1,0:T(8,128)S(1)} %copy-done.3), kind=kLoop, calls=%fused_computation.4 | loop fusion | flops 6029312 | bytes 4722688 | tf_op jit(solution)/shard_map/reduce_sum | solution.py:108
  (13 shorter events, 0.1 us)
Async XLA Ops:
  7.2 71.8 %copy-start = (bf16[128,8,768]{2,1,0:T(8,128)(2,1)S(1)}, bf16[128,8,768]{2,1,0:T(8,128)(2,1)}, u32[]{:S(2)}) copy-start(bf16[128,8,768]{2,1,0:T(8,128)(2,1)} %param.7) | copy-start | bytes 4718596
  7.2 52.6 %copy-start.4 = (s32[128,8]{0,1:T(8,128)S(1)}, s32[128,8]{0,1:T(8,128)}, u32[]{:S(2)}) copy-start(s32[128,8]{0,1:T(8,128)} %param.8) | copy-start | bytes 12292
  7.2 52.5 %all-gather.3.cloned.1.call-start = ((), (), s32[]{:S(2)}) async-start(), calls=%async_computation.3 | async-start | bytes 1966080 | tf_op jit(solution)/shard_map/all_gather | solution.py:32
  10.6 147.4 %all-gather.5.cloned.1.call-start = ((), (), s32[]{:S(2)}) async-start(), calls=%async_computation.4 | async-start | bytes 7864320 | tf_op jit(solution)/shard_map/all_gather | solution.py:32
  167.0 2.7 copy-start.1
  171.2 57.4 %all-to-all-start.1 = ((bf16[32,2,8,2048]{3,2,1,0:T(8,128)(2,1)}), bf16[32,2,8,2048]{3,2,1,0:T(8,128)(2,1)}, u32[]{:S(2)}, u32[]{:S(2)}) async-start(bf16[32,2,8,2048]{3,2,1,0:T(8,128)(2,1)} %split.8), calls=%async_computation.1 | async-start | bytes 4194304 | tf_op jit(solution)/shard_map/all_to_all | solution.py:59
  182.9 60.0 %copy-start.2 = (bf16[2,48,2048]{2,1,0:T(8,128)(2,1)S(1)}, bf16[2,48,2048]{2,1,0:T(8,128)(2,1)}, u32[]{:S(2)}) copy-start(bf16[2,48,2048]{2,1,0:T(8,128)(2,1)} %param.11) | copy-start | bytes 1179652
  183.0 73.8 %copy-start.5 = (s32[128,8]{0,1:T(8,128)S(1)}, s32[128,8]{0,1:T(8,128)}, u32[]{:S(2)}) copy-start(s32[128,8]{0,1:T(8,128)} %param.9) | copy-start | bytes 12292
  228.6 130.7 %all-to-all-start.2 = ((bf16[32,2,16,2048]{3,2,1,0:T(8,128)(2,1)}), bf16[32,2,16,2048]{3,2,1,0:T(8,128)(2,1)}, u32[]{:S(2)}, u32[]{:S(2)}) async-start(bf16[32,2,16,2048]{3,2,1,0:T(8,128)(2,1)} %split.9), calls=%async_computation.2 | async-start | bytes 8388608 | tf_op jit(solution)/shard_map/all_to_all | solution.py:59
  242.9 39.1 %collective-permute-start = (bf16[2,48,2048]{2,1,0:T(8,128)(2,1)S(1)}, bf16[2,48,2048]{2,1,0:T(8,128)(2,1)S(1)}, u32[]{:S(2)}, u32[]{:S(2)}) collective-permute-start(bf16[2,48,2048]{2,1,0:T(8,128)(2,1)S(1)} %copy-done.2), channel_id=1, source_target_pairs={{0,256},{32,288},{64,320},{96,352},{128,384},{160,416},{192,448},{... | collective-permute-start | bytes 1179656 | tf_op jit(solution)/shard_map/ppermute | solution.py:26
  244.9 37.2 %collective-permute-start.1 = (bf16[2,48,2048]{2,1,0:T(8,128)(2,1)}, bf16[2,48,2048]{2,1,0:T(8,128)(2,1)S(1)}, u32[]{:S(2)}, u32[]{:S(2)}) collective-permute-start(bf16[2,48,2048]{2,1,0:T(8,128)(2,1)} %param.13), channel_id=1, source_target_pairs={{0,256},{32,288},{64,320},{96,352},{128,384},{160,416},{192,448},{... | collective-permute-start | bytes 1179656 | tf_op jit(solution)/shard_map/ppermute | solution.py:26
  249.8 32.3 %collective-permute-start.2 = (bf16[2,48,2048]{2,1,0:T(8,128)(2,1)}, bf16[2,48,2048]{2,1,0:T(8,128)(2,1)S(1)}, u32[]{:S(2)}, u32[]{:S(2)}) collective-permute-start(bf16[2,48,2048]{2,1,0:T(8,128)(2,1)} %param.12), channel_id=1, source_target_pairs={{0,256},{32,288},{64,320},{96,352},{128,384},{160,416},{192,448},{... | collective-permute-start | bytes 1179656 | tf_op jit(solution)/shard_map/ppermute | solution.py:26
  251.7 30.4 %collective-permute-start.3 = (bf16[2,48,2048]{2,1,0:T(8,128)(2,1)}, bf16[2,48,2048]{2,1,0:T(8,128)(2,1)S(1)}, u32[]{:S(2)}, u32[]{:S(2)}) collective-permute-start(bf16[2,48,2048]{2,1,0:T(8,128)(2,1)} %get-tuple-element.2), channel_id=1, source_target_pairs={{0,256},{32,288},{64,320},{96,352},{128,384},{160,416},{192,448},{... | collective-permute-start | bytes 1179656 | tf_op jit(solution)/shard_map/ppermute | solution.py:26
  366.0 12.4 %copy-start.3 = (f32[128,8]{1,0:T(8,128)S(1)}, f32[128,8]{1,0:T(8,128)}, u32[]{:S(2)}) copy-start(f32[128,8]{1,0:T(8,128)} %copy.26) | copy-start | bytes 12292
Sparse Core Ops, SparseCore 0:
  10.7 48.9 all-gather.2
  61.8 69.9 all-gather.4
where the time goes:
time: 393 us
  waiting for transfers between devices  195 us (50%)
  blocking collectives  70.6 us (18%)
  other arithmetic  37.1 us (9%)
  starting transfers between devices  35.1 us (9%)
  local copies, waits for them, and re-layouts  32.7 us (8%)
  between operations  14.2 us (4%)
  matrix products  7.85 us (2%)
    all_to_all x2, waiting for transfers between devices, exchange_in_pieces(): lax.all_to_all(piece, axis, split_axis=0, concat_axis=0, tiled=True)  121 us
    all_to_all x1, blocking collectives, body(): lax.all_to_all(outgoing, 'ep', split_axis=0, concat_axis=1, tiled=True)  70.6 us
    all_gather x2, waiting for transfers between devices, gather_axes(): nearer = lax.all_gather(shard, axes[-1], axis=dim, tiled=True)  49 us
    ppermute x4, waiting for transfers between devices, from_behind(): return lax.ppermute(value, axis, pairs)  24.6 us
    all_to_all x2, starting transfers between devices, exchange_in_pieces(): lax.all_to_all(piece, axis, split_axis=0, concat_axis=0, tiled=True)  21.2 us
    another operation x3, other arithmetic  18.2 us
    ppermute x4, starting transfers between devices, from_behind(): return lax.ppermute(value, axis, pairs)  13.8 us
    gather x1, local copies, waits for them, and re-layouts, body(): picked = returned.reshape(experts * capacity, width)[positions]  12.4 us
  transfers between devices with their start and end apart: 8, of which 4 were waited for; matrix products, arithmetic and copies ran while one was open for 9% of the time, Pallas kernels for 0%

commit v1 on v0

v1 whole, which is shorter than its diff:
```python
import math

import jax
import jax.numpy as jnp
from jax import lax
from jax.sharding import PartitionSpec as P

beta_one = 0.9
beta_two = 0.95
corr_one = 1.0 - 0.9**40
corr_two = 1.0 - 0.95**40
learn_rate = 0.05
decay_rate = 0.1
adam_eps = 1e-08
gate_unit = 65536.0


def adamw_step(master, moment_one, moment_two, gradient):
    widened = gradient.astype(jnp.float32)
    first_moment = beta_one * moment_one.astype(jnp.float32) + (1.0 - beta_one) * widened
    second_moment = beta_two * moment_two.astype(jnp.float32) + (1.0 - beta_two) * widened * widened
    return (
        first_moment / corr_one / (jnp.sqrt(second_moment / corr_two) + adam_eps)
        + decay_rate * master
    )


def slot_positions(ids, capacity):
    count = ids.shape[0]
    rows = lax.broadcasted_iota(jnp.int32, (count, count), 0)
    cols = lax.broadcasted_iota(jnp.int32, (count, count), 1)
    same = (ids[:, None] == ids[None, :]) & (cols < rows)
    slot_index = jnp.sum(same.astype(jnp.int32), axis=1)
    return ids * capacity + slot_index


def body(slot_hidden, expert_ids, gate_fixed, master, moment_one, moment_two, gradient):
    groups = lax.axis_size("grp")
    ranks = lax.axis_size("ep")
    local_experts = master.shape[0]
    experts = local_experts * ranks
    tok_count, top_count, hidden_width = slot_hidden.shape
    width = master.shape[2]
    capacity = max(2, tok_count * top_count // experts + tok_count * top_count // (2 * experts))
    slots = experts * capacity
    scaling = 1.0 / math.sqrt(hidden_width)

    step_dir = adamw_step(master, moment_one, moment_two, gradient)
    updated = master - learn_rate * step_dir
    weights = updated.astype(jnp.bfloat16)
    gathered = lax.all_gather(weights, "grp", axis=1, tiled=True)

    shift = groups // 2
    backup = lax.ppermute(step_dir, "grp", [(s, (s + shift) % groups) for s in range(groups)])

    pairs = tok_count * top_count
    positions = slot_positions(expert_ids.reshape(pairs), capacity)
    slot_ids = lax.broadcasted_iota(jnp.int32, (slots, pairs), 0)
    placing = (positions[None, :] == slot_ids).astype(jnp.bfloat16)
    outgoing = jnp.dot(placing, slot_hidden.reshape(pairs, hidden_width),
                       preferred_element_type=jnp.float32).astype(jnp.bfloat16)
    outgoing = outgoing.reshape(experts, capacity, hidden_width)
    arrived = lax.all_to_all(outgoing, "ep", split_axis=0, concat_axis=1, tiled=True)

    product = jnp.einsum("erh,ehd->erd", arrived, gathered, preferred_element_type=jnp.float32)
    results = (product * scaling).astype(jnp.bfloat16)
    tiles = results.reshape(local_experts, ranks, capacity, width).transpose(1, 0, 2, 3)
    returned = lax.all_to_all(tiles, "ep", split_axis=0, concat_axis=0, tiled=True)
    returned = returned.reshape(slots, width)

    factors = gate_fixed.astype(jnp.float32) / gate_unit
    token_pos = positions.reshape(tok_count, top_count)
    slot_row = lax.broadcasted_iota(jnp.int32, (tok_count, top_count, slots), 2)
    combine = jnp.sum(jnp.where(token_pos[:, :, None] == slot_row, factors[:, :, None], 0.0), axis=1)
    combine_hi = combine.astype(jnp.bfloat16)
    combine_lo = (combine - combine_hi.astype(jnp.float32)).astype(jnp.bfloat16)
    mixed = jnp.dot(combine_hi, returned, preferred_element_type=jnp.float32) + jnp.dot(
        combine_lo, returned, preferred_element_type=jnp.float32)
    return (mixed.astype(jnp.bfloat16), backup)


def solution(mesh):
    tokens = P(("grp", "ep"), None, None)
    pair_spec = P(("grp", "ep"), None)
    state = P("ep", "grp", None)
    in_specs = (tokens, pair_spec, pair_spec, state, state, state, state)
    out_specs = (pair_spec, state)
    return jax.shard_map(body, mesh=mesh, in_specs=in_specs, out_specs=out_specs, check_vma=False)
```

time: 393 us -> 427 us (1.087)
  waiting for transfers between devices: 195 us -> 290 us
  other arithmetic: 37.1 us -> 5.84 us
  local copies, waits for them, and re-layouts: 32.7 us -> 6.93 us
  starting transfers between devices: 35.1 us -> 15.2 us
  matrix products: 7.85 us -> 19.3 us
  blocking collectives: 70.6 us -> 75.1 us
    all_gather x2 -> x1, waiting for transfers between devices: 49 us -> 119 us  [body(): gathered = lax.all_gather(weights, 'grp', axis=1, tiled=True)]
    all_to_all x2 -> x1, waiting for transfers between devices: 121 us -> 155 us  [body(): lax.all_to_all(tiles, 'ep', split_axis=0, concat_axis=0, tiled=True)]
    another operation x3 -> x0, other arithmetic: 18.2 us -> none
    gather x1 -> x0, local copies, waits for them, and re-layouts: 12.4 us -> none  [body(): picked = returned.reshape(experts * capacity, width)[positions]]
    dot_general x0 -> x3, matrix products: none -> 11.5 us  [the longest x1 4.65 us: body(): jnp.dot(combine_lo, returned, preferred_element_type=jnp.float32)]
    all_to_all x2 -> x1, starting transfers between devices: 21.2 us -> 11.1 us  [body(): lax.all_to_all(tiles, 'ep', split_axis=0, concat_axis=0, tiled=True)]
    ppermute x4 -> x1, starting transfers between devices: 13.8 us -> 4.06 us  [body(): lax.ppermute(step_dir, 'grp', [(s, (s + shift) % groups) for s in range(g...]
    ppermute x4 -> x1, waiting for transfers between devices: 24.6 us -> 16 us  [body(): lax.ppermute(step_dir, 'grp', [(s, (s + shift) % groups) for s in range(g...]
  transfers between devices with their start and end apart: 8 -> 3, of which waited for: 4 -> 3; matrix products, arithmetic and copies ran while one was open for 9% -> 2% of each run, Pallas kernels for 0% -> 0%
where the time goes in v1:
time: 427 us; the launch traced here: 426 us
  waiting for transfers between devices  290 us (68%)
  blocking collectives  75.1 us (18%)
  matrix products  19.3 us (5%)
  starting transfers between devices  15.2 us (4%)
  between operations  14.1 us (3%)
  local copies, waits for them, and re-layouts  6.93 us (2%)
  other arithmetic  5.84 us (1%)
    all_to_all x1, waiting for transfers between devices, body(): lax.all_to_all(tiles, 'ep', split_axis=0, concat_axis=0, tiled=True)  155 us
    all_gather x1, waiting for transfers between devices, body(): gathered = lax.all_gather(weights, 'grp', axis=1, tiled=True)  119 us
    all_to_all x1, blocking collectives, body(): lax.all_to_all(outgoing, 'ep', split_axis=0, concat_axis=1, tiled=True)  75.1 us
    ppermute x1, waiting for transfers between devices, body(): lax.ppermute(step_dir, 'grp', [(s, (s + shift) % groups) for s in range(g...  16 us
    all_to_all x1, starting transfers between devices, body(): lax.all_to_all(tiles, 'ep', split_axis=0, concat_axis=0, tiled=True)  11.1 us
  transfers between devices with their start and end apart: 3, of which 3 were waited for; matrix products, arithmetic and copies ran while one was open for 2% of the time, Pallas kernels for 0%

profile of v1, /device:TPU:21, one launch (start us, length us, event | category | flops | bytes accessed | tf_op | source)
XLA Modules:
  0.0 426.3 jit_solution(7426811078113007954)
XLA Ops:
  7.2 0.0 copy-start
  7.2 0.0 all-gather.2.cloned.1.call-start
  7.2 3.3 subtract_convert_fusion.1
  10.5 0.0 all-gather.2.cloned.1.call-update
  10.5 0.8 copy.24
  11.3 0.1 eq.31
  11.4 0.5 convert_reduce_fusion
  11.9 0.0 copy-done
  11.9 3.0 fusion.2
  15.0 75.1 %all_to_all.23 = bf16[64,24,768]{2,1,0:T(8,128)(2,1)S(1)} all-to-all(bf16[64,24,768]{2,1,0:T(8,128)(2,1)S(1)} %bitcast.21), channel_id=1, replica_groups=mesh['grp'=16,'ep'=32] {'ep'}, dimensions={0} | all-to-all | bytes 4718592 | tf_op jit(solution)/shard_map/all_to_all | solution.py:63
  90.1 1.6 copy.28
  91.6 118.8 %all-gather.2.cloned.1.call-done = bf16[2,768,2048]{2,1,0:T(8,128)(2,1)} async-done(((bf16[2,48,2048]{2,1,0:T(8,128)(2,1)}), bf16[2,768,2048]{2,1,0:T(8,128)(2,1)}) %all-gather.2.cloned.1.call-update) | async-done | bytes 6291472 | tf_op jit(solution)/shard_map/all_gather | solution.py:51
  210.5 7.9 %multiply_convert_fusion = bf16[2,768,2048]{2,1,0:T(8,128)(2,1)S(1)} fusion(bf16[2,768,768]{2,1,0:T(8,128)(2,1)} %bitcast.20, bf16[2,768,2048]{2,1,0:T(8,128)(2,1)} %all-gather.2.cloned.1.call-done), kind=kOutput, calls=%fused_computation | convolution fusion | flops 4838129664 | bytes 14942208 | tf_op jit(solution)/shard_map/erh,ehd->erd/dot_general | solution.py:65
  218.3 3.2 copy.31
  221.6 0.0 copy-start.1
  221.6 0.0 copy-start.2
  221.6 11.1 %all-to-all-start.1 = ((bf16[32,2,24,2048]{3,2,1,0:T(8,128)(2,1)}), bf16[32,2,24,2048]{3,2,1,0:T(8,128)(2,1)}, u32[]{:S(2)}, u32[]{:S(2)}) async-start(bf16[32,2,24,2048]{3,2,1,0:T(8,128)(2,1)} %bitcast.17), calls=%async_computation.1 | async-start | bytes 12582912 | tf_op jit(solution)/shard_map/all_to_all | solution.py:68
  232.7 4.1 collective-permute-start
  236.7 0.1 reduce_sum.21
  236.9 0.0 copy-done.1
  236.9 0.1 copy.26
  237.0 0.0 copy-done.2
  237.0 0.1 copy.27
  237.1 2.0 select_reduce_fusion
  239.2 16.0 %collective-permute-done = f32[2,48,2048]{2,1,0:T(8,128)S(1)} collective-permute-done((f32[2,48,2048]{2,1,0:T(8,128)}, f32[2,48,2048]{2,1,0:T(8,128)S(1)}, u32[]{:S(2)}, u32[]{:S(2)}) %collective-permute-start) | collective-permute-done | bytes 786464 | tf_op jit(solution)/shard_map/ppermute | solution.py:54
  255.1 155.0 %all-to-all-done.1 = bf16[32,2,24,2048]{3,2,1,0:T(8,128)(2,1)} async-done(((bf16[32,2,24,2048]{3,2,1,0:T(8,128)(2,1)}), bf16[32,2,24,2048]{3,2,1,0:T(8,128)(2,1)}, u32[]{:S(2)}, u32[]{:S(2)}) %all-to-all-start.1) | async-done | bytes 6291488 | tf_op jit(solution)/shard_map/all_to_all | solution.py:68
  410.1 3.8 fusion.15
  413.9 4.7 %fusion.4 = bf16[128,2048]{1,0:T(8,128)(2,1)} fusion(f32[128,2048]{1,0:T(8,128)S(1)} %fusion.15, bf16[1536,2048]{1,0:T(8,128)(2,1)} %bitcast.7, f32[128,1536]{1,0:T(8,128)S(1)} %select_reduce_fusion), kind=kOutput, calls=%fused_computation.12 | convolution fusion | flops 806617088 | bytes 8650752 | tf_op jit(solution)/shard_map/dot_general | solution.py:77
  418.6 0.9 copy.33
  (4 shorter events, 0.1 us)
Async XLA Ops:
  7.2 4.8 %copy-start = (bf16[128,8,768]{2,1,0:T(8,128)(2,1)S(1)}, bf16[128,8,768]{2,1,0:T(8,128)(2,1)}, u32[]{:S(2)}) copy-start(bf16[128,8,768]{2,1,0:T(8,128)(2,1)} %param.7) | copy-start | bytes 4718596
  7.2 203.3 %all-gather.2.cloned.1.call-start = ((), (), s32[]{:S(2)}) async-start(), calls=%async_computation.2 | async-start | bytes 6684672 | tf_op jit(solution)/shard_map/all_gather | solution.py:51
  221.6 15.3 %copy-start.1 = (s32[128,8]{0,1:T(8,128)S(1)}, s32[128,8]{0,1:T(8,128)}, u32[]{:S(2)}) copy-start(s32[128,8]{0,1:T(8,128)} %param.8) | copy-start | bytes 12292
  221.6 15.4 %copy-start.2 = (s32[128,8]{0,1:T(8,128)S(1)}, s32[128,8]{0,1:T(8,128)}, u32[]{:S(2)}) copy-start(s32[128,8]{0,1:T(8,128)} %param.9) | copy-start | bytes 12292
  221.6 188.5 %all-to-all-start.1 = ((bf16[32,2,24,2048]{3,2,1,0:T(8,128)(2,1)}), bf16[32,2,24,2048]{3,2,1,0:T(8,128)(2,1)}, u32[]{:S(2)}, u32[]{:S(2)}) async-start(bf16[32,2,24,2048]{3,2,1,0:T(8,128)(2,1)} %bitcast.17), calls=%async_computation.1 | async-start | bytes 12582912 | tf_op jit(solution)/shard_map/all_to_all | solution.py:68
  232.7 22.5 %collective-permute-start = (f32[2,48,2048]{2,1,0:T(8,128)}, f32[2,48,2048]{2,1,0:T(8,128)S(1)}, u32[]{:S(2)}, u32[]{:S(2)}) collective-permute-start(f32[2,48,2048]{2,1,0:T(8,128)} %get-tuple-element.3), channel_id=1, source_target_pairs={{0,256},{32,288},{64,320},{96,352},{128,384},{160,416},{192,448},{... | collective-permute-start | bytes 2359304 | tf_op jit(solution)/shard_map/ppermute | solution.py:54
Sparse Core Ops, SparseCore 0:
  10.7 199.7 all-gather.1

commit v2 on v1

--- a/solution.py
+++ b/solution.py
@@ -3,7 +3,10 @@
 import jax
 import jax.numpy as jnp
 from jax import lax
+from jax.sharding import Mesh
 from jax.sharding import PartitionSpec as P
+
+GRP = ("grp_0", "grp_1")
 
 beta_one = 0.9
 beta_two = 0.95
@@ -35,7 +38,7 @@
 
 
 def body(slot_hidden, expert_ids, gate_fixed, master, moment_one, moment_two, gradient):
-    groups = lax.axis_size("grp")
+    outer = lax.axis_size("grp_0")
     ranks = lax.axis_size("ep")
     local_experts = master.shape[0]
     experts = local_experts * ranks
@@ -48,10 +51,11 @@
     step_dir = adamw_step(master, moment_one, moment_two, gradient)
     updated = master - learn_rate * step_dir
     weights = updated.astype(jnp.bfloat16)
-    gathered = lax.all_gather(weights, "grp", axis=1, tiled=True)
+    nearer = lax.all_gather(weights, "grp_1", axis=1, tiled=True)
+    gathered = lax.all_gather(nearer, "grp_0", axis=1, tiled=True)
 
-    shift = groups // 2
-    backup = lax.ppermute(step_dir, "grp", [(s, (s + shift) % groups) for s in range(groups)])
+    shift = outer // 2
+    backup = lax.ppermute(step_dir, "grp_0", [(s, (s + shift) % outer) for s in range(outer)])
 
     pairs = tok_count * top_count
     positions = slot_positions(expert_ids.reshape(pairs), capacity)
@@ -65,24 +69,33 @@
     product = jnp.einsum("erh,ehd->erd", arrived, gathered, preferred_element_type=jnp.float32)
     results = (product * scaling).astype(jnp.bfloat16)
     tiles = results.reshape(local_experts, ranks, capacity, width).transpose(1, 0, 2, 3)
-    returned = lax.all_to_all(tiles, "ep", split_axis=0, concat_axis=0, tiled=True)
-    returned = returned.reshape(slots, width)
 
-    factors = gate_fixed.astype(jnp.float32) / gate_unit
+    high = (gate_fixed // 256).astype(jnp.float32) / 256.0
+    low = (gate_fixed % 256).astype(jnp.float32) / gate_unit
     token_pos = positions.reshape(tok_count, top_count)
     slot_row = lax.broadcasted_iota(jnp.int32, (tok_count, top_count, slots), 2)
-    combine = jnp.sum(jnp.where(token_pos[:, :, None] == slot_row, factors[:, :, None], 0.0), axis=1)
-    combine_hi = combine.astype(jnp.bfloat16)
-    combine_lo = (combine - combine_hi.astype(jnp.float32)).astype(jnp.bfloat16)
-    mixed = jnp.dot(combine_hi, returned, preferred_element_type=jnp.float32) + jnp.dot(
-        combine_lo, returned, preferred_element_type=jnp.float32)
+    hit = token_pos[:, :, None] == slot_row
+    combine_hi = jnp.sum(jnp.where(hit, high[:, :, None], 0.0), axis=1).astype(jnp.bfloat16)
+    combine_lo = jnp.sum(jnp.where(hit, low[:, :, None], 0.0), axis=1).astype(jnp.bfloat16)
+    combine_hi = combine_hi.reshape(tok_count, experts, capacity)
+    combine_lo = combine_lo.reshape(tok_count, experts, capacity)
+
+    mixed = jnp.zeros((tok_count, width), jnp.float32)
+    half = capacity // 2
+    for start, stop in ((0, half), (half, capacity)):
+        piece = lax.all_to_all(tiles[:, :, start:stop], "ep", split_axis=0, concat_axis=0, tiled=True)
+        piece = piece.reshape(experts * (stop - start), width)
+        for part in (combine_hi, combine_lo):
+            weight = part[:, :, start:stop].reshape(tok_count, experts * (stop - start))
+            mixed = mixed + jnp.dot(weight, piece, preferred_element_type=jnp.float32)
     return (mixed.astype(jnp.bfloat16), backup)
 
 
 def solution(mesh):
-    tokens = P(("grp", "ep"), None, None)
-    pair_spec = P(("grp", "ep"), None)
-    state = P("ep", "grp", None)
+    torus = Mesh(mesh.devices.reshape(4, 4, mesh.shape["ep"]), ("grp_0", "grp_1", "ep"))
+    tokens = P(GRP + ("ep",), None, None)
+    pair_spec = P(GRP + ("ep",), None)
+    state = P("ep", GRP, None)
     in_specs = (tokens, pair_spec, pair_spec, state, state, state, state)
     out_specs = (pair_spec, state)
-    return jax.shard_map(body, mesh=mesh, in_specs=in_specs, out_specs=out_specs, check_vma=False)
+    return jax.shard_map(body, mesh=torus, in_specs=in_specs, out_specs=out_specs, check_vma=False)

time: 427 us -> 364 us (0.85)
  the two profiles are of different devices: /device:TPU:21 before, /device:TPU:56 now
where the time goes in v2:
time: 364 us; the launch traced here: 363 us
  blocking collectives  156 us (43%)
  waiting for transfers between devices  102 us (28%)
  local copies, waits for them, and re-layouts  54.1 us (15%)
  starting transfers between devices  14.3 us (4%)
  matrix products  14.3 us (4%)
  between operations  14.2 us (4%)
  other arithmetic  8.75 us (2%)
    all_to_all x1, blocking collectives, body(): lax.all_to_all(tiles[:, :, start:stop], 'ep', split_axis=0, concat_axis=0...  86.7 us
    all_to_all x1, blocking collectives, body(): lax.all_to_all(outgoing, 'ep', split_axis=0, concat_axis=1, tiled=True)  69 us
    all_to_all x1, waiting for transfers between devices, body(): lax.all_to_all(tiles[:, :, start:stop], 'ep', split_axis=0, concat_axis=0...  49.5 us
    all_gather x1, waiting for transfers between devices, body(): nearer = lax.all_gather(weights, 'grp_1', axis=1, tiled=True)  48.9 us
    reshape x1, local copies, waits for them, and re-layouts, body(): results.reshape(local_experts, ranks, capacity, width).transpose(1, 0, 2, 3)  13.5 us
    reshape x2, local copies, waits for them, and re-layouts, body(): piece = piece.reshape(experts * (stop - start), width)  10.9 us
    all_to_all x1, starting transfers between devices, body(): lax.all_to_all(tiles[:, :, start:stop], 'ep', split_axis=0, concat_axis=0...  9.78 us
    all_to_all x2, local copies, waits for them, and re-layouts, body(): lax.all_to_all(tiles[:, :, start:stop], 'ep', split_axis=0, concat_axis=0...  8.99 us
  transfers between devices with their start and end apart: 4, of which 3 were waited for; matrix products, arithmetic and copies ran while one was open for 8% of the time, Pallas kernels for 0%

profile of v2, /device:TPU:56, one launch (start us, length us, event | category | flops | bytes accessed | tf_op | source)
XLA Modules:
  0.0 363.0 jit_solution(953442847284173106)
XLA Ops:
  7.2 0.0 copy-start
  7.2 0.0 all-gather.3.cloned.1.call-start
  7.2 3.3 subtract_convert_fusion
  10.5 0.0 all-gather.3.cloned.1.call-update
  10.5 0.0 all-gather.5.cloned.1.call-start
  10.6 48.9 %all-gather.3.cloned.1.call-done = bf16[2,192,2048]{2,1,0:T(8,128)(2,1)} async-done(((bf16[2,48,2048]{2,1,0:T(8,128)(2,1)}), bf16[2,192,2048]{2,1,0:T(8,128)(2,1)}) %all-gather.3.cloned.1.call-update) | async-done | bytes 1572880 | tf_op jit(solution)/shard_map/all_gather | solution.py:54
  59.5 0.0 all-gather.5.cloned.1.call-update
  59.6 0.1 copy.40
  59.7 0.1 eq.33
  59.8 0.5 convert_reduce_fusion
  60.3 0.0 copy-done
  60.3 3.0 fusion.2
  63.3 69.0 %all_to_all.28 = bf16[64,24,768]{2,1,0:T(8,128)(2,1)S(1)} all-to-all(bf16[64,24,768]{2,1,0:T(8,128)(2,1)S(1)} %bitcast.36), channel_id=1, replica_groups=mesh['grp_0'=4,'grp_1'=4,'ep'=32] {'ep'}, dimensions={0} | all-to-all | bytes 4718592 | tf_op jit(solution)/shard_map/all_to_all | solution.py:67
  132.3 0.2 copy.45
  132.5 0.0 all-gather.5.cloned.1.call-done
  132.5 8.0 %multiply_convert_fusion = bf16[2,768,2048]{2,1,0:T(8,128)(2,1)S(1)} fusion(bf16[2,768,768]{2,1,0:T(8,128)(2,1)S(1)} %bitcast.35, bf16[2,768,2048]{2,1,0:T(8,128)(2,1)} %all-gather.5.cloned.1.call-done), kind=kOutput, calls=%fused_computation | convolution fusion | flops 4838129664 | bytes 14942208 | tf_op jit(solution)/shard_map/erh,ehd->erd/dot_general | solution.py:69
  140.6 13.5 %copy.52 = bf16[2,32,24,2048]{3,0,2,1:T(2,128)(2,1)S(1)} copy(bf16[2,32,24,2048]{3,2,1,0:T(8,128)(2,1)S(1)} %bitcast.34) | data formatting | bytes 12582912 | tf_op jit(solution)/shard_map/reshape | solution.py:71
  154.1 6.0 %fusion.21 = (bf16[32,2,12,2048]{3,1,2,0:T(2,128)(2,1)}, bf16[32,2,12,2048]{3,1,2,0:T(2,128)(2,1)S(1)}) fusion(bf16[32,2,24,2048]{3,1,2,0:T(2,128)(2,1)S(1)} %bitcast.32), kind=kLoop, calls=%fused_computation.42 | loop fusion | bytes 12582912 | tf_op jit(solution)/shard_map/slice | solution.py:86
  160.1 86.7 %all_to_all.29 = bf16[32,2,12,2048]{3,1,2,0:T(2,128)(2,1)S(1)} all-to-all(bf16[32,2,12,2048]{3,1,2,0:T(2,128)(2,1)S(1)} %get-tuple-element.7), channel_id=1, replica_groups=mesh['grp_0'=4,'grp_1'=4,'ep'=32] {'ep'}, dimensions={0} | all-to-all | bytes 6291456 | tf_op jit(solution)/shard_map/all_to_all | solution.py:86
  246.8 9.8 %all-to-all-start.2 = ((bf16[32,2,12,2048]{3,1,2,0:T(2,128)(2,1)}), bf16[32,2,12,2048]{3,1,2,0:T(2,128)(2,1)}, u32[]{:S(2)}, u32[]{:S(2)}) async-start(bf16[32,2,12,2048]{3,1,2,0:T(2,128)(2,1)} %get-tuple-element.6), calls=%async_computation.2 | async-start | bytes 6291456 | tf_op jit(solution)/shard_map/all_to_all | solution.py:86
  256.6 4.5 %collective-permute-start = (f32[2,48,2048]{2,1,0:T(8,128)}, f32[2,48,2048]{2,1,0:T(8,128)}, u32[]{:S(2)}, u32[]{:S(2)}) collective-permute-start(f32[2,48,2048]{2,1,0:T(8,128)} %get-tuple-element.5), channel_id=1, source_target_pairs={{0,256},{128,384},{256,0},{384,128},{1,257},{129,385},{257,1},{385... | collective-permute-start | bytes 2359304 | tf_op jit(solution)/shard_map/ppermute | solution.py:58
  261.0 0.1 reduce_sum.30
  261.2 0.1 copy.42
  261.3 0.1 copy.43
  261.4 0.1 copy.48
  261.5 4.9 %select_reduce_fusion = (bf16[128,1536]{1,0:T(8,128)(2,1)}, bf16[128,1536]{1,0:T(8,128)(2,1)}) fusion(f32[128,8]{1,0:T(8,128)S(1)} %copy.48, s32[128,8]{1,0:T(8,128)S(1)} %copy.42, f32[128,8]{1,0:T(8,128)S(1)} %copy.43), kind=kLoop, calls=%fused_computation.2 | loop fusion | flops 7471104 | bytes 798720 | tf_op jit(solution)/shard_map/reduce_sum | solution.py:79
  266.5 1.2 copy.44
  267.7 0.9 fusion.23
  268.6 1.7 reshape.56
  270.2 1.2 copy.49
  271.4 0.9 fusion.22
  272.3 1.7 reshape.61
  274.0 1.7 reshape.62
  275.7 1.0 reshape.64
  276.7 3.2 collective-permute-done
  279.9 3.6 copy.47
  283.4 4.7 %reshape.60 = bf16[768,2048]{1,0:T(8,128)(2,1)S(1)} reshape(bf16[32,2,12,2048]{3,2,1,0:T(8,128)(2,1)} %copy.47) | data formatting | bytes 6291456 | tf_op jit(solution)/shard_map/reshape | solution.py:87
  288.2 49.5 %all-to-all-done.2 = bf16[32,2,12,2048]{3,1,2,0:T(2,128)(2,1)} async-done(((bf16[32,2,12,2048]{3,1,2,0:T(2,128)(2,1)}), bf16[32,2,12,2048]{3,1,2,0:T(2,128)(2,1)}, u32[]{:S(2)}, u32[]{:S(2)}) %all-to-all-start.2) | async-done | bytes 3145760 | tf_op jit(solution)/shard_map/all_to_all | solution.py:86
  337.6 5.4 %copy.50 = bf16[32,2,12,2048]{3,2,1,0:T(8,128)(2,1)} copy(bf16[32,2,12,2048]{3,1,2,0:T(2,128)(2,1)} %all-to-all-done.2) | data formatting | bytes 6291456 | tf_op jit(solution)/shard_map/all_to_all | solution.py:86
  343.1 6.2 %reshape.63 = bf16[768,2048]{1,0:T(8,128)(2,1)} reshape(bf16[32,2,12,2048]{3,2,1,0:T(8,128)(2,1)} %copy.50) | data formatting | bytes 6291456 | tf_op jit(solution)/shard_map/reshape | solution.py:87
  349.3 0.6 fusion.24
  349.9 0.3 copy-done.5
  350.2 0.6 convolution_add_fusion.2
  350.8 1.3 copy-done.2
  352.1 0.0 copy-done.4
  352.1 0.6 convolution_add_fusion.1
  352.7 1.4 fusion.4
  354.1 2.1 copy.54
  (15 shorter events, 0.1 us)
Async XLA Ops:
  7.2 53.1 %copy-start = (bf16[128,8,768]{2,1,0:T(8,128)(2,1)S(1)}, bf16[128,8,768]{2,1,0:T(8,128)(2,1)}, u32[]{:S(2)}) copy-start(bf16[128,8,768]{2,1,0:T(8,128)(2,1)} %param.7) | copy-start | bytes 4718596
  7.2 52.4 %copy-start.6 = (s32[128,8]{0,1:T(8,128)S(1)}, s32[128,8]{0,1:T(8,128)}, u32[]{:S(2)}) copy-start(s32[128,8]{0,1:T(8,128)} %param.8) | copy-start | bytes 12292
  7.2 52.3 %all-gather.3.cloned.1.call-start = ((), (), s32[]{:S(2)}) async-start(), calls=%async_computation.3 | async-start | bytes 1966080 | tf_op jit(solution)/shard_map/all_gather | solution.py:54
  10.5 122.0 %all-gather.5.cloned.1.call-start = ((), (), s32[]{:S(2)}) async-start(), calls=%async_computation.4 | async-start | bytes 7864320 | tf_op jit(solution)/shard_map/all_gather | solution.py:55
  246.8 14.5 %copy-start.7 = (s32[128,8]{0,1:T(8,128)S(1)}, s32[128,8]{0,1:T(8,128)}, u32[]{:S(2)}) copy-start(s32[128,8]{0,1:T(8,128)} %param.9) | copy-start | bytes 12292
  246.8 90.9 %all-to-all-start.2 = ((bf16[32,2,12,2048]{3,1,2,0:T(2,128)(2,1)}), bf16[32,2,12,2048]{3,1,2,0:T(2,128)(2,1)}, u32[]{:S(2)}, u32[]{:S(2)}) async-start(bf16[32,2,12,2048]{3,1,2,0:T(2,128)(2,1)} %get-tuple-element.6), calls=%async_computation.2 | async-start | bytes 6291456 | tf_op jit(solution)/shard_map/all_to_all | solution.py:86
  256.6 23.3 %collective-permute-start = (f32[2,48,2048]{2,1,0:T(8,128)}, f32[2,48,2048]{2,1,0:T(8,128)}, u32[]{:S(2)}, u32[]{:S(2)}) collective-permute-start(f32[2,48,2048]{2,1,0:T(8,128)} %get-tuple-element.5), channel_id=1, source_target_pairs={{0,256},{128,384},{256,0},{384,128},{1,257},{129,385},{257,1},{385... | collective-permute-start | bytes 2359304 | tf_op jit(solution)/shard_map/ppermute | solution.py:58
  343.1 6.2 %copy-start.3 = (bf16[128,768]{0,1:T(8,128)(2,1)S(1)}, bf16[128,768]{0,1:T(8,128)(2,1)}, u32[]{:S(2)}) copy-start(bf16[128,768]{0,1:T(8,128)(2,1)} %reshape.56) | copy-start | bytes 589828
  349.3 0.9 copy-start.5
  350.2 1.9 copy-start.2
  350.2 1.9 copy-start.4
  352.1 4.1 %copy-start.1 = (bf16[128,8,768]{2,1,0:T(8,128)(2,1)S(1)}, bf16[128,8,768]{2,1,0:T(8,128)(2,1)}, u32[]{:S(2)}) copy-start(bf16[128,8,768]{2,1,0:T(8,128)(2,1)} %param.7) | copy-start | bytes 4718596
Sparse Core Ops, SparseCore 0:
  10.7 48.7 all-gather.2
  61.6 70.2 all-gather.4

commit v3 on v2

--- a/solution.py
+++ b/solution.py
@@ -59,35 +59,30 @@
 
     pairs = tok_count * top_count
     positions = slot_positions(expert_ids.reshape(pairs), capacity)
-    slot_ids = lax.broadcasted_iota(jnp.int32, (slots, pairs), 0)
-    placing = (positions[None, :] == slot_ids).astype(jnp.bfloat16)
-    outgoing = jnp.dot(placing, slot_hidden.reshape(pairs, hidden_width),
-                       preferred_element_type=jnp.float32).astype(jnp.bfloat16)
-    outgoing = outgoing.reshape(experts, capacity, hidden_width)
-    arrived = lax.all_to_all(outgoing, "ep", split_axis=0, concat_axis=1, tiled=True)
-
-    product = jnp.einsum("erh,ehd->erd", arrived, gathered, preferred_element_type=jnp.float32)
-    results = (product * scaling).astype(jnp.bfloat16)
-    tiles = results.reshape(local_experts, ranks, capacity, width).transpose(1, 0, 2, 3)
-
+    hidden_rows = slot_hidden.reshape(pairs, hidden_width)
+    token_pos = positions.reshape(tok_count, top_count)
     high = (gate_fixed // 256).astype(jnp.float32) / 256.0
     low = (gate_fixed % 256).astype(jnp.float32) / gate_unit
-    token_pos = positions.reshape(tok_count, top_count)
-    slot_row = lax.broadcasted_iota(jnp.int32, (tok_count, top_count, slots), 2)
-    hit = token_pos[:, :, None] == slot_row
-    combine_hi = jnp.sum(jnp.where(hit, high[:, :, None], 0.0), axis=1).astype(jnp.bfloat16)
-    combine_lo = jnp.sum(jnp.where(hit, low[:, :, None], 0.0), axis=1).astype(jnp.bfloat16)
-    combine_hi = combine_hi.reshape(tok_count, experts, capacity)
-    combine_lo = combine_lo.reshape(tok_count, experts, capacity)
+    chunk = ranks * capacity
 
     mixed = jnp.zeros((tok_count, width), jnp.float32)
-    half = capacity // 2
-    for start, stop in ((0, half), (half, capacity)):
-        piece = lax.all_to_all(tiles[:, :, start:stop], "ep", split_axis=0, concat_axis=0, tiled=True)
-        piece = piece.reshape(experts * (stop - start), width)
-        for part in (combine_hi, combine_lo):
-            weight = part[:, :, start:stop].reshape(tok_count, experts * (stop - start))
-            mixed = mixed + jnp.dot(weight, piece, preferred_element_type=jnp.float32)
+    for local in range(local_experts):
+        column = lax.broadcasted_iota(jnp.int32, (chunk,), 0)
+        slot_of = ((column // capacity) * local_experts + local) * capacity + column % capacity
+        placing = (positions[None, :] == slot_of[:, None]).astype(jnp.bfloat16)
+        outgoing = jnp.dot(placing, hidden_rows, preferred_element_type=jnp.float32).astype(jnp.bfloat16)
+        arrived = lax.all_to_all(outgoing.reshape(ranks, capacity, hidden_width), "ep",
+                                 split_axis=0, concat_axis=0, tiled=True)
+        product = jnp.dot(arrived.reshape(chunk, hidden_width), gathered[local],
+                          preferred_element_type=jnp.float32)
+        results = (product * scaling).astype(jnp.bfloat16)
+        returned = lax.all_to_all(results.reshape(ranks, capacity, width), "ep",
+                                  split_axis=0, concat_axis=0, tiled=True)
+        returned = returned.reshape(chunk, width)
+        hit = token_pos[:, :, None] == slot_of[None, None, :]
+        for part in (high, low):
+            weight = jnp.sum(jnp.where(hit, part[:, :, None], 0.0), axis=1).astype(jnp.bfloat16)
+            mixed = mixed + jnp.dot(weight, returned, preferred_element_type=jnp.float32)
     return (mixed.astype(jnp.bfloat16), backup)
 
 

time: 364 us -> 342 us (0.940)
  blocking collectives: 156 us -> 0 us
  waiting for transfers between devices: 102 us -> 247 us
  local copies, waits for them, and re-layouts: 54.1 us -> 1.54 us
  starting transfers between devices: 14.3 us -> 42.2 us
  matrix products: 14.3 us -> 28.5 us
    all_to_all x2 -> x0, blocking collectives: 156 us -> none  [the longest x1 86.7 us: body(): lax.all_to_all(tiles[:, :, start:stop], 'ep', split_axis=0, concat_axis=0...]
    all_to_all x1 -> x4, waiting for transfers between devices: 49.5 us -> 166 us  [the longest x2 130 us: body(): lax.all_to_all(results.reshape(ranks, capacity, width), 'ep', split_axis=...]
    reshape x7 -> x0, local copies, waits for them, and re-layouts: 30.5 us -> none  [the longest x1 13.5 us: body(): results.reshape(local_experts, ranks, capacity, width).transpose(1, 0, 2, 3)]
    all_to_all x1 -> x4, starting transfers between devices: 9.78 us -> 37 us  [the longest x2 19.1 us: body(): lax.all_to_all(outgoing.reshape(ranks, capacity, hidden_width), 'ep', spl...]
    all_gather x1, waiting for transfers between devices: 0.02 us -> 18.3 us  [body(): gathered = lax.all_gather(nearer, 'grp_0', axis=1, tiled=True)]
    dot_general x6 -> x8, matrix products: 14.3 us -> 28.5 us  [the longest x2 12.3 us: body(): jnp.dot(arrived.reshape(chunk, hidden_width), gathered[local], preferred_...]
    ppermute x1, waiting for transfers between devices: 3.23 us -> 13.7 us  [body(): lax.ppermute(step_dir, 'grp_0', [(s, (s + shift) % outer) for s in range(...]
    all_to_all x3 -> x0, local copies, waits for them, and re-layouts: 9.14 us -> none  [the longest x2 8.99 us: body(): lax.all_to_all(tiles[:, :, start:stop], 'ep', split_axis=0, concat_axis=0...]
  transfers between devices with their start and end apart: 4 -> 7, of which waited for: 3 -> 7; matrix products, arithmetic and copies ran while one was open for 8% -> 8% of each run, Pallas kernels for 0% -> 0%
where the time goes in v3:
time: 342 us; the launch traced here: 341 us
  waiting for transfers between devices  247 us (72%)
  starting transfers between devices  42.2 us (12%)
  matrix products  28.5 us (8%)
  between operations  14.2 us (4%)
  other arithmetic  7.64 us (2%)
    all_to_all x2, waiting for transfers between devices, body(): lax.all_to_all(results.reshape(ranks, capacity, width), 'ep', split_axis=...  130 us
    all_gather x1, waiting for transfers between devices, body(): nearer = lax.all_gather(weights, 'grp_1', axis=1, tiled=True)  48.9 us
    all_to_all x2, waiting for transfers between devices, body(): lax.all_to_all(outgoing.reshape(ranks, capacity, hidden_width), 'ep', spl...  36.5 us
    all_to_all x2, starting transfers between devices, body(): lax.all_to_all(outgoing.reshape(ranks, capacity, hidden_width), 'ep', spl...  19.1 us
    all_gather x1, waiting for transfers between devices, body(): gathered = lax.all_gather(nearer, 'grp_0', axis=1, tiled=True)  18.3 us
    all_to_all x2, starting transfers between devices, body(): lax.all_to_all(results.reshape(ranks, capacity, width), 'ep', split_axis=...  17.8 us
    ppermute x1, waiting for transfers between devices, body(): lax.ppermute(step_dir, 'grp_0', [(s, (s + shift) % outer) for s in range(...  13.7 us
    dot_general x2, matrix products, body(): jnp.dot(arrived.reshape(chunk, hidden_width), gathered[local], preferred_...  12.3 us
  transfers between devices with their start and end apart: 7, of which 7 were waited for; matrix products, arithmetic and copies ran while one was open for 8% of the time, Pallas kernels for 0%

profile of v3, /device:TPU:56, one launch (start us, length us, event | category | flops | bytes accessed | tf_op | source)
XLA Modules:
  0.0 341.2 jit_solution(6127338167899430739)
XLA Ops:
  7.2 0.0 copy-start
  7.2 0.0 copy-start.3
  7.2 0.0 all-gather.3.cloned.1.call-start
  7.2 3.3 subtract_convert_fusion
  10.5 0.0 all-gather.3.cloned.1.call-update
  10.5 0.0 all-gather.5.cloned.1.call-start
  10.6 48.9 %all-gather.3.cloned.1.call-done = bf16[2,192,2048]{2,1,0:T(8,128)(2,1)} async-done(((bf16[2,48,2048]{2,1,0:T(8,128)(2,1)}), bf16[2,192,2048]{2,1,0:T(8,128)(2,1)}) %all-gather.3.cloned.1.call-update) | async-done | bytes 1572880 | tf_op jit(solution)/shard_map/all_gather | solution.py:54
  59.5 0.0 all-gather.5.cloned.1.call-update
  59.5 0.0 copy-done.3
  59.6 0.1 copy.22
  59.7 0.1 eq.33
  59.8 0.5 convert_reduce_fusion
  60.3 0.0 copy-done
  60.3 2.5 fusion.16
  62.8 10.9 %all-to-all-start = ((bf16[32,24,768]{2,1,0:T(8,128)(2,1)}), bf16[32,24,768]{2,1,0:T(8,128)(2,1)S(1)}, u32[]{:S(2)}, u32[]{:S(2)}) async-start(bf16[32,24,768]{2,1,0:T(8,128)(2,1)} %bitcast.37), calls=%async_computation | async-start | bytes 2359296 | tf_op jit(solution)/shard_map/all_to_all | solution.py:74
  73.6 2.6 fusion.21
  76.2 29.2 %all-to-all-done = bf16[32,24,768]{2,1,0:T(8,128)(2,1)S(1)} async-done(((bf16[32,24,768]{2,1,0:T(8,128)(2,1)}), bf16[32,24,768]{2,1,0:T(8,128)(2,1)S(1)}, u32[]{:S(2)}, u32[]{:S(2)}) %all-to-all-start) | async-done | bytes 1179680 | tf_op jit(solution)/shard_map/all_to_all | solution.py:74
  105.4 8.3 %all-to-all-start.2 = ((bf16[32,24,768]{2,1,0:T(8,128)(2,1)}), bf16[32,24,768]{2,1,0:T(8,128)(2,1)}, u32[]{:S(2)}, u32[]{:S(2)}) async-start(bf16[32,24,768]{2,1,0:T(8,128)(2,1)} %bitcast.36), calls=%async_computation.2 | async-start | bytes 2359296 | tf_op jit(solution)/shard_map/all_to_all | solution.py:74
  113.7 18.3 %all-gather.5.cloned.1.call-done = bf16[2,768,2048]{2,1,0:T(8,128)(2,1)} async-done(((bf16[2,192,2048]{2,1,0:T(8,128)(2,1)}), bf16[2,768,2048]{2,1,0:T(8,128)(2,1)}) %all-gather.5.cloned.1.call-update) | async-done | bytes 6291472 | tf_op jit(solution)/shard_map/all_gather | solution.py:55
  131.9 5.9 %multiply_convert_fusion.1 = bf16[768,2048]{1,0:T(8,128)(2,1)} fusion(bf16[768,768]{1,0:T(8,128)(2,1)S(1)} %bitcast.35, bf16[2,768,2048]{2,1,0:T(8,128)(2,1)} %all-gather.5.cloned.1.call-done), kind=kOutput, calls=%fused_computation.1 | convolution fusion | flops 2419064832 | bytes 7471104 | tf_op jit(solution)/shard_map/dot_general | solution.py:76
  137.8 7.3 %all-to-all-done.2 = bf16[32,24,768]{2,1,0:T(8,128)(2,1)} async-done(((bf16[32,24,768]{2,1,0:T(8,128)(2,1)}), bf16[32,24,768]{2,1,0:T(8,128)(2,1)}, u32[]{:S(2)}, u32[]{:S(2)}) %all-to-all-start.2) | async-done | bytes 1179680 | tf_op jit(solution)/shard_map/all_to_all | solution.py:74
  145.1 8.5 %all-to-all-start.1 = ((bf16[32,24,2048]{2,1,0:T(8,128)(2,1)}), bf16[32,24,2048]{2,1,0:T(8,128)(2,1)}, u32[]{:S(2)}, u32[]{:S(2)}) async-start(bf16[32,24,2048]{2,1,0:T(8,128)(2,1)} %bitcast.34), calls=%async_computation.1 | async-start | bytes 6291456 | tf_op jit(solution)/shard_map/all_to_all | solution.py:79
  153.6 6.5 %multiply_convert_fusion = bf16[768,2048]{1,0:T(8,128)(2,1)} fusion(bf16[768,768]{1,0:T(8,128)(2,1)} %bitcast.7, bf16[2,768,2048]{2,1,0:T(8,128)(2,1)} %all-gather.5.cloned.1.call-done), kind=kOutput, calls=%fused_computation | convolution fusion | flops 2419064832 | bytes 7471104 | tf_op jit(solution)/shard_map/dot_general | solution.py:76
  160.1 75.7 %all-to-all-done.1 = bf16[32,24,2048]{2,1,0:T(8,128)(2,1)} async-done(((bf16[32,24,2048]{2,1,0:T(8,128)(2,1)}), bf16[32,24,2048]{2,1,0:T(8,128)(2,1)}, u32[]{:S(2)}, u32[]{:S(2)}) %all-to-all-start.1) | async-done | bytes 3145760 | tf_op jit(solution)/shard_map/all_to_all | solution.py:79
  235.8 0.0 copy-start.4
  235.8 9.3 %all-to-all-start.3 = ((bf16[32,24,2048]{2,1,0:T(8,128)(2,1)}), bf16[32,24,2048]{2,1,0:T(8,128)(2,1)}, u32[]{:S(2)}, u32[]{:S(2)}) async-start(bf16[32,24,2048]{2,1,0:T(8,128)(2,1)} %bitcast.33), calls=%async_computation.3 | async-start | bytes 6291456 | tf_op jit(solution)/shard_map/all_to_all | solution.py:79
  245.1 5.2 %collective-permute-start = (f32[2,48,2048]{2,1,0:T(8,128)}, f32[2,48,2048]{2,1,0:T(8,128)S(1)}, u32[]{:S(2)}, u32[]{:S(2)}) collective-permute-start(f32[2,48,2048]{2,1,0:T(8,128)} %get-tuple-element.9), channel_id=1, source_target_pairs={{0,256},{128,384},{256,0},{384,128},{1,257},{129,385},{257,1},{385... | collective-permute-start | bytes 2359304 | tf_op jit(solution)/shard_map/ppermute | solution.py:58
  250.3 0.1 reduce_sum.48
  250.4 0.1 copy.24
  250.5 0.0 copy-done.4
  250.6 0.1 copy.25
  250.7 0.1 copy.26
  250.8 3.8 %fusion.3 = (bf16[128,768]{1,0:T(8,128)(2,1)S(1)}, bf16[128,768]{1,0:T(8,128)(2,1)S(1)}, bf16[128,768]{1,0:T(8,128)(2,1)S(1)}, bf16[128,768]{1,0:T(8,128)(2,1)S(1)}) fusion(s32[768]{0:T(1024)S(1)} %get-tuple-element.12, f32[128,8]{1,0:T(8,128)S(1)} %copy.25, s32[128,8]{1,0:T(8,128)S(1)} %copy.24, s32[768]{0:T(1024)S(1)} %get-tuple-element.13, ...), kind=kLoop, calls=%fused_computation.11 | loop fusion | flops 7471104 | bytes 804864 | tf_op jit(solution)/shard_map/reduce_sum | solution.py:84
  254.6 13.7 %collective-permute-done = f32[2,48,2048]{2,1,0:T(8,128)S(1)} collective-permute-done((f32[2,48,2048]{2,1,0:T(8,128)}, f32[2,48,2048]{2,1,0:T(8,128)S(1)}, u32[]{:S(2)}, u32[]{:S(2)}) %collective-permute-start) | collective-permute-done | bytes 786464 | tf_op jit(solution)/shard_map/ppermute | solution.py:58
  268.3 0.0 copy-start.1
  268.3 2.8 fusion.55
  271.1 0.0 copy-done.1
  271.1 2.5 convolution_add_fusion.2
  273.6 54.0 %all-to-all-done.3 = bf16[32,24,2048]{2,1,0:T(8,128)(2,1)} async-done(((bf16[32,24,2048]{2,1,0:T(8,128)(2,1)}), bf16[32,24,2048]{2,1,0:T(8,128)(2,1)}, u32[]{:S(2)}, u32[]{:S(2)}) %all-to-all-start.3) | async-done | bytes 3145760 | tf_op jit(solution)/shard_map/all_to_all | solution.py:79
  327.6 2.5 convolution_add_fusion.1
  330.1 0.0 copy-start.2
  330.1 3.4 fusion.9
  333.5 0.0 copy-done.2
  333.5 0.9 copy.28
  (5 shorter events, 0.1 us)
Async XLA Ops:
  7.2 53.1 %copy-start = (bf16[128,8,768]{2,1,0:T(8,128)(2,1)S(1)}, bf16[128,8,768]{2,1,0:T(8,128)(2,1)}, u32[]{:S(2)}) copy-start(bf16[128,8,768]{2,1,0:T(8,128)(2,1)} %param.7) | copy-start | bytes 4718596
  7.2 52.4 %copy-start.3 = (s32[128,8]{0,1:T(8,128)S(1)}, s32[128,8]{0,1:T(8,128)}, u32[]{:S(2)}) copy-start(s32[128,8]{0,1:T(8,128)} %param.8) | copy-start | bytes 12292
  7.2 52.3 %all-gather.3.cloned.1.call-start = ((), (), s32[]{:S(2)}) async-start(), calls=%async_computation.4 | async-start | bytes 1966080 | tf_op jit(solution)/shard_map/all_gather | solution.py:54
  10.5 121.4 %all-gather.5.cloned.1.call-start = ((), (), s32[]{:S(2)}) async-start(), calls=%async_computation.5 | async-start | bytes 7864320 | tf_op jit(solution)/shard_map/all_gather | solution.py:55
  62.8 42.6 %all-to-all-start = ((bf16[32,24,768]{2,1,0:T(8,128)(2,1)}), bf16[32,24,768]{2,1,0:T(8,128)(2,1)S(1)}, u32[]{:S(2)}, u32[]{:S(2)}) async-start(bf16[32,24,768]{2,1,0:T(8,128)(2,1)} %bitcast.37), calls=%async_computation | async-start | bytes 2359296 | tf_op jit(solution)/shard_map/all_to_all | solution.py:74
  105.4 39.7 %all-to-all-start.2 = ((bf16[32,24,768]{2,1,0:T(8,128)(2,1)}), bf16[32,24,768]{2,1,0:T(8,128)(2,1)}, u32[]{:S(2)}, u32[]{:S(2)}) async-start(bf16[32,24,768]{2,1,0:T(8,128)(2,1)} %bitcast.36), calls=%async_computation.2 | async-start | bytes 2359296 | tf_op jit(solution)/shard_map/all_to_all | solution.py:74
  145.1 90.7 %all-to-all-start.1 = ((bf16[32,24,2048]{2,1,0:T(8,128)(2,1)}), bf16[32,24,2048]{2,1,0:T(8,128)(2,1)}, u32[]{:S(2)}, u32[]{:S(2)}) async-start(bf16[32,24,2048]{2,1,0:T(8,128)(2,1)} %bitcast.34), calls=%async_computation.1 | async-start | bytes 6291456 | tf_op jit(solution)/shard_map/all_to_all | solution.py:79
  235.8 14.7 %copy-start.4 = (s32[128,8]{0,1:T(8,128)S(1)}, s32[128,8]{0,1:T(8,128)}, u32[]{:S(2)}) copy-start(s32[128,8]{0,1:T(8,128)} %param.9) | copy-start | bytes 12292
  235.8 91.8 %all-to-all-start.3 = ((bf16[32,24,2048]{2,1,0:T(8,128)(2,1)}), bf16[32,24,2048]{2,1,0:T(8,128)(2,1)}, u32[]{:S(2)}, u32[]{:S(2)}) async-start(bf16[32,24,2048]{2,1,0:T(8,128)(2,1)} %bitcast.33), calls=%async_computation.3 | async-start | bytes 6291456 | tf_op jit(solution)/shard_map/all_to_all | solution.py:79
  245.1 23.2 %collective-permute-start = (f32[2,48,2048]{2,1,0:T(8,128)}, f32[2,48,2048]{2,1,0:T(8,128)S(1)}, u32[]{:S(2)}, u32[]{:S(2)}) collective-permute-start(f32[2,48,2048]{2,1,0:T(8,128)} %get-tuple-element.9), channel_id=1, source_target_pairs={{0,256},{128,384},{256,0},{384,128},{1,257},{129,385},{257,1},{385... | collective-permute-start | bytes 2359304 | tf_op jit(solution)/shard_map/ppermute | solution.py:58
  268.3 2.8 copy-start.1
  330.1 3.4 copy-start.2
Sparse Core Ops, SparseCore 0:
  10.7 48.7 all-gather.2
  61.6 70.2 all-gather.4

commit v4 on v3

--- a/solution.py
+++ b/solution.py
@@ -52,7 +52,12 @@
     updated = master - learn_rate * step_dir
     weights = updated.astype(jnp.bfloat16)
     nearer = lax.all_gather(weights, "grp_1", axis=1, tiled=True)
-    gathered = lax.all_gather(nearer, "grp_0", axis=1, tiled=True)
+    gathered = []
+    for local in range(local_experts):
+        rows = nearer[local]
+        if gathered:
+            rows, _ = lax.optimization_barrier((rows, gathered[-1]))
+        gathered.append(lax.all_gather(rows, "grp_0", axis=0, tiled=True))
 
     shift = outer // 2
     backup = lax.ppermute(step_dir, "grp_0", [(s, (s + shift) % outer) for s in range(outer)])

time: 342 us -> 345 us (level)
  local copies, waits for them, and re-layouts: 1.54 us -> 5.45 us
    all_to_all x2, waiting for transfers between devices: 130 us -> 80.1 us  [body(): lax.all_to_all(results.reshape(ranks, capacity, width), 'ep', split_axis=...]
    all_gather x1 -> x2, waiting for transfers between devices: 18.3 us -> 47.7 us  [body(): gathered.append(lax.all_gather(rows, 'grp_0', axis=0, tiled=True))]
    all_to_all x2, waiting for transfers between devices: 36.5 us -> 54.1 us  [body(): lax.all_to_all(outgoing.reshape(ranks, capacity, hidden_width), 'ep', spl...]
  transfers between devices with their start and end apart: 7 -> 8, of which waited for: 7 -> 7; matrix products, arithmetic and copies ran while one was open for 8% -> 8% of each run, Pallas kernels for 0% -> 0%
where the time goes in v4:
time: 345 us; the launch traced here: 344 us
  waiting for transfers between devices  245 us (71%)
  starting transfers between devices  43.1 us (12%)
  matrix products  28.5 us (8%)
  between operations  13.9 us (4%)
  other arithmetic  7.64 us (2%)
  local copies, waits for them, and re-layouts  5.45 us (2%)
    all_to_all x2, waiting for transfers between devices, body(): lax.all_to_all(results.reshape(ranks, capacity, width), 'ep', split_axis=...  80.1 us
    all_to_all x2, waiting for transfers between devices, body(): lax.all_to_all(outgoing.reshape(ranks, capacity, hidden_width), 'ep', spl...  54.1 us
    all_gather x1, waiting for transfers between devices, body(): nearer = lax.all_gather(weights, 'grp_1', axis=1, tiled=True)  48.7 us
    all_gather x2, waiting for transfers between devices, body(): gathered.append(lax.all_gather(rows, 'grp_0', axis=0, tiled=True))  47.7 us
    all_to_all x2, starting transfers between devices, body(): lax.all_to_all(outgoing.reshape(ranks, capacity, hidden_width), 'ep', spl...  19.1 us
    all_to_all x2, starting transfers between devices, body(): lax.all_to_all(results.reshape(ranks, capacity, width), 'ep', split_axis=...  18.8 us
    ppermute x1, waiting for transfers between devices, body(): lax.ppermute(step_dir, 'grp_0', [(s, (s + shift) % outer) for s in range(...  13.8 us
    dot_general x2, matrix products, body(): jnp.dot(arrived.reshape(chunk, hidden_width), gathered[local], preferred_...  12.4 us
  transfers between devices with their start and end apart: 8, of which 7 were waited for; matrix products, arithmetic and copies ran while one was open for 8% of the time, Pallas kernels for 0%

profile of v4, /device:TPU:56, one launch (start us, length us, event | category | flops | bytes accessed | tf_op | source)
XLA Modules:
  0.0 343.9 jit_solution(6317559873047085141)
XLA Ops:
  7.2 0.0 copy-start
  7.2 0.0 copy-start.4
  7.2 0.0 all-gather.5.cloned.1.call-start
  7.2 3.3 subtract_convert_fusion
  10.5 0.0 all-gather.5.cloned.1.call-update
  10.5 0.0 all-gather.9.cloned.1.call-start
  10.6 0.0 copy-done.4
  10.6 0.1 copy.22
  10.7 0.1 eq.33
  10.8 48.7 %all-gather.5.cloned.1.call-done = bf16[2,192,2048]{2,1,0:T(8,128)(2,1)} async-done(((bf16[2,48,2048]{2,1,0:T(8,128)(2,1)}), bf16[2,192,2048]{2,1,0:T(8,128)(2,1)}) %all-gather.5.cloned.1.call-update) | async-done | bytes 1572880 | tf_op jit(solution)/shard_map/all_gather | solution.py:54
  59.5 2.8 slice_bitcast_fusion
  62.3 0.0 all-gather.9.cloned.1.call-update
  62.3 0.5 convert_reduce_fusion
  62.9 0.0 copy-done
  62.9 2.5 fusion.16
  65.4 10.9 %all-to-all-start = ((bf16[32,24,768]{2,1,0:T(8,128)(2,1)}), bf16[32,24,768]{2,1,0:T(8,128)(2,1)S(1)}, u32[]{:S(2)}, u32[]{:S(2)}) async-start(bf16[32,24,768]{2,1,0:T(8,128)(2,1)} %bitcast.38), calls=%async_computation | async-start | bytes 2359296 | tf_op jit(solution)/shard_map/all_to_all | solution.py:79
  76.2 2.5 fusion.21
  78.7 29.3 %all-to-all-done = bf16[32,24,768]{2,1,0:T(8,128)(2,1)S(1)} async-done(((bf16[32,24,768]{2,1,0:T(8,128)(2,1)}), bf16[32,24,768]{2,1,0:T(8,128)(2,1)S(1)}, u32[]{:S(2)}, u32[]{:S(2)}) %all-to-all-start) | async-done | bytes 1179680 | tf_op jit(solution)/shard_map/all_to_all | solution.py:79
  108.0 0.0 copy-start.1
  108.0 1.1 copy-done.1
  109.1 8.2 %all-to-all-start.2 = ((bf16[32,24,768]{2,1,0:T(8,128)(2,1)}), bf16[32,24,768]{2,1,0:T(8,128)(2,1)S(1)}, u32[]{:S(2)}, u32[]{:S(2)}) async-start(bf16[32,24,768]{2,1,0:T(8,128)(2,1)} %bitcast.37), calls=%async_computation.2 | async-start | bytes 2359296 | tf_op jit(solution)/shard_map/all_to_all | solution.py:79
  117.4 0.0 all-gather.9.cloned.1.call-done
  117.4 6.5 %multiply_convert_fusion.1 = bf16[768,2048]{1,0:T(8,128)(2,1)} fusion(bf16[768,768]{1,0:T(8,128)(2,1)} %bitcast.36, bf16[1,768,2048]{2,1,0:T(8,128)(2,1)} %all-gather.9.cloned.1.call-done), kind=kOutput, calls=%fused_computation.1 | convolution fusion | flops 2419064832 | bytes 7471104 | tf_op jit(solution)/shard_map/dot_general | solution.py:81
  123.9 24.9 %all-to-all-done.2 = bf16[32,24,768]{2,1,0:T(8,128)(2,1)S(1)} async-done(((bf16[32,24,768]{2,1,0:T(8,128)(2,1)}), bf16[32,24,768]{2,1,0:T(8,128)(2,1)S(1)}, u32[]{:S(2)}, u32[]{:S(2)}) %all-to-all-start.2) | async-done | bytes 1179680 | tf_op jit(solution)/shard_map/all_to_all | solution.py:79
  148.7 9.5 %all-to-all-start.1 = ((bf16[32,24,2048]{2,1,0:T(8,128)(2,1)}), bf16[32,24,2048]{2,1,0:T(8,128)(2,1)}, u32[]{:S(2)}, u32[]{:S(2)}) async-start(bf16[32,24,2048]{2,1,0:T(8,128)(2,1)} %bitcast.34), calls=%async_computation.1 | async-start | bytes 6291456 | tf_op jit(solution)/shard_map/all_to_all | solution.py:84
  158.2 0.0 all-gather.7.cloned.1.call-start
  158.3 0.7 all-gather.7.cloned.1.call-update
  159.0 47.7 %all-gather.7.cloned.1.call-done = bf16[768,2048]{1,0:T(8,128)(2,1)} async-done(((bf16[192,2048]{1,0:T(8,128)(2,1)}), bf16[768,2048]{1,0:T(8,128)(2,1)}) %all-gather.7.cloned.1.call-update) | async-done | bytes 3145744 | tf_op jit(solution)/shard_map/all_gather | solution.py:60
  206.7 5.9 %multiply_convert_fusion = bf16[768,2048]{1,0:T(8,128)(2,1)} fusion(bf16[768,768]{1,0:T(8,128)(2,1)S(1)} %bitcast.35, bf16[768,2048]{1,0:T(8,128)(2,1)} %all-gather.7.cloned.1.call-done), kind=kOutput, calls=%fused_computation | convolution fusion | flops 2419064832 | bytes 7471104 | tf_op jit(solution)/shard_map/dot_general | solution.py:81
  212.6 26.9 %all-to-all-done.1 = bf16[32,24,2048]{2,1,0:T(8,128)(2,1)} async-done(((bf16[32,24,2048]{2,1,0:T(8,128)(2,1)}), bf16[32,24,2048]{2,1,0:T(8,128)(2,1)}, u32[]{:S(2)}, u32[]{:S(2)}) %all-to-all-start.1) | async-done | bytes 3145760 | tf_op jit(solution)/shard_map/all_to_all | solution.py:84
  239.5 9.3 %all-to-all-start.3 = ((bf16[32,24,2048]{2,1,0:T(8,128)(2,1)}), bf16[32,24,2048]{2,1,0:T(8,128)(2,1)}, u32[]{:S(2)}, u32[]{:S(2)}) async-start(bf16[32,24,2048]{2,1,0:T(8,128)(2,1)} %bitcast.33), calls=%async_computation.3 | async-start | bytes 6291456 | tf_op jit(solution)/shard_map/all_to_all | solution.py:84
  248.8 5.1 %collective-permute-start = (f32[2,48,2048]{2,1,0:T(8,128)}, f32[2,48,2048]{2,1,0:T(8,128)S(1)}, u32[]{:S(2)}, u32[]{:S(2)}) collective-permute-start(f32[2,48,2048]{2,1,0:T(8,128)} %get-tuple-element.11), channel_id=1, source_target_pairs={{0,256},{128,384},{256,0},{384,128},{1,257},{129,385},{257,1},{385... | collective-permute-start | bytes 2359304 | tf_op jit(solution)/shard_map/ppermute | solution.py:63
  253.8 0.1 reduce_sum.48
  254.0 0.1 copy.24
  254.1 0.0 copy-done.5
  254.1 0.1 copy.25
  254.2 0.1 copy.26
  254.3 3.8 %fusion.3 = (bf16[128,768]{1,0:T(8,128)(2,1)S(1)}, bf16[128,768]{1,0:T(8,128)(2,1)S(1)}, bf16[128,768]{1,0:T(8,128)(2,1)S(1)}, bf16[128,768]{1,0:T(8,128)(2,1)S(1)}) fusion(s32[768]{0:T(1024)S(1)} %get-tuple-element.16, f32[128,8]{1,0:T(8,128)S(1)} %copy.25, s32[128,8]{1,0:T(8,128)S(1)} %copy.24, s32[768]{0:T(1024)S(1)} %get-tuple-element.17, ...), kind=kLoop, calls=%fused_computation.11 | loop fusion | flops 7471104 | bytes 804864 | tf_op jit(solution)/shard_map/reduce_sum | solution.py:89
  258.2 13.8 %collective-permute-done = f32[2,48,2048]{2,1,0:T(8,128)S(1)} collective-permute-done((f32[2,48,2048]{2,1,0:T(8,128)}, f32[2,48,2048]{2,1,0:T(8,128)S(1)}, u32[]{:S(2)}, u32[]{:S(2)}) %collective-permute-start) | collective-permute-done | bytes 786464 | tf_op jit(solution)/shard_map/ppermute | solution.py:63
  272.0 2.8 fusion.56
  274.8 0.0 copy-done.2
  274.8 2.5 convolution_add_fusion.2
  277.3 53.3 %all-to-all-done.3 = bf16[32,24,2048]{2,1,0:T(8,128)(2,1)} async-done(((bf16[32,24,2048]{2,1,0:T(8,128)(2,1)}), bf16[32,24,2048]{2,1,0:T(8,128)(2,1)}, u32[]{:S(2)}, u32[]{:S(2)}) %all-to-all-start.3) | async-done | bytes 3145760 | tf_op jit(solution)/shard_map/all_to_all | solution.py:84
  330.6 2.5 convolution_add_fusion.1
  333.1 0.0 copy-start.3
  333.1 3.4 fusion.9
  336.4 0.0 copy-done.3
  336.4 0.9 copy.28
  (7 shorter events, 0.1 us)
Async XLA Ops:
  7.2 55.7 %copy-start = (bf16[128,8,768]{2,1,0:T(8,128)(2,1)S(1)}, bf16[128,8,768]{2,1,0:T(8,128)(2,1)}, u32[]{:S(2)}) copy-start(bf16[128,8,768]{2,1,0:T(8,128)(2,1)} %param.7) | copy-start | bytes 4718596
  7.2 3.4 copy-start.4
  7.2 52.3 %all-gather.5.cloned.1.call-start = ((), (), s32[]{:S(2)}) async-start(), calls=%async_computation.4 | async-start | bytes 1966080 | tf_op jit(solution)/shard_map/all_gather | solution.py:54
  10.5 106.9 %all-gather.9.cloned.1.call-start = ((), (), s32[]{:S(2)}) async-start(), calls=%async_computation.6 | async-start | bytes 3932160 | tf_op jit(solution)/shard_map/all_gather | solution.py:60
  65.4 42.6 %all-to-all-start = ((bf16[32,24,768]{2,1,0:T(8,128)(2,1)}), bf16[32,24,768]{2,1,0:T(8,128)(2,1)S(1)}, u32[]{:S(2)}, u32[]{:S(2)}) async-start(bf16[32,24,768]{2,1,0:T(8,128)(2,1)} %bitcast.38), calls=%async_computation | async-start | bytes 2359296 | tf_op jit(solution)/shard_map/all_to_all | solution.py:79
  108.0 1.1 copy-start.1
  109.1 39.6 %all-to-all-start.2 = ((bf16[32,24,768]{2,1,0:T(8,128)(2,1)}), bf16[32,24,768]{2,1,0:T(8,128)(2,1)S(1)}, u32[]{:S(2)}, u32[]{:S(2)}) async-start(bf16[32,24,768]{2,1,0:T(8,128)(2,1)} %bitcast.37), calls=%async_computation.2 | async-start | bytes 2359296 | tf_op jit(solution)/shard_map/all_to_all | solution.py:79
  148.7 90.7 %all-to-all-start.1 = ((bf16[32,24,2048]{2,1,0:T(8,128)(2,1)}), bf16[32,24,2048]{2,1,0:T(8,128)(2,1)}, u32[]{:S(2)}, u32[]{:S(2)}) async-start(bf16[32,24,2048]{2,1,0:T(8,128)(2,1)} %bitcast.34), calls=%async_computation.1 | async-start | bytes 6291456 | tf_op jit(solution)/shard_map/all_to_all | solution.py:84
  158.2 48.4 %all-gather.7.cloned.1.call-start = ((), (), s32[]{:S(2)}) async-start(), calls=%async_computation.5 | async-start | bytes 3932160 | tf_op jit(solution)/shard_map/all_gather | solution.py:60
  239.5 14.7 %copy-start.5 = (s32[128,8]{0,1:T(8,128)S(1)}, s32[128,8]{0,1:T(8,128)}, u32[]{:S(2)}) copy-start(s32[128,8]{0,1:T(8,128)} %param.9) | copy-start | bytes 12292
  239.5 91.1 %all-to-all-start.3 = ((bf16[32,24,2048]{2,1,0:T(8,128)(2,1)}), bf16[32,24,2048]{2,1,0:T(8,128)(2,1)}, u32[]{:S(2)}, u32[]{:S(2)}) async-start(bf16[32,24,2048]{2,1,0:T(8,128)(2,1)} %bitcast.33), calls=%async_computation.3 | async-start | bytes 6291456 | tf_op jit(solution)/shard_map/all_to_all | solution.py:84
  248.8 23.2 %collective-permute-start = (f32[2,48,2048]{2,1,0:T(8,128)}, f32[2,48,2048]{2,1,0:T(8,128)S(1)}, u32[]{:S(2)}, u32[]{:S(2)}) collective-permute-start(f32[2,48,2048]{2,1,0:T(8,128)} %get-tuple-element.11), channel_id=1, source_target_pairs={{0,256},{128,384},{256,0},{384,128},{1,257},{129,385},{257,1},{385... | collective-permute-start | bytes 2359304 | tf_op jit(solution)/shard_map/ppermute | solution.py:63
  272.0 2.8 copy-start.2
  333.1 3.4 copy-start.3
Sparse Core Ops, SparseCore 0:
  10.7 48.7 all-gather.4
  62.4 44.1 all-gather.8
  161.2 45.4 all-gather.6

commit v5 on v4

--- a/solution.py
+++ b/solution.py
@@ -51,7 +51,14 @@
     step_dir = adamw_step(master, moment_one, moment_two, gradient)
     updated = master - learn_rate * step_dir
     weights = updated.astype(jnp.bfloat16)
-    nearer = lax.all_gather(weights, "grp_1", axis=1, tiled=True)
+    inner = lax.axis_size("grp_1")
+    here = lax.axis_index("grp_1")
+    received = [weights]
+    for shift_by in range(1, inner):
+        received.append(lax.ppermute(weights, "grp_1", [(s, (s + shift_by) % inner) for s in range(inner)]))
+    ordered = jnp.stack([received[(-k) % inner] for k in range(inner)], axis=1)
+    ordered = jnp.roll(ordered, here, axis=1)
+    nearer = ordered.reshape(local_experts, inner * weights.shape[1], width)
     gathered = []
     for local in range(local_experts):
         rows = nearer[local]

time: 345 us -> 346 us (level)
  waiting for transfers between devices: 245 us -> 225 us
  starting transfers between devices: 43.1 us -> 56.8 us
  local copies, waits for them, and re-layouts: 5.45 us -> 12 us
    all_gather x1 -> x0, waiting for transfers between devices: 48.7 us -> none  [body(): nearer = lax.all_gather(weights, 'grp_1', axis=1, tiled=True)]
    ppermute x0 -> x3, waiting for transfers between devices: none -> 27.1 us  [body(): lax.ppermute(weights, 'grp_1', [(s, (s + shift_by) % inner) for s in rang...]
    ppermute x0 -> x3, starting transfers between devices: none -> 12.3 us  [body(): lax.ppermute(weights, 'grp_1', [(s, (s + shift_by) % inner) for s in rang...]
    unnamed x14 -> x18, local copies, waits for them, and re-layouts: 2.13 us -> 7.96 us
  transfers between devices with their start and end apart: 8 -> 10, of which waited for: 7 -> 8; matrix products, arithmetic and copies ran while one was open for 8% -> 8% of each run, Pallas kernels for 0% -> 0%
where the time goes in v5:
time: 346 us; the launch traced here: 344 us
  waiting for transfers between devices  225 us (65%)
  starting transfers between devices  56.8 us (16%)
  matrix products  28.2 us (8%)
  between operations  14.3 us (4%)
  local copies, waits for them, and re-layouts  12 us (3%)
  other arithmetic  7.64 us (2%)
    all_to_all x2, waiting for transfers between devices, body(): lax.all_to_all(results.reshape(ranks, capacity, width), 'ep', split_axis=...  80.5 us
    all_to_all x2, waiting for transfers between devices, body(): lax.all_to_all(outgoing.reshape(ranks, capacity, hidden_width), 'ep', spl...  54.9 us
    all_gather x2, waiting for transfers between devices, body(): gathered.append(lax.all_gather(rows, 'grp_0', axis=0, tiled=True))  48.5 us
    ppermute x3, waiting for transfers between devices, body(): lax.ppermute(weights, 'grp_1', [(s, (s + shift_by) % inner) for s in rang...  27.1 us
    all_to_all x2, starting transfers between devices, body(): lax.all_to_all(outgoing.reshape(ranks, capacity, hidden_width), 'ep', spl...  21.7 us
    all_to_all x2, starting transfers between devices, body(): lax.all_to_all(results.reshape(ranks, capacity, width), 'ep', split_axis=...  17.4 us
    ppermute x1, waiting for transfers between devices, body(): lax.ppermute(step_dir, 'grp_0', [(s, (s + shift) % outer) for s in range(...  13.5 us
    dot_general x2, matrix products, body(): jnp.dot(arrived.reshape(chunk, hidden_width), gathered[local], preferred_...  12.4 us
  transfers between devices with their start and end apart: 10, of which 8 were waited for; matrix products, arithmetic and copies ran while one was open for 8% of the time, Pallas kernels for 0%

profile of v5, /device:TPU:56, one launch (start us, length us, event | category | flops | bytes accessed | tf_op | source)
XLA Modules:
  0.0 344.1 jit_solution(7907465215535572543)
XLA Ops:
  7.2 0.0 all-gather.3.cloned.1.call-start
  7.2 3.3 bitcast_dynamic-update-slice_fusion.6
  10.5 7.9 %collective-permute-start = (bf16[2,48,2048]{2,1,0:T(8,128)(2,1)S(1)}, bf16[2,48,2048]{2,1,0:T(8,128)(2,1)S(1)}, u32[]{:S(2)}, u32[]{:S(2)}) collective-permute-start(bf16[2,48,2048]{2,1,0:T(8,128)(2,1)S(1)} %get-tuple-element.11), channel_id=1, source_target_pairs={{0,96},{32,0},{64,32},{96,64},{1,97},{33,1},{65,33},{97,65},{2,98}... | collective-permute-start | bytes 1179656 | tf_op jit(solution)/shard_map/ppermute | solution.py:58
  18.4 1.9 collective-permute-start.1
  20.3 2.5 collective-permute-start.2
  22.8 0.1 copy.22
  22.9 0.1 eq.36
  23.0 4.9 %collective-permute-done = bf16[2,48,2048]{2,1,0:T(8,128)(2,1)S(1)} collective-permute-done((bf16[2,48,2048]{2,1,0:T(8,128)(2,1)S(1)}, bf16[2,48,2048]{2,1,0:T(8,128)(2,1)S(1)}, u32[]{:S(2)}, u32[]{:S(2)}) %collective-permute-start) | collective-permute-done | bytes 393248 | tf_op jit(solution)/shard_map/ppermute | solution.py:58
  28.0 0.8 bitcast_dynamic-update-slice_fusion.4
  28.8 22.2 %collective-permute-done.1 = bf16[2,48,2048]{2,1,0:T(8,128)(2,1)S(1)} collective-permute-done((bf16[2,48,2048]{2,1,0:T(8,128)(2,1)S(1)}, bf16[2,48,2048]{2,1,0:T(8,128)(2,1)S(1)}, u32[]{:S(2)}, u32[]{:S(2)}) %collective-permute-start.1) | collective-permute-done | bytes 393248 | tf_op jit(solution)/shard_map/ppermute | solution.py:58
  51.0 0.8 bitcast_dynamic-update-slice_fusion.2
  51.7 0.8 bitcast_dynamic-update-slice_fusion
  52.5 0.8 bitcast_dynamic-update-slice_fusion.7
  53.3 0.8 bitcast_dynamic-update-slice_fusion.5
  54.1 0.8 bitcast_dynamic-update-slice_fusion.3
  54.8 0.8 bitcast_dynamic-update-slice_fusion.1
  55.6 2.7 constant_dynamic-slice_fusion.1
  58.4 0.0 all-gather.3.cloned.1.call-update
  58.4 0.5 convert_reduce_fusion
  58.9 2.5 fusion.16
  61.4 14.0 %all-to-all-start = ((bf16[32,24,768]{2,1,0:T(8,128)(2,1)}), bf16[32,24,768]{2,1,0:T(8,128)(2,1)S(1)}, u32[]{:S(2)}, u32[]{:S(2)}) async-start(bf16[32,24,768]{2,1,0:T(8,128)(2,1)} %bitcast.50), calls=%async_computation | async-start | bytes 2359296 | tf_op jit(solution)/shard_map/all_to_all | solution.py:86
  75.4 2.5 fusion.21
  77.9 29.6 %all-to-all-done = bf16[32,24,768]{2,1,0:T(8,128)(2,1)S(1)} async-done(((bf16[32,24,768]{2,1,0:T(8,128)(2,1)}), bf16[32,24,768]{2,1,0:T(8,128)(2,1)S(1)}, u32[]{:S(2)}, u32[]{:S(2)}) %all-to-all-start) | async-done | bytes 1179680 | tf_op jit(solution)/shard_map/all_to_all | solution.py:86
  107.6 1.1 copy-done.1
  108.7 7.7 %all-to-all-start.2 = ((bf16[32,24,768]{2,1,0:T(8,128)(2,1)}), bf16[32,24,768]{2,1,0:T(8,128)(2,1)S(1)}, u32[]{:S(2)}, u32[]{:S(2)}) async-start(bf16[32,24,768]{2,1,0:T(8,128)(2,1)} %bitcast.49), calls=%async_computation.2 | async-start | bytes 2359296 | tf_op jit(solution)/shard_map/all_to_all | solution.py:86
  116.4 0.0 all-gather.3.cloned.1.call-done
  116.5 6.5 %multiply_convert_fusion.1 = bf16[768,2048]{1,0:T(8,128)(2,1)} fusion(bf16[768,768]{1,0:T(8,128)(2,1)} %bitcast.48, bf16[768,2048]{1,0:T(8,128)(2,1)} %all-gather.3.cloned.1.call-done), kind=kOutput, calls=%fused_computation.1 | convolution fusion | flops 2419064832 | bytes 7471104 | tf_op jit(solution)/shard_map/dot_general | solution.py:88
  123.0 25.2 %all-to-all-done.2 = bf16[32,24,768]{2,1,0:T(8,128)(2,1)S(1)} async-done(((bf16[32,24,768]{2,1,0:T(8,128)(2,1)}), bf16[32,24,768]{2,1,0:T(8,128)(2,1)S(1)}, u32[]{:S(2)}, u32[]{:S(2)}) %all-to-all-start.2) | async-done | bytes 1179680 | tf_op jit(solution)/shard_map/all_to_all | solution.py:86
  148.2 8.1 %all-to-all-start.1 = ((bf16[32,24,2048]{2,1,0:T(8,128)(2,1)}), bf16[32,24,2048]{2,1,0:T(8,128)(2,1)}, u32[]{:S(2)}, u32[]{:S(2)}) async-start(bf16[32,24,2048]{2,1,0:T(8,128)(2,1)} %bitcast.44), calls=%async_computation.1 | async-start | bytes 6291456 | tf_op jit(solution)/shard_map/all_to_all | solution.py:91
  156.3 0.0 all-gather.5.cloned.1.call-start
  156.4 0.7 all-gather.5.cloned.1.call-update
  157.1 48.5 %all-gather.5.cloned.1.call-done = bf16[768,2048]{1,0:T(8,128)(2,1)} async-done(((bf16[192,2048]{1,0:T(8,128)(2,1)}), bf16[768,2048]{1,0:T(8,128)(2,1)}) %all-gather.5.cloned.1.call-update) | async-done | bytes 3145744 | tf_op jit(solution)/shard_map/all_gather | solution.py:67
  205.6 5.9 %multiply_convert_fusion = bf16[768,2048]{1,0:T(8,128)(2,1)} fusion(bf16[768,768]{1,0:T(8,128)(2,1)S(1)} %bitcast.47, bf16[768,2048]{1,0:T(8,128)(2,1)} %all-gather.5.cloned.1.call-done), kind=kOutput, calls=%fused_computation | convolution fusion | flops 2419064832 | bytes 7471104 | tf_op jit(solution)/shard_map/dot_general | solution.py:88
  211.5 26.2 %all-to-all-done.1 = bf16[32,24,2048]{2,1,0:T(8,128)(2,1)} async-done(((bf16[32,24,2048]{2,1,0:T(8,128)(2,1)}), bf16[32,24,2048]{2,1,0:T(8,128)(2,1)}, u32[]{:S(2)}, u32[]{:S(2)}) %all-to-all-start.1) | async-done | bytes 3145760 | tf_op jit(solution)/shard_map/all_to_all | solution.py:91
  237.7 9.3 %all-to-all-start.3 = ((bf16[32,24,2048]{2,1,0:T(8,128)(2,1)}), bf16[32,24,2048]{2,1,0:T(8,128)(2,1)}, u32[]{:S(2)}, u32[]{:S(2)}) async-start(bf16[32,24,2048]{2,1,0:T(8,128)(2,1)} %bitcast.43), calls=%async_computation.3 | async-start | bytes 6291456 | tf_op jit(solution)/shard_map/all_to_all | solution.py:91
  247.1 5.2 %collective-permute-start.3 = (f32[2,48,2048]{2,1,0:T(8,128)S(1)}, f32[2,48,2048]{2,1,0:T(8,128)}, u32[]{:S(2)}, u32[]{:S(2)}) collective-permute-start(f32[2,48,2048]{2,1,0:T(8,128)S(1)} %copy-done.2), channel_id=1, source_target_pairs={{0,256},{128,384},{256,0},{384,128},{1,257},{129,385},{257,1},{385... | collective-permute-start | bytes 2359304 | tf_op jit(solution)/shard_map/ppermute | solution.py:70
  252.3 0.1 reduce_sum.48
  252.5 0.1 copy.24
  252.6 0.1 copy.25
  252.7 0.1 copy.26
  252.8 3.8 %fusion.3 = (bf16[128,768]{1,0:T(8,128)(2,1)S(1)}, bf16[128,768]{1,0:T(8,128)(2,1)S(1)}, bf16[128,768]{1,0:T(8,128)(2,1)S(1)}, bf16[128,768]{1,0:T(8,128)(2,1)S(1)}) fusion(s32[768]{0:T(1024)S(1)} %get-tuple-element.17, f32[128,8]{1,0:T(8,128)S(1)} %copy.25, s32[128,8]{1,0:T(8,128)S(1)} %copy.24, s32[768]{0:T(1024)S(1)} %get-tuple-element.18, ...), kind=kLoop, calls=%fused_computation.11 | loop fusion | flops 7471104 | bytes 804864 | tf_op jit(solution)/shard_map/reduce_sum | solution.py:96
  256.6 13.5 %collective-permute-done.3 = f32[2,48,2048]{2,1,0:T(8,128)} collective-permute-done((f32[2,48,2048]{2,1,0:T(8,128)S(1)}, f32[2,48,2048]{2,1,0:T(8,128)}, u32[]{:S(2)}, u32[]{:S(2)}) %collective-permute-start.3) | collective-permute-done | bytes 786464 | tf_op jit(solution)/shard_map/ppermute | solution.py:70
  270.2 2.5 fusion.55
  272.7 2.5 convolution_add_fusion.2
  275.2 54.3 %all-to-all-done.3 = bf16[32,24,2048]{2,1,0:T(8,128)(2,1)} async-done(((bf16[32,24,2048]{2,1,0:T(8,128)(2,1)}), bf16[32,24,2048]{2,1,0:T(8,128)(2,1)}, u32[]{:S(2)}, u32[]{:S(2)}) %all-to-all-start.3) | async-done | bytes 3145760 | tf_op jit(solution)/shard_map/all_to_all | solution.py:91
  329.5 2.5 convolution_add_fusion.1
  331.9 3.3 fusion.9
  335.2 2.1 copy.35
  (15 shorter events, 0.1 us)
Async XLA Ops:
  7.2 51.8 %copy-start = (bf16[128,8,768]{2,1,0:T(8,128)(2,1)S(1)}, bf16[128,8,768]{2,1,0:T(8,128)(2,1)}, u32[]{:S(2)}) copy-start(bf16[128,8,768]{2,1,0:T(8,128)(2,1)} %param.7) | copy-start | bytes 4718596
  7.2 15.6 %copy-start.3 = (s32[128,8]{0,1:T(8,128)S(1)}, s32[128,8]{0,1:T(8,128)}, u32[]{:S(2)}) copy-start(s32[128,8]{0,1:T(8,128)} %param.8) | copy-start | bytes 12292
  7.2 109.3 %all-gather.3.cloned.1.call-start = ((), (), s32[]{:S(2)}) async-start(), calls=%async_computation.4 | async-start | bytes 3932160 | tf_op jit(solution)/shard_map/all_gather | solution.py:67
  10.5 17.5 %collective-permute-start = (bf16[2,48,2048]{2,1,0:T(8,128)(2,1)S(1)}, bf16[2,48,2048]{2,1,0:T(8,128)(2,1)S(1)}, u32[]{:S(2)}, u32[]{:S(2)}) collective-permute-start(bf16[2,48,2048]{2,1,0:T(8,128)(2,1)S(1)} %get-tuple-element.11), channel_id=1, source_target_pairs={{0,96},{32,0},{64,32},{96,64},{1,97},{33,1},{65,33},{97,65},{2,98}... | collective-permute-start | bytes 1179656 | tf_op jit(solution)/shard_map/ppermute | solution.py:58
  18.4 32.6 %collective-permute-start.1 = (bf16[2,48,2048]{2,1,0:T(8,128)(2,1)S(1)}, bf16[2,48,2048]{2,1,0:T(8,128)(2,1)S(1)}, u32[]{:S(2)}, u32[]{:S(2)}) collective-permute-start(bf16[2,48,2048]{2,1,0:T(8,128)(2,1)S(1)} %get-tuple-element.11), channel_id=1, source_target_pairs={{0,64},{32,96},{64,0},{96,32},{1,65},{33,97},{65,1},{97,33},{2,66}... | collective-permute-start | bytes 1179656 | tf_op jit(solution)/shard_map/ppermute | solution.py:58
  20.3 31.4 %collective-permute-start.2 = (bf16[2,48,2048]{2,1,0:T(8,128)(2,1)S(1)}, bf16[2,48,2048]{2,1,0:T(8,128)(2,1)S(1)}, u32[]{:S(2)}, u32[]{:S(2)}) collective-permute-start(bf16[2,48,2048]{2,1,0:T(8,128)(2,1)S(1)} %get-tuple-element.11), channel_id=1, source_target_pairs={{0,32},{32,64},{64,96},{96,0},{1,33},{33,65},{65,97},{97,1},{2,34}... | collective-permute-start | bytes 1179656 | tf_op jit(solution)/shard_map/ppermute | solution.py:58
  61.4 46.1 %all-to-all-start = ((bf16[32,24,768]{2,1,0:T(8,128)(2,1)}), bf16[32,24,768]{2,1,0:T(8,128)(2,1)S(1)}, u32[]{:S(2)}, u32[]{:S(2)}) async-start(bf16[32,24,768]{2,1,0:T(8,128)(2,1)} %bitcast.50), calls=%async_computation | async-start | bytes 2359296 | tf_op jit(solution)/shard_map/all_to_all | solution.py:86
  107.6 1.1 copy-start.1
  108.7 39.5 %all-to-all-start.2 = ((bf16[32,24,768]{2,1,0:T(8,128)(2,1)}), bf16[32,24,768]{2,1,0:T(8,128)(2,1)S(1)}, u32[]{:S(2)}, u32[]{:S(2)}) async-start(bf16[32,24,768]{2,1,0:T(8,128)(2,1)} %bitcast.49), calls=%async_computation.2 | async-start | bytes 2359296 | tf_op jit(solution)/shard_map/all_to_all | solution.py:86
  148.2 89.5 %all-to-all-start.1 = ((bf16[32,24,2048]{2,1,0:T(8,128)(2,1)}), bf16[32,24,2048]{2,1,0:T(8,128)(2,1)}, u32[]{:S(2)}, u32[]{:S(2)}) async-start(bf16[32,24,2048]{2,1,0:T(8,128)(2,1)} %bitcast.44), calls=%async_computation.1 | async-start | bytes 6291456 | tf_op jit(solution)/shard_map/all_to_all | solution.py:91
  156.3 49.3 %all-gather.5.cloned.1.call-start = ((), (), s32[]{:S(2)}) async-start(), calls=%async_computation.5 | async-start | bytes 3932160 | tf_op jit(solution)/shard_map/all_gather | solution.py:67
  237.7 9.3 %copy-start.2 = (f32[2,48,2048]{2,1,0:T(8,128)S(1)}, f32[2,48,2048]{2,1,0:T(8,128)}, u32[]{:S(2)}) copy-start(f32[2,48,2048]{2,1,0:T(8,128)} %get-tuple-element.12) | copy-start | bytes 2359300
  237.7 14.8 %copy-start.4 = (s32[128,8]{0,1:T(8,128)S(1)}, s32[128,8]{0,1:T(8,128)}, u32[]{:S(2)}) copy-start(s32[128,8]{0,1:T(8,128)} %param.9) | copy-start | bytes 12292
  237.7 91.7 %all-to-all-start.3 = ((bf16[32,24,2048]{2,1,0:T(8,128)(2,1)}), bf16[32,24,2048]{2,1,0:T(8,128)(2,1)}, u32[]{:S(2)}, u32[]{:S(2)}) async-start(bf16[32,24,2048]{2,1,0:T(8,128)(2,1)} %bitcast.43), calls=%async_computation.3 | async-start | bytes 6291456 | tf_op jit(solution)/shard_map/all_to_all | solution.py:91
  247.1 23.1 %collective-permute-start.3 = (f32[2,48,2048]{2,1,0:T(8,128)S(1)}, f32[2,48,2048]{2,1,0:T(8,128)}, u32[]{:S(2)}, u32[]{:S(2)}) collective-permute-start(f32[2,48,2048]{2,1,0:T(8,128)S(1)} %copy-done.2), channel_id=1, source_target_pairs={{0,256},{128,384},{256,0},{384,128},{1,257},{129,385},{257,1},{385... | collective-permute-start | bytes 2359304 | tf_op jit(solution)/shard_map/ppermute | solution.py:70
Sparse Core Ops, SparseCore 0:
  58.5 47.4 all-gather.2
  159.3 46.2 all-gather.4

commit v6 on v3

--- a/solution.py
+++ b/solution.py
@@ -52,7 +52,6 @@
     updated = master - learn_rate * step_dir
     weights = updated.astype(jnp.bfloat16)
     nearer = lax.all_gather(weights, "grp_1", axis=1, tiled=True)
-    gathered = lax.all_gather(nearer, "grp_0", axis=1, tiled=True)
 
     shift = outer // 2
     backup = lax.ppermute(step_dir, "grp_0", [(s, (s + shift) % outer) for s in range(outer)])
@@ -65,21 +64,32 @@
     low = (gate_fixed % 256).astype(jnp.float32) / gate_unit
     chunk = ranks * capacity
 
+    column = lax.broadcasted_iota(jnp.int32, (chunk,), 0)
+    slot_of = []
+    arrived = []
+    for local in range(local_experts):
+        slot_of.append(((column // capacity) * local_experts + local) * capacity + column % capacity)
+        placing = (positions[None, :] == slot_of[local][:, None]).astype(jnp.bfloat16)
+        outgoing = jnp.dot(placing, hidden_rows, preferred_element_type=jnp.float32).astype(jnp.bfloat16)
+        arrived.append(lax.all_to_all(outgoing.reshape(ranks, capacity, hidden_width), "ep",
+                                      split_axis=0, concat_axis=0, tiled=True))
+
+    gathered = []
+    for local in range(local_experts):
+        rows, tie = lax.optimization_barrier((nearer[local], gathered[-1] if gathered else arrived[0]))
+        if not gathered:
+            arrived[0] = tie
+        gathered.append(lax.all_gather(rows, "grp_0", axis=0, tiled=True))
+
     mixed = jnp.zeros((tok_count, width), jnp.float32)
     for local in range(local_experts):
-        column = lax.broadcasted_iota(jnp.int32, (chunk,), 0)
-        slot_of = ((column // capacity) * local_experts + local) * capacity + column % capacity
-        placing = (positions[None, :] == slot_of[:, None]).astype(jnp.bfloat16)
-        outgoing = jnp.dot(placing, hidden_rows, preferred_element_type=jnp.float32).astype(jnp.bfloat16)
-        arrived = lax.all_to_all(outgoing.reshape(ranks, capacity, hidden_width), "ep",
-                                 split_axis=0, concat_axis=0, tiled=True)
-        product = jnp.dot(arrived.reshape(chunk, hidden_width), gathered[local],
+        product = jnp.dot(arrived[local].reshape(chunk, hidden_width), gathered[local],
                           preferred_element_type=jnp.float32)
         results = (product * scaling).astype(jnp.bfloat16)
         returned = lax.all_to_all(results.reshape(ranks, capacity, width), "ep",
                                   split_axis=0, concat_axis=0, tiled=True)
         returned = returned.reshape(chunk, width)
-        hit = token_pos[:, :, None] == slot_of[None, None, :]
+        hit = token_pos[:, :, None] == slot_of[local][None, None, :]
         for part in (high, low):
             weight = jnp.sum(jnp.where(hit, part[:, :, None], 0.0), axis=1).astype(jnp.bfloat16)
             mixed = mixed + jnp.dot(weight, returned, preferred_element_type=jnp.float32)

time: 342 us -> 336 us (0.982)
  waiting for transfers between devices: 247 us -> 229 us
  starting transfers between devices: 42.2 us -> 52.4 us
    all_gather x1 -> x2, waiting for transfers between devices: 18.3 us -> 77.6 us  [body(): gathered.append(lax.all_gather(rows, 'grp_0', axis=0, tiled=True))]
    all_to_all x2, waiting for transfers between devices: 130 us -> 80.6 us  [body(): lax.all_to_all(results.reshape(ranks, capacity, width), 'ep', split_axis=...]
    all_to_all x2, waiting for transfers between devices: 36.5 us -> 0.01 us  [body(): lax.all_to_all(outgoing.reshape(ranks, capacity, hidden_width), 'ep', spl...]
    all_to_all x2, starting transfers between devices: 19.1 us -> 26 us  [body(): lax.all_to_all(outgoing.reshape(ranks, capacity, hidden_width), 'ep', spl...]
    all_gather x1, waiting for transfers between devices: 48.9 us -> 55.3 us  [body(): nearer = lax.all_gather(weights, 'grp_1', axis=1, tiled=True)]
    all_to_all x2, starting transfers between devices: 17.8 us -> 22.3 us  [body(): lax.all_to_all(results.reshape(ranks, capacity, width), 'ep', split_axis=...]
  transfers between devices with their start and end apart: 7 -> 8, of which waited for: 7 -> 6; matrix products, arithmetic and copies ran while one was open for 8% -> 9% of each run, Pallas kernels for 0% -> 0%
where the time goes in v6:
time: 336 us
  waiting for transfers between devices  229 us (68%)
  starting transfers between devices  52.4 us (16%)
  matrix products  28.5 us (8%)
  between operations  13.9 us (4%)
  other arithmetic  7.64 us (2%)
  local copies, waits for them, and re-layouts  4.33 us (1%)
    all_to_all x2, waiting for transfers between devices, body(): lax.all_to_all(results.reshape(ranks, capacity, width), 'ep', split_axis=...  80.6 us
    all_gather x2, waiting for transfers between devices, body(): gathered.append(lax.all_gather(rows, 'grp_0', axis=0, tiled=True))  77.6 us
    all_gather x1, waiting for transfers between devices, body(): nearer = lax.all_gather(weights, 'grp_1', axis=1, tiled=True)  55.3 us
    all_to_all x2, starting transfers between devices, body(): lax.all_to_all(outgoing.reshape(ranks, capacity, hidden_width), 'ep', spl...  26 us
    all_to_all x2, starting transfers between devices, body(): lax.all_to_all(results.reshape(ranks, capacity, width), 'ep', split_axis=...  22.3 us
    ppermute x1, waiting for transfers between devices, body(): lax.ppermute(step_dir, 'grp_0', [(s, (s + shift) % outer) for s in range(...  14.8 us
    dot_general x2, matrix products, body(): jnp.dot(arrived[local].reshape(chunk, hidden_width), gathered[local], pre...  12.4 us
    dot_general x4, matrix products, body(): jnp.dot(weight, returned, preferred_element_type=jnp.float32)  11.1 us
  transfers between devices with their start and end apart: 8, of which 6 were waited for; matrix products, arithmetic and copies ran while one was open for 9% of the time, Pallas kernels for 0%

profile of v6, /device:TPU:56, one launch (start us, length us, event | category | flops | bytes accessed | tf_op | source)
XLA Modules:
  0.0 335.7 jit_solution(1052248926024861481)
XLA Ops:
  7.2 0.0 copy-start
  7.2 0.0 copy-start.3
  7.2 0.0 all-gather.4.cloned.1.call-start
  7.2 3.3 subtract_convert_fusion
  10.5 0.0 all-gather.4.cloned.1.call-update
  10.5 0.0 copy-done.3
  10.5 0.1 copy.22
  10.6 0.1 eq.33
  10.7 0.5 convert_reduce_fusion
  11.3 0.0 copy-done
  11.3 2.5 fusion.16
  13.8 15.5 %all-to-all-start = ((bf16[32,24,768]{2,1,0:T(8,128)(2,1)}), bf16[32,24,768]{2,1,0:T(8,128)(2,1)S(1)}, u32[]{:S(2)}, u32[]{:S(2)}) async-start(bf16[32,24,768]{2,1,0:T(8,128)(2,1)} %bitcast.36), calls=%async_computation | async-start | bytes 2359296 | tf_op jit(solution)/shard_map/all_to_all | solution.py:74
  29.3 0.0 all-gather.6.cloned.1.call-start
  29.4 55.3 %all-gather.4.cloned.1.call-done = bf16[2,192,2048]{2,1,0:T(8,128)(2,1)} async-done(((bf16[2,48,2048]{2,1,0:T(8,128)(2,1)}), bf16[2,192,2048]{2,1,0:T(8,128)(2,1)}) %all-gather.4.cloned.1.call-update) | async-done | bytes 1572880 | tf_op jit(solution)/shard_map/all_gather | solution.py:54
  84.6 2.8 slice_bitcast_fusion
  87.4 0.0 all-to-all-done
  87.4 0.0 all-gather.6.cloned.1.call-update
  87.5 2.5 fusion.21
  89.9 10.4 %all-to-all-start.2 = ((bf16[32,24,768]{2,1,0:T(8,128)(2,1)}), bf16[32,24,768]{2,1,0:T(8,128)(2,1)}, u32[]{:S(2)}, u32[]{:S(2)}) async-start(bf16[32,24,768]{2,1,0:T(8,128)(2,1)} %bitcast.37), calls=%async_computation.2 | async-start | bytes 2359296 | tf_op jit(solution)/shard_map/all_to_all | solution.py:74
  100.3 30.9 %all-gather.6.cloned.1.call-done = bf16[768,2048]{1,0:T(8,128)(2,1)} async-done(((bf16[192,2048]{1,0:T(8,128)(2,1)}), bf16[768,2048]{1,0:T(8,128)(2,1)}) %all-gather.6.cloned.1.call-update) | async-done | bytes 3145744 | tf_op jit(solution)/shard_map/all_gather | solution.py:82
  131.3 5.8 %multiply_convert_fusion.1 = bf16[768,2048]{1,0:T(8,128)(2,1)} fusion(bf16[768,768]{1,0:T(8,128)(2,1)S(1)} %bitcast.35, bf16[768,2048]{1,0:T(8,128)(2,1)} %all-gather.6.cloned.1.call-done), kind=kOutput, calls=%fused_computation.1 | convolution fusion | flops 2419064832 | bytes 7471104 | tf_op jit(solution)/shard_map/dot_general | solution.py:86
  137.1 0.0 all-to-all-done.2
  137.1 13.0 %all-to-all-start.1 = ((bf16[32,24,2048]{2,1,0:T(8,128)(2,1)}), bf16[32,24,2048]{2,1,0:T(8,128)(2,1)}, u32[]{:S(2)}, u32[]{:S(2)}) async-start(bf16[32,24,2048]{2,1,0:T(8,128)(2,1)} %bitcast.34), calls=%async_computation.1 | async-start | bytes 6291456 | tf_op jit(solution)/shard_map/all_to_all | solution.py:89
  150.1 0.0 all-gather.8.cloned.1.call-start
  150.1 0.7 all-gather.8.cloned.1.call-update
  150.8 46.6 %all-gather.8.cloned.1.call-done = bf16[768,2048]{1,0:T(8,128)(2,1)} async-done(((bf16[192,2048]{1,0:T(8,128)(2,1)}), bf16[768,2048]{1,0:T(8,128)(2,1)}) %all-gather.8.cloned.1.call-update) | async-done | bytes 3145744 | tf_op jit(solution)/shard_map/all_gather | solution.py:82
  197.4 6.6 %multiply_convert_fusion = bf16[768,2048]{1,0:T(8,128)(2,1)} fusion(bf16[768,768]{1,0:T(8,128)(2,1)} %bitcast.7, bf16[768,2048]{1,0:T(8,128)(2,1)} %all-gather.8.cloned.1.call-done), kind=kOutput, calls=%fused_computation | convolution fusion | flops 2419064832 | bytes 7471104 | tf_op jit(solution)/shard_map/dot_general | solution.py:86
  204.0 28.2 %all-to-all-done.1 = bf16[32,24,2048]{2,1,0:T(8,128)(2,1)} async-done(((bf16[32,24,2048]{2,1,0:T(8,128)(2,1)}), bf16[32,24,2048]{2,1,0:T(8,128)(2,1)}, u32[]{:S(2)}, u32[]{:S(2)}) %all-to-all-start.1) | async-done | bytes 3145760 | tf_op jit(solution)/shard_map/all_to_all | solution.py:89
  232.2 0.0 copy-start.4
  232.2 9.3 %all-to-all-start.3 = ((bf16[32,24,2048]{2,1,0:T(8,128)(2,1)}), bf16[32,24,2048]{2,1,0:T(8,128)(2,1)}, u32[]{:S(2)}, u32[]{:S(2)}) async-start(bf16[32,24,2048]{2,1,0:T(8,128)(2,1)} %bitcast.33), calls=%async_computation.3 | async-start | bytes 6291456 | tf_op jit(solution)/shard_map/all_to_all | solution.py:89
  241.5 4.1 %collective-permute-start = (f32[2,48,2048]{2,1,0:T(8,128)}, f32[2,48,2048]{2,1,0:T(8,128)S(1)}, u32[]{:S(2)}, u32[]{:S(2)}) collective-permute-start(f32[2,48,2048]{2,1,0:T(8,128)} %get-tuple-element.15), channel_id=1, source_target_pairs={{0,256},{128,384},{256,0},{384,128},{1,257},{129,385},{257,1},{385... | collective-permute-start | bytes 2359304 | tf_op jit(solution)/shard_map/ppermute | solution.py:57
  245.6 0.1 reduce_sum.48
  245.7 0.1 copy.24
  245.9 0.0 copy-done.4
  245.9 0.1 copy.25
  246.0 0.1 copy.26
  246.1 3.8 %fusion.3 = (bf16[128,768]{1,0:T(8,128)(2,1)S(1)}, bf16[128,768]{1,0:T(8,128)(2,1)S(1)}, bf16[128,768]{1,0:T(8,128)(2,1)S(1)}, bf16[128,768]{1,0:T(8,128)(2,1)S(1)}) fusion(s32[768]{0:T(1024)S(1)} %get-tuple-element.20, f32[128,8]{1,0:T(8,128)S(1)} %copy.25, s32[128,8]{1,0:T(8,128)S(1)} %copy.24, s32[768]{0:T(1024)S(1)} %get-tuple-element.21, ...), kind=kLoop, calls=%fused_computation.11 | loop fusion | flops 7471104 | bytes 804864 | tf_op jit(solution)/shard_map/reduce_sum | solution.py:94
  249.9 14.8 %collective-permute-done = f32[2,48,2048]{2,1,0:T(8,128)S(1)} collective-permute-done((f32[2,48,2048]{2,1,0:T(8,128)}, f32[2,48,2048]{2,1,0:T(8,128)S(1)}, u32[]{:S(2)}, u32[]{:S(2)}) %collective-permute-start) | collective-permute-done | bytes 786464 | tf_op jit(solution)/shard_map/ppermute | solution.py:57
  264.7 0.0 copy-start.1
  264.7 2.8 fusion.55
  267.5 0.0 copy-done.1
  267.5 2.5 convolution_add_fusion.2
  270.0 52.4 %all-to-all-done.3 = bf16[32,24,2048]{2,1,0:T(8,128)(2,1)} async-done(((bf16[32,24,2048]{2,1,0:T(8,128)(2,1)}), bf16[32,24,2048]{2,1,0:T(8,128)(2,1)}, u32[]{:S(2)}, u32[]{:S(2)}) %all-to-all-start.3) | async-done | bytes 3145760 | tf_op jit(solution)/shard_map/all_to_all | solution.py:89
  322.5 2.5 convolution_add_fusion.1
  324.9 0.0 copy-start.2
  324.9 3.4 %fusion.9 = bf16[128,2048]{1,0:T(8,128)(2,1)} fusion(f32[128,2048]{1,0:T(8,128)S(1)} %convolution_add_fusion.1, bf16[768,2048]{1,0:T(8,128)(2,1)} %bitcast.10, bf16[128,768]{1,0:T(8,128)(2,1)S(1)} %get-tuple-element.13), kind=kOutput, calls=%fused_computation.20 | convolution fusion | flops 403177472 | bytes 4915200 | tf_op jit(solution)/shard_map/dot_general | solution.py:95
  328.3 0.0 copy-done.2
  328.3 0.9 copy.28
  (5 shorter events, 0.1 us)
Async XLA Ops:
  7.2 4.1 %copy-start = (bf16[128,8,768]{2,1,0:T(8,128)(2,1)S(1)}, bf16[128,8,768]{2,1,0:T(8,128)(2,1)}, u32[]{:S(2)}) copy-start(bf16[128,8,768]{2,1,0:T(8,128)(2,1)} %param.7) | copy-start | bytes 4718596
  7.2 3.3 copy-start.3
  7.2 77.5 %all-gather.4.cloned.1.call-start = ((), (), s32[]{:S(2)}) async-start(), calls=%async_computation.4 | async-start | bytes 1966080 | tf_op jit(solution)/shard_map/all_gather | solution.py:54
  13.8 73.7 %all-to-all-start = ((bf16[32,24,768]{2,1,0:T(8,128)(2,1)}), bf16[32,24,768]{2,1,0:T(8,128)(2,1)S(1)}, u32[]{:S(2)}, u32[]{:S(2)}) async-start(bf16[32,24,768]{2,1,0:T(8,128)(2,1)} %bitcast.36), calls=%async_computation | async-start | bytes 2359296 | tf_op jit(solution)/shard_map/all_to_all | solution.py:74
  29.3 102.0 %all-gather.6.cloned.1.call-start = ((), (), s32[]{:S(2)}) async-start(), calls=%async_computation.5 | async-start | bytes 3932160 | tf_op jit(solution)/shard_map/all_gather | solution.py:82
  89.9 47.2 %all-to-all-start.2 = ((bf16[32,24,768]{2,1,0:T(8,128)(2,1)}), bf16[32,24,768]{2,1,0:T(8,128)(2,1)}, u32[]{:S(2)}, u32[]{:S(2)}) async-start(bf16[32,24,768]{2,1,0:T(8,128)(2,1)} %bitcast.37), calls=%async_computation.2 | async-start | bytes 2359296 | tf_op jit(solution)/shard_map/all_to_all | solution.py:74
  137.1 95.1 %all-to-all-start.1 = ((bf16[32,24,2048]{2,1,0:T(8,128)(2,1)}), bf16[32,24,2048]{2,1,0:T(8,128)(2,1)}, u32[]{:S(2)}, u32[]{:S(2)}) async-start(bf16[32,24,2048]{2,1,0:T(8,128)(2,1)} %bitcast.34), calls=%async_computation.1 | async-start | bytes 6291456 | tf_op jit(solution)/shard_map/all_to_all | solution.py:89
  150.1 47.4 %all-gather.8.cloned.1.call-start = ((), (), s32[]{:S(2)}) async-start(), calls=%async_computation.6 | async-start | bytes 3932160 | tf_op jit(solution)/shard_map/all_gather | solution.py:82
  232.2 13.7 %copy-start.4 = (s32[128,8]{0,1:T(8,128)S(1)}, s32[128,8]{0,1:T(8,128)}, u32[]{:S(2)}) copy-start(s32[128,8]{0,1:T(8,128)} %param.9) | copy-start | bytes 12292
  232.2 90.2 %all-to-all-start.3 = ((bf16[32,24,2048]{2,1,0:T(8,128)(2,1)}), bf16[32,24,2048]{2,1,0:T(8,128)(2,1)}, u32[]{:S(2)}, u32[]{:S(2)}) async-start(bf16[32,24,2048]{2,1,0:T(8,128)(2,1)} %bitcast.33), calls=%async_computation.3 | async-start | bytes 6291456 | tf_op jit(solution)/shard_map/all_to_all | solution.py:89
  241.5 23.2 %collective-permute-start = (f32[2,48,2048]{2,1,0:T(8,128)}, f32[2,48,2048]{2,1,0:T(8,128)S(1)}, u32[]{:S(2)}, u32[]{:S(2)}) collective-permute-start(f32[2,48,2048]{2,1,0:T(8,128)} %get-tuple-element.15), channel_id=1, source_target_pairs={{0,256},{128,384},{256,0},{384,128},{1,257},{129,385},{257,1},{385... | collective-permute-start | bytes 2359304 | tf_op jit(solution)/shard_map/ppermute | solution.py:57
  264.7 2.8 copy-start.1
  324.9 3.4 %copy-start.2 = (f32[2,48,2048]{2,1,0:T(8,128)S(1)}, f32[2,48,2048]{2,1,0:T(8,128)}, u32[]{:S(2)}) copy-start(f32[2,48,2048]{2,1,0:T(8,128)} %copy-done.1) | copy-start | bytes 2359300
Sparse Core Ops, SparseCore 0:
  10.7 73.8 all-gather.3
  87.6 43.6 all-gather.5
  153.0 44.3 all-gather.7

commit v7 on v6

--- a/solution.py
+++ b/solution.py
@@ -51,7 +51,8 @@
     step_dir = adamw_step(master, moment_one, moment_two, gradient)
     updated = master - learn_rate * step_dir
     weights = updated.astype(jnp.bfloat16)
-    nearer = lax.all_gather(weights, "grp_1", axis=1, tiled=True)
+    inner = lax.axis_size("grp_1")
+    nearer = lax.all_gather(weights, "grp_0", axis=1, tiled=True)
 
     shift = outer // 2
     backup = lax.ppermute(step_dir, "grp_0", [(s, (s + shift) % outer) for s in range(outer)])
@@ -79,12 +80,14 @@
         rows, tie = lax.optimization_barrier((nearer[local], gathered[-1] if gathered else arrived[0]))
         if not gathered:
             arrived[0] = tie
-        gathered.append(lax.all_gather(rows, "grp_0", axis=0, tiled=True))
+        gathered.append(lax.all_gather(rows, "grp_1", axis=0, tiled=True))
 
     mixed = jnp.zeros((tok_count, width), jnp.float32)
     for local in range(local_experts):
-        product = jnp.dot(arrived[local].reshape(chunk, hidden_width), gathered[local],
-                          preferred_element_type=jnp.float32)
+        block = weights.shape[1]
+        product = jnp.einsum(
+            "cxzh,zxhd->cd", arrived[local].reshape(chunk, outer, inner, block),
+            gathered[local].reshape(inner, outer, block, width), preferred_element_type=jnp.float32)
         results = (product * scaling).astype(jnp.bfloat16)
         returned = lax.all_to_all(results.reshape(ranks, capacity, width), "ep",
                                   split_axis=0, concat_axis=0, tiled=True)

time: 336 us -> 410 us (1.22)
  waiting for transfers between devices: 229 us -> 291 us
  local copies, waits for them, and re-layouts: 4.33 us -> 14.8 us
  matrix products: 28.5 us -> 34.3 us
  starting transfers between devices: 52.4 us -> 48 us
    all_gather x3, waiting for transfers between devices: 133 us -> 211 us  [the longest x2 194 us: body(): gathered.append(lax.all_gather(rows, 'grp_1', axis=0, tiled=True))]
    all_to_all x2, waiting for transfers between devices: 80.6 us -> 52.8 us  [body(): lax.all_to_all(results.reshape(ranks, capacity, width), 'ep', split_axis=...]
    all_to_all x2, waiting for transfers between devices: 0.01 us -> 12.4 us  [body(): lax.all_to_all(outgoing.reshape(ranks, capacity, hidden_width), 'ep', spl...]
    reshape x0 -> x2, local copies, waits for them, and re-layouts: none -> 10.6 us  [body(): arrived[local].reshape(chunk, outer, inner, block)]
    dot_general x2, matrix products: 12.4 us -> 18.1 us  [body(): jnp.einsum('cxzh,zxhd->cd', arrived[local].reshape(chunk, outer, inner, b...]
  transfers between devices with their start and end apart: 8 -> 8, of which waited for: 6 -> 6; matrix products, arithmetic and copies ran while one was open for 9% -> 11% of each run, Pallas kernels for 0% -> 0%
where the time goes in v7:
time: 410 us; the launch traced here: 409 us
  waiting for transfers between devices  291 us (71%)
  starting transfers between devices  48 us (12%)
  matrix products  34.3 us (8%)
  local copies, waits for them, and re-layouts  14.8 us (4%)
  between operations  13.9 us (3%)
  other arithmetic  7.64 us (2%)
    all_gather x2, waiting for transfers between devices, body(): gathered.append(lax.all_gather(rows, 'grp_1', axis=0, tiled=True))  194 us
    all_to_all x2, waiting for transfers between devices, body(): lax.all_to_all(results.reshape(ranks, capacity, width), 'ep', split_axis=...  52.8 us
    all_to_all x2, starting transfers between devices, body(): lax.all_to_all(outgoing.reshape(ranks, capacity, hidden_width), 'ep', spl...  23.5 us
    all_to_all x2, starting transfers between devices, body(): lax.all_to_all(results.reshape(ranks, capacity, width), 'ep', split_axis=...  19.5 us
    dot_general x2, matrix products, body(): jnp.einsum('cxzh,zxhd->cd', arrived[local].reshape(chunk, outer, inner, b...  18.1 us
    all_gather x1, waiting for transfers between devices, body(): nearer = lax.all_gather(weights, 'grp_0', axis=1, tiled=True)  17.2 us
    ppermute x1, waiting for transfers between devices, body(): lax.ppermute(step_dir, 'grp_0', [(s, (s + shift) % outer) for s in range(...  14 us
    all_to_all x2, waiting for transfers between devices, body(): lax.all_to_all(outgoing.reshape(ranks, capacity, hidden_width), 'ep', spl...  12.4 us
  transfers between devices with their start and end apart: 8, of which 6 were waited for; matrix products, arithmetic and copies ran while one was open for 11% of the time, Pallas kernels for 0%

profile of v7, /device:TPU:56, one launch (start us, length us, event | category | flops | bytes accessed | tf_op | source)
XLA Modules:
  0.0 409.2 jit_solution(12001482716123442961)
XLA Ops:
  7.2 0.0 copy-start
  7.2 0.0 copy-start.3
  7.2 0.0 all-gather.4.cloned.1.call-start
  7.2 3.3 subtract_convert_fusion
  10.5 0.0 all-gather.4.cloned.1.call-update
  10.5 0.0 copy-done.3
  10.5 0.1 copy.32
  10.6 0.1 eq.33
  10.7 0.5 convert_reduce_fusion
  11.3 0.0 copy-done
  11.3 2.5 fusion.22
  13.8 15.5 %all-to-all-start = ((bf16[32,24,768]{2,1,0:T(8,128)(2,1)}), bf16[32,24,768]{2,1,0:T(8,128)(2,1)S(1)}, u32[]{:S(2)}, u32[]{:S(2)}) async-start(bf16[32,24,768]{2,1,0:T(8,128)(2,1)} %bitcast.44), calls=%async_computation | async-start | bytes 2359296 | tf_op jit(solution)/shard_map/all_to_all | solution.py:75
  29.3 0.0 all-gather.6.cloned.1.call-start
  29.4 17.2 %all-gather.4.cloned.1.call-done = bf16[2,192,2048]{2,1,0:T(8,128)(2,1)} async-done(((bf16[2,48,2048]{2,1,0:T(8,128)(2,1)}), bf16[2,192,2048]{2,1,0:T(8,128)(2,1)}) %all-gather.4.cloned.1.call-update) | async-done | bytes 1572880 | tf_op jit(solution)/shard_map/all_gather | solution.py:55
  46.6 2.7 slice_bitcast_fusion
  49.3 12.4 %all-to-all-done = bf16[32,24,768]{2,1,0:T(8,128)(2,1)S(1)} async-done(((bf16[32,24,768]{2,1,0:T(8,128)(2,1)}), bf16[32,24,768]{2,1,0:T(8,128)(2,1)S(1)}, u32[]{:S(2)}, u32[]{:S(2)}) %all-to-all-start) | async-done | bytes 1179680 | tf_op jit(solution)/shard_map/all_to_all | solution.py:75
  61.6 0.0 all-gather.6.cloned.1.call-update
  61.7 2.5 fusion.27
  64.2 7.9 %all-to-all-start.2 = ((bf16[32,24,768]{2,1,0:T(8,128)(2,1)}), bf16[32,24,768]{2,1,0:T(8,128)(2,1)}, u32[]{:S(2)}, u32[]{:S(2)}) async-start(bf16[32,24,768]{2,1,0:T(8,128)(2,1)} %bitcast.43), calls=%async_computation.2 | async-start | bytes 2359296 | tf_op jit(solution)/shard_map/all_to_all | solution.py:75
  72.1 0.0 all-gather.8.cloned.1.call-start
  72.2 4.8 %reshape.108 = bf16[768,4,4,48]{3,2,1,0:T(4,128)(2,1)} reshape(bf16[32,24,768]{2,1,0:T(8,128)(2,1)S(1)} %all-to-all-done) | data formatting | bytes 2359296 | tf_op jit(solution)/shard_map/reshape | solution.py:89
  76.9 74.6 %all-gather.6.cloned.1.call-done = bf16[768,2048]{1,0:T(8,128)(2,1)} async-done(((bf16[192,2048]{1,0:T(8,128)(2,1)}), bf16[768,2048]{1,0:T(8,128)(2,1)}) %all-gather.6.cloned.1.call-update) | async-done | bytes 3145744 | tf_op jit(solution)/shard_map/all_gather | solution.py:83
  151.5 0.0 all-gather.8.cloned.1.call-update
  151.5 9.1 %fusion.1 = bf16[768,2048]{1,0:T(8,128)(2,1)} fusion(bf16[4,4,48,2048]{3,2,1,0:T(8,128)(2,1)} %bitcast.45, bf16[768,4,4,48]{3,2,1,0:T(4,128)(2,1)} %reshape.108), kind=kOutput, calls=%fused_computation.3 | convolution fusion | flops 2419064832 | bytes 7471104 | tf_op jit(solution)/shard_map/cxzh,zxhd->cd/dot_general | solution.py:88
  160.6 0.0 all-to-all-done.2
  160.6 11.2 %all-to-all-start.1 = ((bf16[32,24,2048]{2,1,0:T(8,128)(2,1)}), bf16[32,24,2048]{2,1,0:T(8,128)(2,1)}, u32[]{:S(2)}, u32[]{:S(2)}) async-start(bf16[32,24,2048]{2,1,0:T(8,128)(2,1)} %bitcast.42), calls=%async_computation.1 | async-start | bytes 6291456 | tf_op jit(solution)/shard_map/all_to_all | solution.py:92
  171.7 5.8 %reshape.113 = bf16[768,4,4,48]{3,2,1,0:T(4,128)(2,1)} reshape(bf16[32,24,768]{2,1,0:T(8,128)(2,1)} %all-to-all-done.2) | data formatting | bytes 2359296 | tf_op jit(solution)/shard_map/reshape | solution.py:89
  177.5 119.6 %all-gather.8.cloned.1.call-done = bf16[768,2048]{1,0:T(8,128)(2,1)} async-done(((bf16[192,2048]{1,0:T(8,128)(2,1)}), bf16[768,2048]{1,0:T(8,128)(2,1)}) %all-gather.8.cloned.1.call-update) | async-done | bytes 3145744 | tf_op jit(solution)/shard_map/all_gather | solution.py:83
  297.1 9.1 %fusion = bf16[768,2048]{1,0:T(8,128)(2,1)} fusion(bf16[4,4,48,2048]{3,2,1,0:T(8,128)(2,1)} %bitcast.46, bf16[768,4,4,48]{3,2,1,0:T(4,128)(2,1)} %reshape.113), kind=kOutput, calls=%fused_computation.1 | convolution fusion | flops 2419064832 | bytes 7471104 | tf_op jit(solution)/shard_map/cxzh,zxhd->cd/dot_general | solution.py:88
  306.2 0.0 all-to-all-done.1
  306.2 8.4 %all-to-all-start.3 = ((bf16[32,24,2048]{2,1,0:T(8,128)(2,1)}), bf16[32,24,2048]{2,1,0:T(8,128)(2,1)}, u32[]{:S(2)}, u32[]{:S(2)}) async-start(bf16[32,24,2048]{2,1,0:T(8,128)(2,1)} %bitcast.41), calls=%async_computation.3 | async-start | bytes 6291456 | tf_op jit(solution)/shard_map/all_to_all | solution.py:92
  314.6 4.9 %collective-permute-start = (f32[2,48,2048]{2,1,0:T(8,128)}, f32[2,48,2048]{2,1,0:T(8,128)S(1)}, u32[]{:S(2)}, u32[]{:S(2)}) collective-permute-start(f32[2,48,2048]{2,1,0:T(8,128)} %get-tuple-element.15), channel_id=1, source_target_pairs={{0,256},{128,384},{256,0},{384,128},{1,257},{129,385},{257,1},{385... | collective-permute-start | bytes 2359304 | tf_op jit(solution)/shard_map/ppermute | solution.py:58
  319.5 0.1 reduce_sum.48
  319.6 0.1 copy.34
  319.7 0.0 copy-done.4
  319.8 0.1 copy.35
  319.9 0.1 copy.38
  320.0 3.8 fusion.5
  323.8 14.0 %collective-permute-done = f32[2,48,2048]{2,1,0:T(8,128)S(1)} collective-permute-done((f32[2,48,2048]{2,1,0:T(8,128)}, f32[2,48,2048]{2,1,0:T(8,128)S(1)}, u32[]{:S(2)}, u32[]{:S(2)}) %collective-permute-start) | collective-permute-done | bytes 786464 | tf_op jit(solution)/shard_map/ppermute | solution.py:58
  337.8 2.8 fusion.61
  340.6 0.0 copy-done.1
  340.6 2.5 convolution_add_fusion.2
  343.1 52.8 %all-to-all-done.3 = bf16[32,24,2048]{2,1,0:T(8,128)(2,1)} async-done(((bf16[32,24,2048]{2,1,0:T(8,128)(2,1)}), bf16[32,24,2048]{2,1,0:T(8,128)(2,1)}, u32[]{:S(2)}, u32[]{:S(2)}) %all-to-all-start.3) | async-done | bytes 3145760 | tf_op jit(solution)/shard_map/all_to_all | solution.py:92
  395.9 2.5 convolution_add_fusion.1
  398.4 0.0 copy-start.2
  398.4 3.4 fusion.15
  401.7 0.0 copy-done.2
  401.7 0.9 copy.52
  (7 shorter events, 0.1 us)
Async XLA Ops:
  7.2 4.1 %copy-start = (bf16[128,8,768]{2,1,0:T(8,128)(2,1)S(1)}, bf16[128,8,768]{2,1,0:T(8,128)(2,1)}, u32[]{:S(2)}) copy-start(bf16[128,8,768]{2,1,0:T(8,128)(2,1)} %param.7) | copy-start | bytes 4718596
  7.2 3.3 copy-start.3
  7.2 39.4 %all-gather.4.cloned.1.call-start = ((), (), s32[]{:S(2)}) async-start(), calls=%async_computation.4 | async-start | bytes 1966080 | tf_op jit(solution)/shard_map/all_gather | solution.py:55
  13.8 47.9 %all-to-all-start = ((bf16[32,24,768]{2,1,0:T(8,128)(2,1)}), bf16[32,24,768]{2,1,0:T(8,128)(2,1)S(1)}, u32[]{:S(2)}, u32[]{:S(2)}) async-start(bf16[32,24,768]{2,1,0:T(8,128)(2,1)} %bitcast.44), calls=%async_computation | async-start | bytes 2359296 | tf_op jit(solution)/shard_map/all_to_all | solution.py:75
  29.3 122.2 %all-gather.6.cloned.1.call-start = ((), (), s32[]{:S(2)}) async-start(), calls=%async_computation.5 | async-start | bytes 3932160 | tf_op jit(solution)/shard_map/all_gather | solution.py:83
  64.2 96.4 %all-to-all-start.2 = ((bf16[32,24,768]{2,1,0:T(8,128)(2,1)}), bf16[32,24,768]{2,1,0:T(8,128)(2,1)}, u32[]{:S(2)}, u32[]{:S(2)}) async-start(bf16[32,24,768]{2,1,0:T(8,128)(2,1)} %bitcast.43), calls=%async_computation.2 | async-start | bytes 2359296 | tf_op jit(solution)/shard_map/all_to_all | solution.py:75
  72.1 225.0 %all-gather.8.cloned.1.call-start = ((), (), s32[]{:S(2)}) async-start(), calls=%async_computation.6 | async-start | bytes 3932160 | tf_op jit(solution)/shard_map/all_gather | solution.py:83
  160.6 145.6 %all-to-all-start.1 = ((bf16[32,24,2048]{2,1,0:T(8,128)(2,1)}), bf16[32,24,2048]{2,1,0:T(8,128)(2,1)}, u32[]{:S(2)}, u32[]{:S(2)}) async-start(bf16[32,24,2048]{2,1,0:T(8,128)(2,1)} %bitcast.42), calls=%async_computation.1 | async-start | bytes 6291456 | tf_op jit(solution)/shard_map/all_to_all | solution.py:92
  306.2 13.6 %copy-start.4 = (s32[128,8]{0,1:T(8,128)S(1)}, s32[128,8]{0,1:T(8,128)}, u32[]{:S(2)}) copy-start(s32[128,8]{0,1:T(8,128)} %param.9) | copy-start | bytes 12292
  306.2 89.7 %all-to-all-start.3 = ((bf16[32,24,2048]{2,1,0:T(8,128)(2,1)}), bf16[32,24,2048]{2,1,0:T(8,128)(2,1)}, u32[]{:S(2)}, u32[]{:S(2)}) async-start(bf16[32,24,2048]{2,1,0:T(8,128)(2,1)} %bitcast.41), calls=%async_computation.3 | async-start | bytes 6291456 | tf_op jit(solution)/shard_map/all_to_all | solution.py:92
  314.6 23.2 %collective-permute-start = (f32[2,48,2048]{2,1,0:T(8,128)}, f32[2,48,2048]{2,1,0:T(8,128)S(1)}, u32[]{:S(2)}, u32[]{:S(2)}) collective-permute-start(f32[2,48,2048]{2,1,0:T(8,128)} %get-tuple-element.15), channel_id=1, source_target_pairs={{0,256},{128,384},{256,0},{384,128},{1,257},{129,385},{257,1},{385... | collective-permute-start | bytes 2359304 | tf_op jit(solution)/shard_map/ppermute | solution.py:58
  337.8 2.8 copy-start.1
  398.4 3.4 copy-start.2
Sparse Core Ops, SparseCore 0:
  10.7 35.8 all-gather.3
  61.8 89.6 all-gather.5
  153.6 143.4 all-gather.7

commit v8 on v6

--- a/solution.py
+++ b/solution.py
@@ -71,14 +71,16 @@
         slot_of.append(((column // capacity) * local_experts + local) * capacity + column % capacity)
         placing = (positions[None, :] == slot_of[local][:, None]).astype(jnp.bfloat16)
         outgoing = jnp.dot(placing, hidden_rows, preferred_element_type=jnp.float32).astype(jnp.bfloat16)
+        if local == 0:
+            outgoing, nearer = lax.optimization_barrier((outgoing, nearer))
         arrived.append(lax.all_to_all(outgoing.reshape(ranks, capacity, hidden_width), "ep",
                                       split_axis=0, concat_axis=0, tiled=True))
 
     gathered = []
     for local in range(local_experts):
-        rows, tie = lax.optimization_barrier((nearer[local], gathered[-1] if gathered else arrived[0]))
-        if not gathered:
-            arrived[0] = tie
+        rows = nearer[local]
+        if gathered:
+            rows, _ = lax.optimization_barrier((rows, gathered[-1]))
         gathered.append(lax.all_gather(rows, "grp_0", axis=0, tiled=True))
 
     mixed = jnp.zeros((tok_count, width), jnp.float32)

time: 336 us -> 341 us (1.015)
  waiting for transfers between devices: 229 us -> 242 us
  starting transfers between devices: 52.4 us -> 43.1 us
    all_to_all x2, waiting for transfers between devices: 0.01 us -> 54.1 us  [body(): lax.all_to_all(outgoing.reshape(ranks, capacity, hidden_width), 'ep', spl...]
    all_gather x2, waiting for transfers between devices: 77.6 us -> 47.7 us  [body(): gathered.append(lax.all_gather(rows, 'grp_0', axis=0, tiled=True))]
    all_gather x1, waiting for transfers between devices: 55.3 us -> 45.7 us  [body(): nearer = lax.all_gather(weights, 'grp_1', axis=1, tiled=True)]
    all_to_all x2, starting transfers between devices: 26 us -> 19.1 us  [body(): lax.all_to_all(outgoing.reshape(ranks, capacity, hidden_width), 'ep', spl...]
    all_to_all x2, starting transfers between devices: 22.3 us -> 18.8 us  [body(): lax.all_to_all(results.reshape(ranks, capacity, width), 'ep', split_axis=...]
  transfers between devices with their start and end apart: 8 -> 8, of which waited for: 6 -> 7; matrix products, arithmetic and copies ran while one was open for 9% -> 8% of each run, Pallas kernels for 0% -> 0%
where the time goes in v8:
time: 341 us
  waiting for transfers between devices  242 us (71%)
  starting transfers between devices  43.1 us (13%)
  matrix products  28.5 us (8%)
  between operations  13.9 us (4%)
  other arithmetic  7.64 us (2%)
  local copies, waits for them, and re-layouts  5.41 us (2%)
    all_to_all x2, waiting for transfers between devices, body(): lax.all_to_all(results.reshape(ranks, capacity, width), 'ep', split_axis=...  80.1 us
    all_to_all x2, waiting for transfers between devices, body(): lax.all_to_all(outgoing.reshape(ranks, capacity, hidden_width), 'ep', spl...  54.1 us
    all_gather x2, waiting for transfers between devices, body(): gathered.append(lax.all_gather(rows, 'grp_0', axis=0, tiled=True))  47.7 us
    all_gather x1, waiting for transfers between devices, body(): nearer = lax.all_gather(weights, 'grp_1', axis=1, tiled=True)  45.7 us
    all_to_all x2, starting transfers between devices, body(): lax.all_to_all(outgoing.reshape(ranks, capacity, hidden_width), 'ep', spl...  19.1 us
    all_to_all x2, starting transfers between devices, body(): lax.all_to_all(results.reshape(ranks, capacity, width), 'ep', split_axis=...  18.8 us
    ppermute x1, waiting for transfers between devices, body(): lax.ppermute(step_dir, 'grp_0', [(s, (s + shift) % outer) for s in range(...  13.8 us
    dot_general x2, matrix products, body(): jnp.dot(arrived[local].reshape(chunk, hidden_width), gathered[local], pre...  12.4 us
  transfers between devices with their start and end apart: 8, of which 7 were waited for; matrix products, arithmetic and copies ran while one was open for 8% of the time, Pallas kernels for 0%

profile of v8, /device:TPU:56, one launch (start us, length us, event | category | flops | bytes accessed | tf_op | source)
XLA Modules:
  0.0 340.8 jit_solution(15805539583538224107)
XLA Ops:
  7.2 0.0 copy-start
  7.2 0.0 copy-start.4
  7.2 0.0 all-gather.5.cloned.1.call-start
  7.2 3.3 subtract_convert_fusion
  10.5 0.0 all-gather.5.cloned.1.call-update
  10.5 0.0 all-gather.9.cloned.1.call-start
  10.6 0.0 copy-done.4
  10.6 0.1 copy.22
  10.7 0.1 eq.33
  10.8 0.5 convert_reduce_fusion
  11.3 0.0 copy-done
  11.3 2.5 fusion.16
  13.8 45.7 %all-gather.5.cloned.1.call-done = bf16[2,192,2048]{2,1,0:T(8,128)(2,1)} async-done(((bf16[2,48,2048]{2,1,0:T(8,128)(2,1)}), bf16[2,192,2048]{2,1,0:T(8,128)(2,1)}) %all-gather.5.cloned.1.call-update) | async-done | bytes 1572880 | tf_op jit(solution)/shard_map/all_gather | solution.py:54
  59.5 2.7 slice_bitcast_fusion
  62.3 0.0 all-gather.9.cloned.1.call-update
  62.3 10.9 %all-to-all-start = ((bf16[32,24,768]{2,1,0:T(8,128)(2,1)}), bf16[32,24,768]{2,1,0:T(8,128)(2,1)S(1)}, u32[]{:S(2)}, u32[]{:S(2)}) async-start(bf16[32,24,768]{2,1,0:T(8,128)(2,1)} %bitcast.1), calls=%async_computation | async-start | bytes 2359296 | tf_op jit(solution)/shard_map/all_to_all | solution.py:76
  73.2 2.5 fusion.21
  75.7 29.3 %all-to-all-done = bf16[32,24,768]{2,1,0:T(8,128)(2,1)S(1)} async-done(((bf16[32,24,768]{2,1,0:T(8,128)(2,1)}), bf16[32,24,768]{2,1,0:T(8,128)(2,1)S(1)}, u32[]{:S(2)}, u32[]{:S(2)}) %all-to-all-start) | async-done | bytes 1179680 | tf_op jit(solution)/shard_map/all_to_all | solution.py:76
  104.9 0.0 copy-start.1
  104.9 1.1 copy-done.1
  106.0 8.2 %all-to-all-start.2 = ((bf16[32,24,768]{2,1,0:T(8,128)(2,1)}), bf16[32,24,768]{2,1,0:T(8,128)(2,1)S(1)}, u32[]{:S(2)}, u32[]{:S(2)}) async-start(bf16[32,24,768]{2,1,0:T(8,128)(2,1)} %bitcast.37), calls=%async_computation.2 | async-start | bytes 2359296 | tf_op jit(solution)/shard_map/all_to_all | solution.py:76
  114.3 0.0 all-gather.9.cloned.1.call-done
  114.3 6.5 %multiply_convert_fusion.1 = bf16[768,2048]{1,0:T(8,128)(2,1)} fusion(bf16[768,768]{1,0:T(8,128)(2,1)} %bitcast.36, bf16[1,768,2048]{2,1,0:T(8,128)(2,1)} %all-gather.9.cloned.1.call-done), kind=kOutput, calls=%fused_computation.1 | convolution fusion | flops 2419064832 | bytes 7471104 | tf_op jit(solution)/shard_map/dot_general | solution.py:88
  120.8 24.9 %all-to-all-done.2 = bf16[32,24,768]{2,1,0:T(8,128)(2,1)S(1)} async-done(((bf16[32,24,768]{2,1,0:T(8,128)(2,1)}), bf16[32,24,768]{2,1,0:T(8,128)(2,1)S(1)}, u32[]{:S(2)}, u32[]{:S(2)}) %all-to-all-start.2) | async-done | bytes 1179680 | tf_op jit(solution)/shard_map/all_to_all | solution.py:76
  145.7 9.5 %all-to-all-start.1 = ((bf16[32,24,2048]{2,1,0:T(8,128)(2,1)}), bf16[32,24,2048]{2,1,0:T(8,128)(2,1)}, u32[]{:S(2)}, u32[]{:S(2)}) async-start(bf16[32,24,2048]{2,1,0:T(8,128)(2,1)} %bitcast.34), calls=%async_computation.1 | async-start | bytes 6291456 | tf_op jit(solution)/shard_map/all_to_all | solution.py:91
  155.2 0.0 all-gather.7.cloned.1.call-start
  155.2 0.7 all-gather.7.cloned.1.call-update
  155.9 47.7 %all-gather.7.cloned.1.call-done = bf16[768,2048]{1,0:T(8,128)(2,1)} async-done(((bf16[192,2048]{1,0:T(8,128)(2,1)}), bf16[768,2048]{1,0:T(8,128)(2,1)}) %all-gather.7.cloned.1.call-update) | async-done | bytes 3145744 | tf_op jit(solution)/shard_map/all_gather | solution.py:84
  203.6 5.9 %multiply_convert_fusion = bf16[768,2048]{1,0:T(8,128)(2,1)} fusion(bf16[768,768]{1,0:T(8,128)(2,1)S(1)} %bitcast.35, bf16[768,2048]{1,0:T(8,128)(2,1)} %all-gather.7.cloned.1.call-done), kind=kOutput, calls=%fused_computation | convolution fusion | flops 2419064832 | bytes 7471104 | tf_op jit(solution)/shard_map/dot_general | solution.py:88
  209.5 26.9 %all-to-all-done.1 = bf16[32,24,2048]{2,1,0:T(8,128)(2,1)} async-done(((bf16[32,24,2048]{2,1,0:T(8,128)(2,1)}), bf16[32,24,2048]{2,1,0:T(8,128)(2,1)}, u32[]{:S(2)}, u32[]{:S(2)}) %all-to-all-start.1) | async-done | bytes 3145760 | tf_op jit(solution)/shard_map/all_to_all | solution.py:91
  236.4 9.3 %all-to-all-start.3 = ((bf16[32,24,2048]{2,1,0:T(8,128)(2,1)}), bf16[32,24,2048]{2,1,0:T(8,128)(2,1)}, u32[]{:S(2)}, u32[]{:S(2)}) async-start(bf16[32,24,2048]{2,1,0:T(8,128)(2,1)} %bitcast.33), calls=%async_computation.3 | async-start | bytes 6291456 | tf_op jit(solution)/shard_map/all_to_all | solution.py:91
  245.7 5.1 %collective-permute-start = (f32[2,48,2048]{2,1,0:T(8,128)}, f32[2,48,2048]{2,1,0:T(8,128)S(1)}, u32[]{:S(2)}, u32[]{:S(2)}) collective-permute-start(f32[2,48,2048]{2,1,0:T(8,128)} %get-tuple-element.15), channel_id=1, source_target_pairs={{0,256},{128,384},{256,0},{384,128},{1,257},{129,385},{257,1},{385... | collective-permute-start | bytes 2359304 | tf_op jit(solution)/shard_map/ppermute | solution.py:57
  250.8 0.1 reduce_sum.48
  250.9 0.1 copy.24
  251.0 0.0 copy-done.5
  251.1 0.1 copy.25
  251.2 0.1 copy.26
  251.3 3.8 %fusion.3 = (bf16[128,768]{1,0:T(8,128)(2,1)S(1)}, bf16[128,768]{1,0:T(8,128)(2,1)S(1)}, bf16[128,768]{1,0:T(8,128)(2,1)S(1)}, bf16[128,768]{1,0:T(8,128)(2,1)S(1)}) fusion(s32[768]{0:T(1024)S(1)} %fusion.49, f32[128,8]{1,0:T(8,128)S(1)} %copy.25, s32[128,8]{1,0:T(8,128)S(1)} %copy.24, s32[768]{0:T(1024)S(1)} %fusion.50, f32[128,8]{1,0:T(8,128)S(1)} %copy.26), kind=kLoop, calls=%fused_computation.11 | loop fusion | flops 7471104 | bytes 804864 | tf_op jit(solution)/shard_map/reduce_sum | solution.py:96
  255.1 13.8 %collective-permute-done = f32[2,48,2048]{2,1,0:T(8,128)S(1)} collective-permute-done((f32[2,48,2048]{2,1,0:T(8,128)}, f32[2,48,2048]{2,1,0:T(8,128)S(1)}, u32[]{:S(2)}, u32[]{:S(2)}) %collective-permute-start) | collective-permute-done | bytes 786464 | tf_op jit(solution)/shard_map/ppermute | solution.py:57
  268.9 2.8 fusion.56
  271.7 0.0 copy-done.2
  271.7 2.5 convolution_add_fusion.2
  274.2 53.3 %all-to-all-done.3 = bf16[32,24,2048]{2,1,0:T(8,128)(2,1)} async-done(((bf16[32,24,2048]{2,1,0:T(8,128)(2,1)}), bf16[32,24,2048]{2,1,0:T(8,128)(2,1)}, u32[]{:S(2)}, u32[]{:S(2)}) %all-to-all-start.3) | async-done | bytes 3145760 | tf_op jit(solution)/shard_map/all_to_all | solution.py:91
  327.5 2.5 convolution_add_fusion.1
  330.0 0.0 copy-start.3
  330.0 3.4 fusion.9
  333.4 0.0 copy-done.3
  333.4 0.9 copy.28
  (8 shorter events, 0.1 us)
Async XLA Ops:
  7.2 4.2 %copy-start = (bf16[128,8,768]{2,1,0:T(8,128)(2,1)S(1)}, bf16[128,8,768]{2,1,0:T(8,128)(2,1)}, u32[]{:S(2)}) copy-start(bf16[128,8,768]{2,1,0:T(8,128)(2,1)} %param.7) | copy-start | bytes 4718596
  7.2 3.4 copy-start.4
  7.2 52.3 %all-gather.5.cloned.1.call-start = ((), (), s32[]{:S(2)}) async-start(), calls=%async_computation.4 | async-start | bytes 1966080 | tf_op jit(solution)/shard_map/all_gather | solution.py:54
  10.5 103.8 %all-gather.9.cloned.1.call-start = ((), (), s32[]{:S(2)}) async-start(), calls=%async_computation.6 | async-start | bytes 3932160 | tf_op jit(solution)/shard_map/all_gather | solution.py:84
  62.3 42.6 %all-to-all-start = ((bf16[32,24,768]{2,1,0:T(8,128)(2,1)}), bf16[32,24,768]{2,1,0:T(8,128)(2,1)S(1)}, u32[]{:S(2)}, u32[]{:S(2)}) async-start(bf16[32,24,768]{2,1,0:T(8,128)(2,1)} %bitcast.1), calls=%async_computation | async-start | bytes 2359296 | tf_op jit(solution)/shard_map/all_to_all | solution.py:76
  104.9 1.1 copy-start.1
  106.0 39.6 %all-to-all-start.2 = ((bf16[32,24,768]{2,1,0:T(8,128)(2,1)}), bf16[32,24,768]{2,1,0:T(8,128)(2,1)S(1)}, u32[]{:S(2)}, u32[]{:S(2)}) async-start(bf16[32,24,768]{2,1,0:T(8,128)(2,1)} %bitcast.37), calls=%async_computation.2 | async-start | bytes 2359296 | tf_op jit(solution)/shard_map/all_to_all | solution.py:76
  145.7 90.7 %all-to-all-start.1 = ((bf16[32,24,2048]{2,1,0:T(8,128)(2,1)}), bf16[32,24,2048]{2,1,0:T(8,128)(2,1)}, u32[]{:S(2)}, u32[]{:S(2)}) async-start(bf16[32,24,2048]{2,1,0:T(8,128)(2,1)} %bitcast.34), calls=%async_computation.1 | async-start | bytes 6291456 | tf_op jit(solution)/shard_map/all_to_all | solution.py:91
  155.2 48.4 %all-gather.7.cloned.1.call-start = ((), (), s32[]{:S(2)}) async-start(), calls=%async_computation.5 | async-start | bytes 3932160 | tf_op jit(solution)/shard_map/all_gather | solution.py:84
  236.4 14.7 %copy-start.5 = (s32[128,8]{0,1:T(8,128)S(1)}, s32[128,8]{0,1:T(8,128)}, u32[]{:S(2)}) copy-start(s32[128,8]{0,1:T(8,128)} %param.9) | copy-start | bytes 12292
  236.4 91.1 %all-to-all-start.3 = ((bf16[32,24,2048]{2,1,0:T(8,128)(2,1)}), bf16[32,24,2048]{2,1,0:T(8,128)(2,1)}, u32[]{:S(2)}, u32[]{:S(2)}) async-start(bf16[32,24,2048]{2,1,0:T(8,128)(2,1)} %bitcast.33), calls=%async_computation.3 | async-start | bytes 6291456 | tf_op jit(solution)/shard_map/all_to_all | solution.py:91
  245.7 23.2 %collective-permute-start = (f32[2,48,2048]{2,1,0:T(8,128)}, f32[2,48,2048]{2,1,0:T(8,128)S(1)}, u32[]{:S(2)}, u32[]{:S(2)}) collective-permute-start(f32[2,48,2048]{2,1,0:T(8,128)} %get-tuple-element.15), channel_id=1, source_target_pairs={{0,256},{128,384},{256,0},{384,128},{1,257},{129,385},{257,1},{385... | collective-permute-start | bytes 2359304 | tf_op jit(solution)/shard_map/ppermute | solution.py:57
  268.9 2.8 copy-start.2
  330.0 3.4 copy-start.3
Sparse Core Ops, SparseCore 0:
  10.7 48.7 all-gather.4
  62.4 44.1 all-gather.8
  158.1 45.4 all-gather.6

commit v9 on v6

--- a/solution.py
+++ b/solution.py
@@ -66,13 +66,15 @@
 
     column = lax.broadcasted_iota(jnp.int32, (chunk,), 0)
     slot_of = []
-    arrived = []
     for local in range(local_experts):
         slot_of.append(((column // capacity) * local_experts + local) * capacity + column % capacity)
-        placing = (positions[None, :] == slot_of[local][:, None]).astype(jnp.bfloat16)
-        outgoing = jnp.dot(placing, hidden_rows, preferred_element_type=jnp.float32).astype(jnp.bfloat16)
-        arrived.append(lax.all_to_all(outgoing.reshape(ranks, capacity, hidden_width), "ep",
-                                      split_axis=0, concat_axis=0, tiled=True))
+    every_slot = lax.broadcasted_iota(jnp.int32, (slots,), 0)
+    placing = (positions[None, :] == every_slot[:, None]).astype(jnp.bfloat16)
+    outgoing = jnp.dot(placing, hidden_rows, preferred_element_type=jnp.float32).astype(jnp.bfloat16)
+    delivered = lax.all_to_all(outgoing.reshape(ranks, local_experts * capacity, hidden_width), "ep",
+                               split_axis=0, concat_axis=0, tiled=True)
+    delivered = delivered.reshape(ranks, local_experts, capacity, hidden_width)
+    arrived = [delivered[:, local] for local in range(local_experts)]
 
     gathered = []
     for local in range(local_experts):

time: 336 us -> 369 us (1.098)
  waiting for transfers between devices: 229 us -> 271 us
  starting transfers between devices: 52.4 us -> 42 us
    all_gather x1, waiting for transfers between devices: 55.3 us -> 81.3 us  [body(): nearer = lax.all_gather(weights, 'grp_1', axis=1, tiled=True)]
    all_gather x2, waiting for transfers between devices: 77.6 us -> 92 us  [body(): gathered.append(lax.all_gather(rows, 'grp_0', axis=0, tiled=True))]
    all_to_all x2 -> x1, starting transfers between devices: 26 us -> 15.7 us  [body(): lax.all_to_all(outgoing.reshape(ranks, local_experts * capacity, hidden_w...]
  transfers between devices with their start and end apart: 8 -> 7, of which waited for: 6 -> 6; matrix products, arithmetic and copies ran while one was open for 9% -> 5% of each run, Pallas kernels for 0% -> 0%
where the time goes in v9:
time: 369 us; the launch traced here: 368 us
  waiting for transfers between devices  271 us (73%)
  starting transfers between devices  42 us (11%)
  matrix products  27.6 us (7%)
  between operations  13.9 us (4%)
  local copies, waits for them, and re-layouts  7.94 us (2%)
  other arithmetic  6.06 us (2%)
    all_gather x2, waiting for transfers between devices, body(): gathered.append(lax.all_gather(rows, 'grp_0', axis=0, tiled=True))  92 us
    all_to_all x2, waiting for transfers between devices, body(): lax.all_to_all(results.reshape(ranks, capacity, width), 'ep', split_axis=...  81.8 us
    all_gather x1, waiting for transfers between devices, body(): nearer = lax.all_gather(weights, 'grp_1', axis=1, tiled=True)  81.3 us
    all_to_all x2, starting transfers between devices, body(): lax.all_to_all(results.reshape(ranks, capacity, width), 'ep', split_axis=...  22.3 us
    all_to_all x1, starting transfers between devices, body(): lax.all_to_all(outgoing.reshape(ranks, local_experts * capacity, hidden_w...  15.7 us
    ppermute x1, waiting for transfers between devices, body(): lax.ppermute(step_dir, 'grp_0', [(s, (s + shift) % outer) for s in range(...  14.9 us
    dot_general x2, matrix products, body(): jnp.dot(arrived[local].reshape(chunk, hidden_width), gathered[local], pre...  12.4 us
    dot_general x4, matrix products, body(): jnp.dot(weight, returned, preferred_element_type=jnp.float32)  11.1 us
  transfers between devices with their start and end apart: 7, of which 6 were waited for; matrix products, arithmetic and copies ran while one was open for 5% of the time, Pallas kernels for 0%

profile of v9, /device:TPU:56, one launch (start us, length us, event | category | flops | bytes accessed | tf_op | source)
XLA Modules:
  0.0 368.4 jit_solution(865088306051186930)
XLA Ops:
  7.2 0.0 copy-start
  7.2 0.9 copy.22
  8.1 0.1 eq.29
  8.2 0.5 convert_reduce_fusion
  8.7 0.0 copy-done
  8.7 4.0 %fusion.2 = bf16[1536,768]{1,0:T(8,128)(2,1)} fusion(s32[1024]{0:T(1024)S(1)} %multiply_add_fusion, bf16[128,8,768]{2,1,0:T(8,128)(2,1)S(1)} %copy-done), kind=kOutput, calls=%fused_computation.11 | convolution fusion | flops 2418671616 | bytes 3936256 | tf_op jit(solution)/shard_map/dot_general | solution.py:73
  12.8 0.0 copy-start.3
  12.8 15.7 %all-to-all-start = ((bf16[32,48,768]{2,1,0:T(8,128)(2,1)}), bf16[32,48,768]{2,1,0:T(8,128)(2,1)}, u32[]{:S(2)}, u32[]{:S(2)}) async-start(bf16[32,48,768]{2,1,0:T(8,128)(2,1)} %bitcast.31), calls=%async_computation | async-start | bytes 4718592 | tf_op jit(solution)/shard_map/all_to_all | solution.py:74
  28.5 0.0 all-gather.4.cloned.1.call-start
  28.6 0.0 copy-done.3
  28.6 0.0 copy-done.4
  28.6 0.0 copy-done.5
  28.6 0.0 copy-done.6
  28.6 1.7 subtract_convert_fusion
  30.3 0.0 all-gather.4.cloned.1.call-update
  30.3 0.0 all-gather.6.cloned.1.call-start
  30.4 81.3 %all-gather.4.cloned.1.call-done = bf16[2,192,2048]{2,1,0:T(8,128)(2,1)} async-done(((bf16[2,48,2048]{2,1,0:T(8,128)(2,1)}), bf16[2,192,2048]{2,1,0:T(8,128)(2,1)}) %all-gather.4.cloned.1.call-update) | async-done | bytes 1572880 | tf_op jit(solution)/shard_map/all_gather | solution.py:54
  111.7 2.8 slice_bitcast_fusion.1
  114.4 0.0 all-to-all-done
  114.4 2.8 fusion.39
  117.3 0.0 all-gather.6.cloned.1.call-update
  117.3 45.4 %all-gather.6.cloned.1.call-done = bf16[768,2048]{1,0:T(8,128)(2,1)} async-done(((bf16[192,2048]{1,0:T(8,128)(2,1)}), bf16[768,2048]{1,0:T(8,128)(2,1)}) %all-gather.6.cloned.1.call-update) | async-done | bytes 3145744 | tf_op jit(solution)/shard_map/all_gather | solution.py:84
  162.7 6.5 %multiply_convert_fusion.1 = bf16[768,2048]{1,0:T(8,128)(2,1)} fusion(bf16[768,768]{1,0:T(8,128)(2,1)} %bitcast.33, bf16[768,2048]{1,0:T(8,128)(2,1)} %all-gather.6.cloned.1.call-done), kind=kOutput, calls=%fused_computation.1 | convolution fusion | flops 2419064832 | bytes 7471104 | tf_op jit(solution)/shard_map/dot_general | solution.py:88
  169.2 13.0 %all-to-all-start.1 = ((bf16[32,24,2048]{2,1,0:T(8,128)(2,1)}), bf16[32,24,2048]{2,1,0:T(8,128)(2,1)}, u32[]{:S(2)}, u32[]{:S(2)}) async-start(bf16[32,24,2048]{2,1,0:T(8,128)(2,1)} %bitcast.30), calls=%async_computation.1 | async-start | bytes 6291456 | tf_op jit(solution)/shard_map/all_to_all | solution.py:91
  182.2 0.0 all-gather.8.cloned.1.call-start
  182.2 0.7 all-gather.8.cloned.1.call-update
  182.9 46.6 %all-gather.8.cloned.1.call-done = bf16[768,2048]{1,0:T(8,128)(2,1)} async-done(((bf16[192,2048]{1,0:T(8,128)(2,1)}), bf16[768,2048]{1,0:T(8,128)(2,1)}) %all-gather.8.cloned.1.call-update) | async-done | bytes 3145744 | tf_op jit(solution)/shard_map/all_gather | solution.py:84
  229.5 5.9 %multiply_convert_fusion = bf16[768,2048]{1,0:T(8,128)(2,1)} fusion(bf16[768,768]{1,0:T(8,128)(2,1)S(1)} %bitcast.32, bf16[768,2048]{1,0:T(8,128)(2,1)} %all-gather.8.cloned.1.call-done), kind=kOutput, calls=%fused_computation | convolution fusion | flops 2419064832 | bytes 7471104 | tf_op jit(solution)/shard_map/dot_general | solution.py:88
  235.4 28.9 %all-to-all-done.1 = bf16[32,24,2048]{2,1,0:T(8,128)(2,1)} async-done(((bf16[32,24,2048]{2,1,0:T(8,128)(2,1)}), bf16[32,24,2048]{2,1,0:T(8,128)(2,1)}, u32[]{:S(2)}, u32[]{:S(2)}) %all-to-all-start.1) | async-done | bytes 3145760 | tf_op jit(solution)/shard_map/all_to_all | solution.py:91
  264.4 9.3 %all-to-all-start.2 = ((bf16[32,24,2048]{2,1,0:T(8,128)(2,1)}), bf16[32,24,2048]{2,1,0:T(8,128)(2,1)}, u32[]{:S(2)}, u32[]{:S(2)}) async-start(bf16[32,24,2048]{2,1,0:T(8,128)(2,1)} %bitcast.29), calls=%async_computation.2 | async-start | bytes 6291456 | tf_op jit(solution)/shard_map/all_to_all | solution.py:91
  273.7 3.9 %collective-permute-start = (f32[2,48,2048]{2,1,0:T(8,128)}, f32[2,48,2048]{2,1,0:T(8,128)S(1)}, u32[]{:S(2)}, u32[]{:S(2)}) collective-permute-start(f32[2,48,2048]{2,1,0:T(8,128)} %get-tuple-element.15), channel_id=1, source_target_pairs={{0,256},{128,384},{256,0},{384,128},{1,257},{129,385},{257,1},{385... | collective-permute-start | bytes 2359304 | tf_op jit(solution)/shard_map/ppermute | solution.py:57
  277.6 0.1 reduce_sum.48
  277.8 0.0 copy-done.7
  277.8 0.1 copy.24
  277.9 0.0 copy-done.8
  277.9 0.1 copy.25
  278.0 0.1 copy.26
  278.1 3.8 %fusion.5 = (bf16[128,768]{1,0:T(8,128)(2,1)S(1)}, bf16[128,768]{1,0:T(8,128)(2,1)S(1)}, bf16[128,768]{1,0:T(8,128)(2,1)S(1)}, bf16[128,768]{1,0:T(8,128)(2,1)S(1)}) fusion(s32[768]{0:T(1024)S(1)} %get-tuple-element.22, f32[128,8]{1,0:T(8,128)S(1)} %copy.25, s32[128,8]{1,0:T(8,128)S(1)} %copy.24, s32[768]{0:T(1024)S(1)} %get-tuple-element.23, ...), kind=kLoop, calls=%fused_computation.14 | loop fusion | flops 7471104 | bytes 804864 | tf_op jit(solution)/shard_map/reduce_sum | solution.py:96
  282.0 14.9 %collective-permute-done = f32[2,48,2048]{2,1,0:T(8,128)S(1)} collective-permute-done((f32[2,48,2048]{2,1,0:T(8,128)}, f32[2,48,2048]{2,1,0:T(8,128)S(1)}, u32[]{:S(2)}, u32[]{:S(2)}) %collective-permute-start) | collective-permute-done | bytes 786464 | tf_op jit(solution)/shard_map/ppermute | solution.py:57
  296.9 2.8 fusion.40
  299.7 0.0 copy-done.1
  299.7 2.5 convolution_add_fusion.2
  302.2 52.9 %all-to-all-done.2 = bf16[32,24,2048]{2,1,0:T(8,128)(2,1)} async-done(((bf16[32,24,2048]{2,1,0:T(8,128)(2,1)}), bf16[32,24,2048]{2,1,0:T(8,128)(2,1)}, u32[]{:S(2)}, u32[]{:S(2)}) %all-to-all-start.2) | async-done | bytes 3145760 | tf_op jit(solution)/shard_map/all_to_all | solution.py:91
  355.1 2.5 convolution_add_fusion.1
  357.6 0.0 copy-start.2
  357.6 3.4 fusion.8
  361.0 0.0 copy-done.2
  361.0 0.9 copy.28
  (11 shorter events, 0.1 us)
Async XLA Ops:
  7.2 1.6 copy-start
  12.8 15.8 %copy-start.3 = (f32[2,48,2048]{2,1,0:T(8,128)S(1)}, f32[2,48,2048]{2,1,0:T(8,128)}, u32[]{:S(2)}) copy-start(f32[2,48,2048]{2,1,0:T(8,128)} %param.10) | copy-start | bytes 2359300
  12.8 15.8 %copy-start.4 = (bf16[2,48,2048]{2,1,0:T(8,128)(2,1)S(1)}, bf16[2,48,2048]{2,1,0:T(8,128)(2,1)}, u32[]{:S(2)}) copy-start(bf16[2,48,2048]{2,1,0:T(8,128)(2,1)} %param.12) | copy-start | bytes 1179652
  12.8 15.8 %copy-start.5 = (bf16[2,48,2048]{2,1,0:T(8,128)(2,1)S(1)}, bf16[2,48,2048]{2,1,0:T(8,128)(2,1)}, u32[]{:S(2)}) copy-start(bf16[2,48,2048]{2,1,0:T(8,128)(2,1)} %param.13) | copy-start | bytes 1179652
  12.8 15.8 %copy-start.6 = (bf16[2,48,2048]{2,1,0:T(8,128)(2,1)S(1)}, bf16[2,48,2048]{2,1,0:T(8,128)(2,1)}, u32[]{:S(2)}) copy-start(bf16[2,48,2048]{2,1,0:T(8,128)(2,1)} %param.11) | copy-start | bytes 1179652
  12.8 101.7 %all-to-all-start = ((bf16[32,48,768]{2,1,0:T(8,128)(2,1)}), bf16[32,48,768]{2,1,0:T(8,128)(2,1)}, u32[]{:S(2)}, u32[]{:S(2)}) async-start(bf16[32,48,768]{2,1,0:T(8,128)(2,1)} %bitcast.31), calls=%async_computation | async-start | bytes 4718592 | tf_op jit(solution)/shard_map/all_to_all | solution.py:74
  28.5 83.2 %all-gather.4.cloned.1.call-start = ((), (), s32[]{:S(2)}) async-start(), calls=%async_computation.3 | async-start | bytes 1966080 | tf_op jit(solution)/shard_map/all_gather | solution.py:54
  30.3 132.4 %all-gather.6.cloned.1.call-start = ((), (), s32[]{:S(2)}) async-start(), calls=%async_computation.4 | async-start | bytes 3932160 | tf_op jit(solution)/shard_map/all_gather | solution.py:84
  169.2 95.2 %all-to-all-start.1 = ((bf16[32,24,2048]{2,1,0:T(8,128)(2,1)}), bf16[32,24,2048]{2,1,0:T(8,128)(2,1)}, u32[]{:S(2)}, u32[]{:S(2)}) async-start(bf16[32,24,2048]{2,1,0:T(8,128)(2,1)} %bitcast.30), calls=%async_computation.1 | async-start | bytes 6291456 | tf_op jit(solution)/shard_map/all_to_all | solution.py:91
  182.2 47.4 %all-gather.8.cloned.1.call-start = ((), (), s32[]{:S(2)}) async-start(), calls=%async_computation.5 | async-start | bytes 3932160 | tf_op jit(solution)/shard_map/all_gather | solution.py:84
  264.4 13.4 %copy-start.7 = (s32[128,8]{0,1:T(8,128)S(1)}, s32[128,8]{0,1:T(8,128)}, u32[]{:S(2)}) copy-start(s32[128,8]{0,1:T(8,128)} %param.8) | copy-start | bytes 12292
  264.4 13.5 %copy-start.8 = (s32[128,8]{0,1:T(8,128)S(1)}, s32[128,8]{0,1:T(8,128)}, u32[]{:S(2)}) copy-start(s32[128,8]{0,1:T(8,128)} %param.9) | copy-start | bytes 12292
  264.4 90.7 %all-to-all-start.2 = ((bf16[32,24,2048]{2,1,0:T(8,128)(2,1)}), bf16[32,24,2048]{2,1,0:T(8,128)(2,1)}, u32[]{:S(2)}, u32[]{:S(2)}) async-start(bf16[32,24,2048]{2,1,0:T(8,128)(2,1)} %bitcast.29), calls=%async_computation.2 | async-start | bytes 6291456 | tf_op jit(solution)/shard_map/all_to_all | solution.py:91
  273.7 23.2 %collective-permute-start = (f32[2,48,2048]{2,1,0:T(8,128)}, f32[2,48,2048]{2,1,0:T(8,128)S(1)}, u32[]{:S(2)}, u32[]{:S(2)}) collective-permute-start(f32[2,48,2048]{2,1,0:T(8,128)} %get-tuple-element.15), channel_id=1, source_target_pairs={{0,256},{128,384},{256,0},{384,128},{1,257},{129,385},{257,1},{385... | collective-permute-start | bytes 2359304 | tf_op jit(solution)/shard_map/ppermute | solution.py:57
  296.9 2.8 copy-start.1
  357.6 3.4 copy-start.2
Sparse Core Ops, SparseCore 0:
  32.0 79.6 all-gather.3
  117.4 45.2 all-gather.5
  185.1 44.3 all-gather.7

commit v10 on v6

--- a/solution.py
+++ b/solution.py
@@ -51,7 +51,6 @@
     step_dir = adamw_step(master, moment_one, moment_two, gradient)
     updated = master - learn_rate * step_dir
     weights = updated.astype(jnp.bfloat16)
-    nearer = lax.all_gather(weights, "grp_1", axis=1, tiled=True)
 
     shift = outer // 2
     backup = lax.ppermute(step_dir, "grp_0", [(s, (s + shift) % outer) for s in range(outer)])
@@ -76,7 +75,11 @@
 
     gathered = []
     for local in range(local_experts):
-        rows, tie = lax.optimization_barrier((nearer[local], gathered[-1] if gathered else arrived[0]))
+        own = weights[local]
+        if gathered:
+            own, _ = lax.optimization_barrier((own, gathered[-1]))
+        rows = lax.all_gather(own, "grp_1", axis=0, tiled=True)
+        rows, tie = lax.optimization_barrier((rows, gathered[-1] if gathered else arrived[0]))
         if not gathered:
             arrived[0] = tie
         gathered.append(lax.all_gather(rows, "grp_0", axis=0, tiled=True))

time: 336 us -> 380 us (1.13)
  blocking collectives: 0 us -> 128 us
  waiting for transfers between devices: 229 us -> 143 us
    all_gather x0 -> x2, blocking collectives: none -> 128 us  [body(): rows = lax.all_gather(own, 'grp_1', axis=0, tiled=True)]
    all_gather x1 -> x0, waiting for transfers between devices: 55.3 us -> none  [body(): nearer = lax.all_gather(weights, 'grp_1', axis=1, tiled=True)]
    all_to_all x2, waiting for transfers between devices: 80.6 us -> 53.6 us  [body(): lax.all_to_all(results.reshape(ranks, capacity, width), 'ep', split_axis=...]
  transfers between devices with their start and end apart: 8 -> 7, of which waited for: 6 -> 4; matrix products, arithmetic and copies ran while one was open for 9% -> 7% of each run, Pallas kernels for 0% -> 0%
where the time goes in v10:
time: 380 us; the launch traced here: 379 us
  waiting for transfers between devices  143 us (38%)
  blocking collectives  128 us (34%)
  starting transfers between devices  55.8 us (15%)
  matrix products  28.5 us (8%)
  between operations  14.2 us (4%)
  other arithmetic  7.17 us (2%)
    all_gather x2, blocking collectives, body(): rows = lax.all_gather(own, 'grp_1', axis=0, tiled=True)  128 us
    all_gather x2, waiting for transfers between devices, body(): gathered.append(lax.all_gather(rows, 'grp_0', axis=0, tiled=True))  74.2 us
    all_to_all x2, waiting for transfers between devices, body(): lax.all_to_all(results.reshape(ranks, capacity, width), 'ep', split_axis=...  53.6 us
    all_to_all x2, starting transfers between devices, body(): lax.all_to_all(results.reshape(ranks, capacity, width), 'ep', split_axis=...  26.1 us
    all_to_all x2, starting transfers between devices, body(): lax.all_to_all(outgoing.reshape(ranks, capacity, hidden_width), 'ep', spl...  25.7 us
    ppermute x1, waiting for transfers between devices, body(): lax.ppermute(step_dir, 'grp_0', [(s, (s + shift) % outer) for s in range(...  14.9 us
    dot_general x2, matrix products, body(): jnp.dot(arrived[local].reshape(chunk, hidden_width), gathered[local], pre...  12.4 us
    dot_general x4, matrix products, body(): jnp.dot(weight, returned, preferred_element_type=jnp.float32)  11.1 us
  transfers between devices with their start and end apart: 7, of which 4 were waited for; matrix products, arithmetic and copies ran while one was open for 7% of the time, Pallas kernels for 0%

profile of v10, /device:TPU:56, one launch (start us, length us, event | category | flops | bytes accessed | tf_op | source)
XLA Modules:
  0.0 379.3 jit_solution(1374798150363957229)
XLA Ops:
  7.2 0.0 copy-start
  7.2 0.9 copy.22
  8.1 0.1 eq.33
  8.2 0.5 convert_reduce_fusion
  8.7 0.0 copy-done
  8.7 0.0 copy-start.3
  8.7 2.5 fusion.16
  11.2 15.5 %all-to-all-start = ((bf16[32,24,768]{2,1,0:T(8,128)(2,1)}), bf16[32,24,768]{2,1,0:T(8,128)(2,1)S(1)}, u32[]{:S(2)}, u32[]{:S(2)}) async-start(bf16[32,24,768]{2,1,0:T(8,128)(2,1)} %bitcast.36), calls=%async_computation | async-start | bytes 2359296 | tf_op jit(solution)/shard_map/all_to_all | solution.py:73
  26.8 0.0 all-gather.4.cloned.1.call-start
  26.8 0.0 copy-done.3
  26.8 2.8 subtract_convert_fusion
  29.7 41.2 %all-gather = bf16[1,192,2048]{2,1,0:T(8,128)(2,1)} all-gather(bf16[1,48,2048]{2,1,0:T(8,128)(2,1)S(1)} %get-tuple-element.19), channel_id=2, replica_groups=mesh['grp_0'=4,'grp_1'=4,'ep'=32] {'grp_1'}, dimensions={1}, use_global_device_ids=true | all-gather | bytes 983040 | tf_op jit(solution)/shard_map/all_gather | solution.py:81
  70.8 0.0 all-to-all-done
  70.8 0.0 all-gather.4.cloned.1.call-update
  70.8 2.5 fusion.21
  73.3 10.2 %all-to-all-start.2 = ((bf16[32,24,768]{2,1,0:T(8,128)(2,1)}), bf16[32,24,768]{2,1,0:T(8,128)(2,1)}, u32[]{:S(2)}, u32[]{:S(2)}) async-start(bf16[32,24,768]{2,1,0:T(8,128)(2,1)} %bitcast.37), calls=%async_computation.2 | async-start | bytes 2359296 | tf_op jit(solution)/shard_map/all_to_all | solution.py:73
  83.5 30.9 %all-gather.4.cloned.1.call-done = bf16[768,2048]{1,0:T(8,128)(2,1)} async-done(((bf16[192,2048]{1,0:T(8,128)(2,1)}), bf16[768,2048]{1,0:T(8,128)(2,1)}) %all-gather.4.cloned.1.call-update) | async-done | bytes 3145744 | tf_op jit(solution)/shard_map/all_gather | solution.py:85
  114.4 5.8 %multiply_convert_fusion.1 = bf16[768,2048]{1,0:T(8,128)(2,1)} fusion(bf16[768,768]{1,0:T(8,128)(2,1)S(1)} %bitcast.35, bf16[768,2048]{1,0:T(8,128)(2,1)} %all-gather.4.cloned.1.call-done), kind=kOutput, calls=%fused_computation.1 | convolution fusion | flops 2419064832 | bytes 7471104 | tf_op jit(solution)/shard_map/dot_general | solution.py:89
  120.3 0.0 all-to-all-done.2
  120.3 13.0 %all-to-all-start.1 = ((bf16[32,24,2048]{2,1,0:T(8,128)(2,1)}), bf16[32,24,2048]{2,1,0:T(8,128)(2,1)}, u32[]{:S(2)}, u32[]{:S(2)}) async-start(bf16[32,24,2048]{2,1,0:T(8,128)(2,1)} %bitcast.33), calls=%async_computation.1 | async-start | bytes 6291456 | tf_op jit(solution)/shard_map/all_to_all | solution.py:92
  133.2 0.0 all-gather.6.cloned.1.call-start
  133.3 87.2 %all_gather.14 = bf16[192,2048]{1,0:T(8,128)(2,1)} all-gather(bf16[48,2048]{1,0:T(8,128)(2,1)S(1)} %get-tuple-element.8), channel_id=1, replica_groups=mesh['grp_0'=4,'grp_1'=4,'ep'=32] {'grp_1'}, dimensions={0}, use_global_device_ids=true | all-gather | bytes 983040 | tf_op jit(solution)/shard_map/all_gather | solution.py:81
  220.5 0.0 all-gather.6.cloned.1.call-update
  220.5 43.3 %all-gather.6.cloned.1.call-done = bf16[768,2048]{1,0:T(8,128)(2,1)} async-done(((bf16[192,2048]{1,0:T(8,128)(2,1)}), bf16[768,2048]{1,0:T(8,128)(2,1)}) %all-gather.6.cloned.1.call-update) | async-done | bytes 3145744 | tf_op jit(solution)/shard_map/all_gather | solution.py:85
  263.9 6.6 %multiply_convert_fusion = bf16[768,2048]{1,0:T(8,128)(2,1)} fusion(bf16[768,768]{1,0:T(8,128)(2,1)} %bitcast.7, bf16[768,2048]{1,0:T(8,128)(2,1)} %all-gather.6.cloned.1.call-done), kind=kOutput, calls=%fused_computation | convolution fusion | flops 2419064832 | bytes 7471104 | tf_op jit(solution)/shard_map/dot_general | solution.py:89
  270.4 0.0 all-to-all-done.1
  270.4 0.0 copy-start.4
  270.4 0.0 copy-start.5
  270.4 13.1 %all-to-all-start.3 = ((bf16[32,24,2048]{2,1,0:T(8,128)(2,1)}), bf16[32,24,2048]{2,1,0:T(8,128)(2,1)}, u32[]{:S(2)}, u32[]{:S(2)}) async-start(bf16[32,24,2048]{2,1,0:T(8,128)(2,1)} %bitcast.32), calls=%async_computation.3 | async-start | bytes 6291456 | tf_op jit(solution)/shard_map/all_to_all | solution.py:92
  283.5 4.0 %collective-permute-start = (f32[2,48,2048]{2,1,0:T(8,128)}, f32[2,48,2048]{2,1,0:T(8,128)S(1)}, u32[]{:S(2)}, u32[]{:S(2)}) collective-permute-start(f32[2,48,2048]{2,1,0:T(8,128)} %get-tuple-element.17), channel_id=1, source_target_pairs={{0,256},{128,384},{256,0},{384,128},{1,257},{129,385},{257,1},{385... | collective-permute-start | bytes 2359304 | tf_op jit(solution)/shard_map/ppermute | solution.py:56
  287.6 0.1 reduce_sum.48
  287.7 0.0 copy-done.4
  287.7 0.1 copy.24
  287.8 0.0 copy-done.5
  287.8 0.1 copy.25
  287.9 0.1 copy.26
  288.0 3.8 %fusion.3 = (bf16[128,768]{1,0:T(8,128)(2,1)S(1)}, bf16[128,768]{1,0:T(8,128)(2,1)S(1)}, bf16[128,768]{1,0:T(8,128)(2,1)S(1)}, bf16[128,768]{1,0:T(8,128)(2,1)S(1)}) fusion(s32[768]{0:T(1024)S(1)} %get-tuple-element.22, f32[128,8]{1,0:T(8,128)S(1)} %copy.25, s32[128,8]{1,0:T(8,128)S(1)} %copy.24, s32[768]{0:T(1024)S(1)} %get-tuple-element.23, ...), kind=kLoop, calls=%fused_computation.11 | loop fusion | flops 7471104 | bytes 804864 | tf_op jit(solution)/shard_map/reduce_sum | solution.py:97
  291.9 14.9 %collective-permute-done = f32[2,48,2048]{2,1,0:T(8,128)S(1)} collective-permute-done((f32[2,48,2048]{2,1,0:T(8,128)}, f32[2,48,2048]{2,1,0:T(8,128)S(1)}, u32[]{:S(2)}, u32[]{:S(2)}) %collective-permute-start) | collective-permute-done | bytes 786464 | tf_op jit(solution)/shard_map/ppermute | solution.py:56
  306.7 0.0 copy-start.1
  306.7 2.8 fusion.55
  309.5 0.0 copy-done.1
  309.6 2.5 convolution_add_fusion.2
  312.1 53.6 %all-to-all-done.3 = bf16[32,24,2048]{2,1,0:T(8,128)(2,1)} async-done(((bf16[32,24,2048]{2,1,0:T(8,128)(2,1)}), bf16[32,24,2048]{2,1,0:T(8,128)(2,1)}, u32[]{:S(2)}, u32[]{:S(2)}) %all-to-all-start.3) | async-done | bytes 3145760 | tf_op jit(solution)/shard_map/all_to_all | solution.py:92
  365.7 2.5 convolution_add_fusion.1
  368.2 0.0 copy-start.2
  368.2 3.4 fusion.9
  371.5 0.0 copy-done.2
  371.5 0.9 copy.28
  (6 shorter events, 0.1 us)
Async XLA Ops:
  7.2 1.6 copy-start
  8.7 18.1 %copy-start.3 = (f32[2,48,2048]{2,1,0:T(8,128)S(1)}, f32[2,48,2048]{2,1,0:T(8,128)}, u32[]{:S(2)}) copy-start(f32[2,48,2048]{2,1,0:T(8,128)} %param.10) | copy-start | bytes 2359300
  11.2 59.6 %all-to-all-start = ((bf16[32,24,768]{2,1,0:T(8,128)(2,1)}), bf16[32,24,768]{2,1,0:T(8,128)(2,1)S(1)}, u32[]{:S(2)}, u32[]{:S(2)}) async-start(bf16[32,24,768]{2,1,0:T(8,128)(2,1)} %bitcast.36), calls=%async_computation | async-start | bytes 2359296 | tf_op jit(solution)/shard_map/all_to_all | solution.py:73
  26.8 87.7 %all-gather.4.cloned.1.call-start = ((), (), s32[]{:S(2)}) async-start(), calls=%async_computation.4 | async-start | bytes 3932160 | tf_op jit(solution)/shard_map/all_gather | solution.py:85
  73.3 46.9 %all-to-all-start.2 = ((bf16[32,24,768]{2,1,0:T(8,128)(2,1)}), bf16[32,24,768]{2,1,0:T(8,128)(2,1)}, u32[]{:S(2)}, u32[]{:S(2)}) async-start(bf16[32,24,768]{2,1,0:T(8,128)(2,1)} %bitcast.37), calls=%async_computation.2 | async-start | bytes 2359296 | tf_op jit(solution)/shard_map/all_to_all | solution.py:73
  120.3 150.2 %all-to-all-start.1 = ((bf16[32,24,2048]{2,1,0:T(8,128)(2,1)}), bf16[32,24,2048]{2,1,0:T(8,128)(2,1)}, u32[]{:S(2)}, u32[]{:S(2)}) async-start(bf16[32,24,2048]{2,1,0:T(8,128)(2,1)} %bitcast.33), calls=%async_computation.1 | async-start | bytes 6291456 | tf_op jit(solution)/shard_map/all_to_all | solution.py:92
  133.2 130.6 %all-gather.6.cloned.1.call-start = ((), (), s32[]{:S(2)}) async-start(), calls=%async_computation.5 | async-start | bytes 3932160 | tf_op jit(solution)/shard_map/all_gather | solution.py:85
  270.4 17.3 %copy-start.4 = (s32[128,8]{0,1:T(8,128)S(1)}, s32[128,8]{0,1:T(8,128)}, u32[]{:S(2)}) copy-start(s32[128,8]{0,1:T(8,128)} %param.8) | copy-start | bytes 12292
  270.4 17.4 %copy-start.5 = (s32[128,8]{0,1:T(8,128)S(1)}, s32[128,8]{0,1:T(8,128)}, u32[]{:S(2)}) copy-start(s32[128,8]{0,1:T(8,128)} %param.9) | copy-start | bytes 12292
  270.4 95.2 %all-to-all-start.3 = ((bf16[32,24,2048]{2,1,0:T(8,128)(2,1)}), bf16[32,24,2048]{2,1,0:T(8,128)(2,1)}, u32[]{:S(2)}, u32[]{:S(2)}) async-start(bf16[32,24,2048]{2,1,0:T(8,128)(2,1)} %bitcast.32), calls=%async_computation.3 | async-start | bytes 6291456 | tf_op jit(solution)/shard_map/all_to_all | solution.py:92
  283.5 23.2 %collective-permute-start = (f32[2,48,2048]{2,1,0:T(8,128)}, f32[2,48,2048]{2,1,0:T(8,128)S(1)}, u32[]{:S(2)}, u32[]{:S(2)}) collective-permute-start(f32[2,48,2048]{2,1,0:T(8,128)} %get-tuple-element.17), channel_id=1, source_target_pairs={{0,256},{128,384},{256,0},{384,128},{1,257},{129,385},{257,1},{385... | collective-permute-start | bytes 2359304 | tf_op jit(solution)/shard_map/ppermute | solution.py:56
  306.7 2.8 copy-start.1
  368.2 3.4 copy-start.2
Sparse Core Ops, SparseCore 0:
  71.0 43.4 all-gather.3
  220.7 43.1 all-gather.5

commit v11 on v10

--- a/solution.py
+++ b/solution.py
@@ -74,11 +74,13 @@
                                       split_axis=0, concat_axis=0, tiled=True))
 
     gathered = []
+    first_stage = []
     for local in range(local_experts):
         own = weights[local]
-        if gathered:
-            own, _ = lax.optimization_barrier((own, gathered[-1]))
+        if first_stage:
+            own, _ = lax.optimization_barrier((own, arrived[0]))
         rows = lax.all_gather(own, "grp_1", axis=0, tiled=True)
+        first_stage.append(rows)
         rows, tie = lax.optimization_barrier((rows, gathered[-1] if gathered else arrived[0]))
         if not gathered:
             arrived[0] = tie
@@ -89,6 +91,8 @@
         product = jnp.dot(arrived[local].reshape(chunk, hidden_width), gathered[local],
                           preferred_element_type=jnp.float32)
         results = (product * scaling).astype(jnp.bfloat16)
+        if local + 1 < local_experts:
+            results, _ = lax.optimization_barrier((results, first_stage[local + 1]))
         returned = lax.all_to_all(results.reshape(ranks, capacity, width), "ep",
                                   split_axis=0, concat_axis=0, tiled=True)
         returned = returned.reshape(chunk, width)

time: 380 us -> 328 us (0.86)
  blocking collectives: 128 us -> 84.2 us
  starting transfers between devices: 55.8 us -> 49.1 us
    all_gather x2, blocking collectives: 128 us -> 84.2 us  [body(): rows = lax.all_gather(own, 'grp_1', axis=0, tiled=True)]
    all_gather x2, waiting for transfers between devices: 74.2 us -> 47.7 us  [body(): gathered.append(lax.all_gather(rows, 'grp_0', axis=0, tiled=True))]
    all_to_all x2, waiting for transfers between devices: 53.6 us -> 79.2 us  [body(): lax.all_to_all(results.reshape(ranks, capacity, width), 'ep', split_axis=...]
    all_to_all x2, starting transfers between devices: 26.1 us -> 18.4 us  [body(): lax.all_to_all(results.reshape(ranks, capacity, width), 'ep', split_axis=...]
  transfers between devices with their start and end apart: 7 -> 7, of which waited for: 4 -> 4; matrix products, arithmetic and copies ran while one was open for 7% -> 8% of each run, Pallas kernels for 0% -> 0%
where the time goes in v11:
time: 328 us; the launch traced here: 327 us
  waiting for transfers between devices  142 us (43%)
  blocking collectives  84.2 us (26%)
  starting transfers between devices  49.1 us (15%)
  matrix products  28.5 us (9%)
  between operations  14.2 us (4%)
  other arithmetic  7.17 us (2%)
    all_gather x2, blocking collectives, body(): rows = lax.all_gather(own, 'grp_1', axis=0, tiled=True)  84.2 us
    all_to_all x2, waiting for transfers between devices, body(): lax.all_to_all(results.reshape(ranks, capacity, width), 'ep', split_axis=...  79.2 us
    all_gather x2, waiting for transfers between devices, body(): gathered.append(lax.all_gather(rows, 'grp_0', axis=0, tiled=True))  47.7 us
    all_to_all x2, starting transfers between devices, body(): lax.all_to_all(outgoing.reshape(ranks, capacity, hidden_width), 'ep', spl...  25.7 us
    all_to_all x2, starting transfers between devices, body(): lax.all_to_all(results.reshape(ranks, capacity, width), 'ep', split_axis=...  18.4 us
    ppermute x1, waiting for transfers between devices, body(): lax.ppermute(step_dir, 'grp_0', [(s, (s + shift) % outer) for s in range(...  13.9 us
    dot_general x2, matrix products, body(): jnp.dot(arrived[local].reshape(chunk, hidden_width), gathered[local], pre...  12.4 us
    dot_general x4, matrix products, body(): jnp.dot(weight, returned, preferred_element_type=jnp.float32)  11.1 us
  transfers between devices with their start and end apart: 7, of which 4 were waited for; matrix products, arithmetic and copies ran while one was open for 8% of the time, Pallas kernels for 0%

profile of v11, /device:TPU:56, one launch (start us, length us, event | category | flops | bytes accessed | tf_op | source)
XLA Modules:
  0.0 327.1 jit_solution(3572648515389846336)
XLA Ops:
  7.2 0.0 copy-start
  7.2 0.9 copy.22
  8.1 0.1 eq.33
  8.2 0.5 convert_reduce_fusion
  8.7 0.0 copy-done
  8.7 0.0 copy-start.3
  8.7 2.5 fusion.16
  11.2 15.5 %all-to-all-start = ((bf16[32,24,768]{2,1,0:T(8,128)(2,1)}), bf16[32,24,768]{2,1,0:T(8,128)(2,1)S(1)}, u32[]{:S(2)}, u32[]{:S(2)}) async-start(bf16[32,24,768]{2,1,0:T(8,128)(2,1)} %bitcast.37), calls=%async_computation | async-start | bytes 2359296 | tf_op jit(solution)/shard_map/all_to_all | solution.py:73
  26.8 0.0 all-gather.4.cloned.1.call-start
  26.8 0.0 copy-done.3
  26.8 2.8 subtract_convert_fusion
  29.7 41.2 %all-gather = bf16[1,192,2048]{2,1,0:T(8,128)(2,1)} all-gather(bf16[1,48,2048]{2,1,0:T(8,128)(2,1)S(1)} %get-tuple-element.21), channel_id=2, replica_groups=mesh['grp_0'=4,'grp_1'=4,'ep'=32] {'grp_1'}, dimensions={1}, use_global_device_ids=true | all-gather | bytes 983040 | tf_op jit(solution)/shard_map/all_gather | solution.py:82
  70.8 0.0 all-to-all-done
  70.8 0.0 all-gather.4.cloned.1.call-update
  70.8 2.5 fusion.21
  73.3 10.2 %all-to-all-start.2 = ((bf16[32,24,768]{2,1,0:T(8,128)(2,1)}), bf16[32,24,768]{2,1,0:T(8,128)(2,1)}, u32[]{:S(2)}, u32[]{:S(2)}) async-start(bf16[32,24,768]{2,1,0:T(8,128)(2,1)} %bitcast.36), calls=%async_computation.2 | async-start | bytes 2359296 | tf_op jit(solution)/shard_map/all_to_all | solution.py:73
  83.5 43.1 %all_gather.14 = bf16[192,2048]{1,0:T(8,128)(2,1)} all-gather(bf16[48,2048]{1,0:T(8,128)(2,1)S(1)} %get-tuple-element.9), channel_id=1, replica_groups=mesh['grp_0'=4,'grp_1'=4,'ep'=32] {'grp_1'}, dimensions={0}, use_global_device_ids=true | all-gather | bytes 983040 | tf_op jit(solution)/shard_map/all_gather | solution.py:82
  126.6 0.0 all-gather.4.cloned.1.call-done
  126.6 5.8 %multiply_convert_fusion.1 = bf16[768,2048]{1,0:T(8,128)(2,1)} fusion(bf16[768,768]{1,0:T(8,128)(2,1)S(1)} %bitcast.35, bf16[768,2048]{1,0:T(8,128)(2,1)} %all-gather.4.cloned.1.call-done), kind=kOutput, calls=%fused_computation.1 | convolution fusion | flops 2419064832 | bytes 7471104 | tf_op jit(solution)/shard_map/dot_general | solution.py:91
  132.4 0.0 all-to-all-done.2
  132.4 9.1 %all-to-all-start.1 = ((bf16[32,24,2048]{2,1,0:T(8,128)(2,1)}), bf16[32,24,2048]{2,1,0:T(8,128)(2,1)}, u32[]{:S(2)}, u32[]{:S(2)}) async-start(bf16[32,24,2048]{2,1,0:T(8,128)(2,1)} %bitcast.33), calls=%async_computation.1 | async-start | bytes 6291456 | tf_op jit(solution)/shard_map/all_to_all | solution.py:96
  141.5 0.0 all-gather.6.cloned.1.call-start
  141.5 0.7 all-gather.6.cloned.1.call-update
  142.2 47.7 %all-gather.6.cloned.1.call-done = bf16[768,2048]{1,0:T(8,128)(2,1)} async-done(((bf16[192,2048]{1,0:T(8,128)(2,1)}), bf16[768,2048]{1,0:T(8,128)(2,1)}) %all-gather.6.cloned.1.call-update) | async-done | bytes 3145744 | tf_op jit(solution)/shard_map/all_gather | solution.py:87
  190.0 6.6 %multiply_convert_fusion = bf16[768,2048]{1,0:T(8,128)(2,1)} fusion(bf16[768,768]{1,0:T(8,128)(2,1)} %bitcast.8, bf16[768,2048]{1,0:T(8,128)(2,1)} %all-gather.6.cloned.1.call-done), kind=kOutput, calls=%fused_computation | convolution fusion | flops 2419064832 | bytes 7471104 | tf_op jit(solution)/shard_map/dot_general | solution.py:91
  196.5 26.8 %all-to-all-done.1 = bf16[32,24,2048]{2,1,0:T(8,128)(2,1)} async-done(((bf16[32,24,2048]{2,1,0:T(8,128)(2,1)}), bf16[32,24,2048]{2,1,0:T(8,128)(2,1)}, u32[]{:S(2)}, u32[]{:S(2)}) %all-to-all-start.1) | async-done | bytes 3145760 | tf_op jit(solution)/shard_map/all_to_all | solution.py:96
  223.3 0.0 copy-start.4
  223.3 0.0 copy-start.5
  223.3 9.3 %all-to-all-start.3 = ((bf16[32,24,2048]{2,1,0:T(8,128)(2,1)}), bf16[32,24,2048]{2,1,0:T(8,128)(2,1)}, u32[]{:S(2)}, u32[]{:S(2)}) async-start(bf16[32,24,2048]{2,1,0:T(8,128)(2,1)} %bitcast.32), calls=%async_computation.3 | async-start | bytes 6291456 | tf_op jit(solution)/shard_map/all_to_all | solution.py:96
  232.6 5.0 %collective-permute-start = (f32[2,48,2048]{2,1,0:T(8,128)}, f32[2,48,2048]{2,1,0:T(8,128)S(1)}, u32[]{:S(2)}, u32[]{:S(2)}) collective-permute-start(f32[2,48,2048]{2,1,0:T(8,128)} %get-tuple-element.19), channel_id=1, source_target_pairs={{0,256},{128,384},{256,0},{384,128},{1,257},{129,385},{257,1},{385... | collective-permute-start | bytes 2359304 | tf_op jit(solution)/shard_map/ppermute | solution.py:56
  237.6 0.1 reduce_sum.48
  237.8 0.0 copy-done.4
  237.8 0.1 copy.24
  237.9 0.0 copy-done.5
  237.9 0.1 copy.25
  238.0 0.1 copy.26
  238.1 3.8 %fusion.3 = (bf16[128,768]{1,0:T(8,128)(2,1)S(1)}, bf16[128,768]{1,0:T(8,128)(2,1)S(1)}, bf16[128,768]{1,0:T(8,128)(2,1)S(1)}, bf16[128,768]{1,0:T(8,128)(2,1)S(1)}) fusion(s32[768]{0:T(1024)S(1)} %get-tuple-element.24, f32[128,8]{1,0:T(8,128)S(1)} %copy.25, s32[128,8]{1,0:T(8,128)S(1)} %copy.24, s32[768]{0:T(1024)S(1)} %get-tuple-element.25, ...), kind=kLoop, calls=%fused_computation.11 | loop fusion | flops 7471104 | bytes 804864 | tf_op jit(solution)/shard_map/reduce_sum | solution.py:101
  242.0 13.9 %collective-permute-done = f32[2,48,2048]{2,1,0:T(8,128)S(1)} collective-permute-done((f32[2,48,2048]{2,1,0:T(8,128)}, f32[2,48,2048]{2,1,0:T(8,128)S(1)}, u32[]{:S(2)}, u32[]{:S(2)}) %collective-permute-start) | collective-permute-done | bytes 786464 | tf_op jit(solution)/shard_map/ppermute | solution.py:56
  255.8 0.0 copy-start.1
  255.8 2.8 fusion.55
  258.6 0.0 copy-done.1
  258.6 2.5 convolution_add_fusion.2
  261.2 52.4 %all-to-all-done.3 = bf16[32,24,2048]{2,1,0:T(8,128)(2,1)} async-done(((bf16[32,24,2048]{2,1,0:T(8,128)(2,1)}), bf16[32,24,2048]{2,1,0:T(8,128)(2,1)}, u32[]{:S(2)}, u32[]{:S(2)}) %all-to-all-start.3) | async-done | bytes 3145760 | tf_op jit(solution)/shard_map/all_to_all | solution.py:96
  313.6 2.5 convolution_add_fusion.1
  316.0 0.0 copy-start.2
  316.0 3.4 %fusion.9 = bf16[128,2048]{1,0:T(8,128)(2,1)} fusion(f32[128,2048]{1,0:T(8,128)S(1)} %convolution_add_fusion.1, bf16[768,2048]{1,0:T(8,128)(2,1)} %bitcast.10, bf16[128,768]{1,0:T(8,128)(2,1)S(1)} %get-tuple-element.17), kind=kOutput, calls=%fused_computation.20 | convolution fusion | flops 403177472 | bytes 4915200 | tf_op jit(solution)/shard_map/dot_general | solution.py:102
  319.4 0.0 copy-done.2
  319.4 0.9 copy.28
  (6 shorter events, 0.1 us)
Async XLA Ops:
  7.2 1.6 copy-start
  8.7 18.1 %copy-start.3 = (f32[2,48,2048]{2,1,0:T(8,128)S(1)}, f32[2,48,2048]{2,1,0:T(8,128)}, u32[]{:S(2)}) copy-start(f32[2,48,2048]{2,1,0:T(8,128)} %param.10) | copy-start | bytes 2359300
  11.2 59.6 %all-to-all-start = ((bf16[32,24,768]{2,1,0:T(8,128)(2,1)}), bf16[32,24,768]{2,1,0:T(8,128)(2,1)S(1)}, u32[]{:S(2)}, u32[]{:S(2)}) async-start(bf16[32,24,768]{2,1,0:T(8,128)(2,1)} %bitcast.37), calls=%async_computation | async-start | bytes 2359296 | tf_op jit(solution)/shard_map/all_to_all | solution.py:73
  26.8 99.8 %all-gather.4.cloned.1.call-start = ((), (), s32[]{:S(2)}) async-start(), calls=%async_computation.4 | async-start | bytes 3932160 | tf_op jit(solution)/shard_map/all_gather | solution.py:87
  73.3 59.1 %all-to-all-start.2 = ((bf16[32,24,768]{2,1,0:T(8,128)(2,1)}), bf16[32,24,768]{2,1,0:T(8,128)(2,1)}, u32[]{:S(2)}, u32[]{:S(2)}) async-start(bf16[32,24,768]{2,1,0:T(8,128)(2,1)} %bitcast.36), calls=%async_computation.2 | async-start | bytes 2359296 | tf_op jit(solution)/shard_map/all_to_all | solution.py:73
  132.4 90.9 %all-to-all-start.1 = ((bf16[32,24,2048]{2,1,0:T(8,128)(2,1)}), bf16[32,24,2048]{2,1,0:T(8,128)(2,1)}, u32[]{:S(2)}, u32[]{:S(2)}) async-start(bf16[32,24,2048]{2,1,0:T(8,128)(2,1)} %bitcast.33), calls=%async_computation.1 | async-start | bytes 6291456 | tf_op jit(solution)/shard_map/all_to_all | solution.py:96
  141.5 48.5 %all-gather.6.cloned.1.call-start = ((), (), s32[]{:S(2)}) async-start(), calls=%async_computation.5 | async-start | bytes 3932160 | tf_op jit(solution)/shard_map/all_gather | solution.py:87
  223.3 14.5 %copy-start.4 = (s32[128,8]{0,1:T(8,128)S(1)}, s32[128,8]{0,1:T(8,128)}, u32[]{:S(2)}) copy-start(s32[128,8]{0,1:T(8,128)} %param.8) | copy-start | bytes 12292
  223.3 14.6 %copy-start.5 = (s32[128,8]{0,1:T(8,128)S(1)}, s32[128,8]{0,1:T(8,128)}, u32[]{:S(2)}) copy-start(s32[128,8]{0,1:T(8,128)} %param.9) | copy-start | bytes 12292
  223.3 90.2 %all-to-all-start.3 = ((bf16[32,24,2048]{2,1,0:T(8,128)(2,1)}), bf16[32,24,2048]{2,1,0:T(8,128)(2,1)}, u32[]{:S(2)}, u32[]{:S(2)}) async-start(bf16[32,24,2048]{2,1,0:T(8,128)(2,1)} %bitcast.32), calls=%async_computation.3 | async-start | bytes 6291456 | tf_op jit(solution)/shard_map/all_to_all | solution.py:96
  232.6 23.2 %collective-permute-start = (f32[2,48,2048]{2,1,0:T(8,128)}, f32[2,48,2048]{2,1,0:T(8,128)S(1)}, u32[]{:S(2)}, u32[]{:S(2)}) collective-permute-start(f32[2,48,2048]{2,1,0:T(8,128)} %get-tuple-element.19), channel_id=1, source_target_pairs={{0,256},{128,384},{256,0},{384,128},{1,257},{129,385},{257,1},{385... | collective-permute-start | bytes 2359304 | tf_op jit(solution)/shard_map/ppermute | solution.py:56
  255.8 2.8 copy-start.1
  316.0 3.4 %copy-start.2 = (f32[2,48,2048]{2,1,0:T(8,128)S(1)}, f32[2,48,2048]{2,1,0:T(8,128)}, u32[]{:S(2)}) copy-start(f32[2,48,2048]{2,1,0:T(8,128)} %copy-done.1) | copy-start | bytes 2359300
Sparse Core Ops, SparseCore 0:
  71.0 43.4 all-gather.3
  144.4 45.4 all-gather.5

commit v12 on v11

--- a/solution.py
+++ b/solution.py
@@ -73,13 +73,21 @@
         arrived.append(lax.all_to_all(outgoing.reshape(ranks, capacity, hidden_width), "ep",
                                       split_axis=0, concat_axis=0, tiled=True))
 
+    inner = lax.axis_size("grp_1")
+    here = lax.axis_index("grp_1")
     gathered = []
     first_stage = []
     for local in range(local_experts):
         own = weights[local]
         if first_stage:
             own, _ = lax.optimization_barrier((own, arrived[0]))
-        rows = lax.all_gather(own, "grp_1", axis=0, tiled=True)
+        if first_stage:
+            rows = lax.all_gather(own, "grp_1", axis=0, tiled=True)
+        else:
+            received = [own] + [lax.ppermute(own, "grp_1", [(s, (s + k) % inner) for s in range(inner)])
+                                for k in range(1, inner)]
+            ordered = jnp.stack([received[(-k) % inner] for k in range(inner)], axis=0)
+            rows = jnp.roll(ordered, here, axis=0).reshape(inner * own.shape[0], width)
         first_stage.append(rows)
         rows, tie = lax.optimization_barrier((rows, gathered[-1] if gathered else arrived[0]))
         if not gathered:

time: 328 us -> 330 us (level)
  blocking collectives: 84.2 us -> 43.1 us
  waiting for transfers between devices: 142 us -> 165 us
  starting transfers between devices: 49.1 us -> 59.1 us
  local copies, waits for them, and re-layouts: 2.38 us -> 11.2 us
    all_gather x2 -> x1, blocking collectives: 84.2 us -> 43.1 us  [body(): rows = lax.all_gather(own, 'grp_1', axis=0, tiled=True)]
    all_to_all x2, waiting for transfers between devices: 0.01 us -> 23.4 us  [body(): lax.all_to_all(outgoing.reshape(ranks, capacity, hidden_width), 'ep', spl...]
    ppermute x0 -> x3, starting transfers between devices: none -> 12.3 us  [body(): lax.ppermute(own, 'grp_1', [(s, (s + k) % inner) for s in range(inner)])]
    all_to_all x2, starting transfers between devices: 25.7 us -> 21.1 us  [body(): lax.all_to_all(outgoing.reshape(ranks, capacity, hidden_width), 'ep', spl...]
    unnamed x14 -> x23, local copies, waits for them, and re-layouts: 1.82 us -> 5.39 us
  transfers between devices with their start and end apart: 7 -> 10, of which waited for: 4 -> 5; matrix products, arithmetic and copies ran while one was open for 8% -> 11% of each run, Pallas kernels for 0% -> 0%
where the time goes in v12:
time: 330 us; the launch traced here: 329 us
  waiting for transfers between devices  165 us (50%)
  starting transfers between devices  59.1 us (18%)
  blocking collectives  43.1 us (13%)
  matrix products  28.5 us (9%)
  between operations  14.3 us (4%)
  local copies, waits for them, and re-layouts  11.2 us (3%)
  other arithmetic  7.53 us (2%)
    all_to_all x2, waiting for transfers between devices, body(): lax.all_to_all(results.reshape(ranks, capacity, width), 'ep', split_axis=...  79.4 us
    all_gather x2, waiting for transfers between devices, body(): gathered.append(lax.all_gather(rows, 'grp_0', axis=0, tiled=True))  47.5 us
    all_gather x1, blocking collectives, body(): rows = lax.all_gather(own, 'grp_1', axis=0, tiled=True)  43.1 us
    all_to_all x2, waiting for transfers between devices, body(): lax.all_to_all(outgoing.reshape(ranks, capacity, hidden_width), 'ep', spl...  23.4 us
    all_to_all x2, starting transfers between devices, body(): lax.all_to_all(outgoing.reshape(ranks, capacity, hidden_width), 'ep', spl...  21.1 us
    all_to_all x2, starting transfers between devices, body(): lax.all_to_all(results.reshape(ranks, capacity, width), 'ep', split_axis=...  20.8 us
    ppermute x1, waiting for transfers between devices, body(): lax.ppermute(step_dir, 'grp_0', [(s, (s + shift) % outer) for s in range(...  14.1 us
    dot_general x2, matrix products, body(): jnp.dot(arrived[local].reshape(chunk, hidden_width), gathered[local], pre...  12.4 us
  transfers between devices with their start and end apart: 10, of which 5 were waited for; matrix products, arithmetic and copies ran while one was open for 11% of the time, Pallas kernels for 0%

profile of v12, /device:TPU:56, one launch (start us, length us, event | category | flops | bytes accessed | tf_op | source)
XLA Modules:
  0.0 328.9 jit_solution(2956394378448674213)
XLA Ops:
  7.2 0.0 copy-start
  7.2 3.2 subtract_convert_fusion
  10.3 0.8 slice_bitcast_fusion.1
  11.1 7.9 %collective-permute-start = (bf16[48,2048]{1,0:T(8,128)(2,1)}, bf16[48,2048]{1,0:T(8,128)(2,1)S(1)}, u32[]{:S(2)}, u32[]{:S(2)}) collective-permute-start(bf16[48,2048]{1,0:T(8,128)(2,1)} %get-tuple-element.22), channel_id=1, source_target_pairs={{0,96},{32,0},{64,32},{96,64},{1,97},{33,1},{65,33},{97,65},{2,98}... | collective-permute-start | bytes 589832 | tf_op jit(solution)/shard_map/ppermute | solution.py:87
  19.0 1.9 collective-permute-start.1
  20.9 2.5 collective-permute-start.2
  23.4 0.1 copy.22
  23.6 0.1 eq.36
  23.6 0.5 convert_reduce_fusion
  24.2 2.5 fusion.16
  26.7 13.4 %all-to-all-start = ((bf16[32,24,768]{2,1,0:T(8,128)(2,1)}), bf16[32,24,768]{2,1,0:T(8,128)(2,1)S(1)}, u32[]{:S(2)}, u32[]{:S(2)}) async-start(bf16[32,24,768]{2,1,0:T(8,128)(2,1)} %bitcast.47), calls=%async_computation | async-start | bytes 2359296 | tf_op jit(solution)/shard_map/all_to_all | solution.py:73
  40.1 0.0 all-gather.3.cloned.1.call-start
  40.1 0.7 bitcast_dynamic-update-slice_fusion.4
  40.8 0.7 bitcast_dynamic-update-slice_fusion.2
  41.5 1.6 bitcast_dynamic-update-slice_fusion
  43.1 0.8 slice_bitcast_fusion
  43.9 0.7 bitcast_dynamic-update-slice_fusion.5
  44.6 0.7 bitcast_dynamic-update-slice_fusion.3
  45.3 1.6 bitcast_dynamic-update-slice_fusion.1
  46.9 2.1 constant_dynamic-slice_fusion
  49.0 23.4 %all-to-all-done = bf16[32,24,768]{2,1,0:T(8,128)(2,1)S(1)} async-done(((bf16[32,24,768]{2,1,0:T(8,128)(2,1)}), bf16[32,24,768]{2,1,0:T(8,128)(2,1)S(1)}, u32[]{:S(2)}, u32[]{:S(2)}) %all-to-all-start) | async-done | bytes 1179680 | tf_op jit(solution)/shard_map/all_to_all | solution.py:73
  72.4 0.0 all-gather.3.cloned.1.call-update
  72.4 0.0 copy-start.3
  72.5 2.5 fusion.21
  74.9 7.8 %all-to-all-start.2 = ((bf16[32,24,768]{2,1,0:T(8,128)(2,1)}), bf16[32,24,768]{2,1,0:T(8,128)(2,1)}, u32[]{:S(2)}, u32[]{:S(2)}) async-start(bf16[32,24,768]{2,1,0:T(8,128)(2,1)} %bitcast.48), calls=%async_computation.2 | async-start | bytes 2359296 | tf_op jit(solution)/shard_map/all_to_all | solution.py:73
  82.7 43.1 %all_gather.10 = bf16[192,2048]{1,0:T(8,128)(2,1)} all-gather(bf16[48,2048]{1,0:T(8,128)(2,1)S(1)} %copy-done.3), channel_id=1, replica_groups=mesh['grp_0'=4,'grp_1'=4,'ep'=32] {'grp_1'}, dimensions={0}, use_global_device_ids=true | all-gather | bytes 983040 | tf_op jit(solution)/shard_map/all_gather | solution.py:85
  125.8 5.8 %multiply_convert_fusion.1 = bf16[768,2048]{1,0:T(8,128)(2,1)} fusion(bf16[768,768]{1,0:T(8,128)(2,1)S(1)} %bitcast.46, bf16[768,2048]{1,0:T(8,128)(2,1)} %all-gather.3.cloned.1.call-done), kind=kOutput, calls=%fused_computation.1 | convolution fusion | flops 2419064832 | bytes 7471104 | tf_op jit(solution)/shard_map/dot_general | solution.py:99
  131.6 11.5 %all-to-all-start.1 = ((bf16[32,24,2048]{2,1,0:T(8,128)(2,1)}), bf16[32,24,2048]{2,1,0:T(8,128)(2,1)}, u32[]{:S(2)}, u32[]{:S(2)}) async-start(bf16[32,24,2048]{2,1,0:T(8,128)(2,1)} %bitcast.44), calls=%async_computation.1 | async-start | bytes 6291456 | tf_op jit(solution)/shard_map/all_to_all | solution.py:104
  143.2 0.0 all-gather.5.cloned.1.call-start
  143.2 0.7 all-gather.5.cloned.1.call-update
  143.9 47.5 %all-gather.5.cloned.1.call-done = bf16[768,2048]{1,0:T(8,128)(2,1)} async-done(((bf16[192,2048]{1,0:T(8,128)(2,1)}), bf16[768,2048]{1,0:T(8,128)(2,1)}) %all-gather.5.cloned.1.call-update) | async-done | bytes 3145744 | tf_op jit(solution)/shard_map/all_gather | solution.py:95
  191.5 6.6 %multiply_convert_fusion = bf16[768,2048]{1,0:T(8,128)(2,1)} fusion(bf16[768,768]{1,0:T(8,128)(2,1)} %bitcast.12, bf16[768,2048]{1,0:T(8,128)(2,1)} %all-gather.5.cloned.1.call-done), kind=kOutput, calls=%fused_computation | convolution fusion | flops 2419064832 | bytes 7471104 | tf_op jit(solution)/shard_map/dot_general | solution.py:99
  198.0 27.0 %all-to-all-done.1 = bf16[32,24,2048]{2,1,0:T(8,128)(2,1)} async-done(((bf16[32,24,2048]{2,1,0:T(8,128)(2,1)}), bf16[32,24,2048]{2,1,0:T(8,128)(2,1)}, u32[]{:S(2)}, u32[]{:S(2)}) %all-to-all-start.1) | async-done | bytes 3145760 | tf_op jit(solution)/shard_map/all_to_all | solution.py:104
  225.0 9.3 %all-to-all-start.3 = ((bf16[32,24,2048]{2,1,0:T(8,128)(2,1)}), bf16[32,24,2048]{2,1,0:T(8,128)(2,1)}, u32[]{:S(2)}, u32[]{:S(2)}) async-start(bf16[32,24,2048]{2,1,0:T(8,128)(2,1)} %bitcast.43), calls=%async_computation.3 | async-start | bytes 6291456 | tf_op jit(solution)/shard_map/all_to_all | solution.py:104
  234.3 4.8 %collective-permute-start.3 = (f32[2,48,2048]{2,1,0:T(8,128)}, f32[2,48,2048]{2,1,0:T(8,128)S(1)}, u32[]{:S(2)}, u32[]{:S(2)}) collective-permute-start(f32[2,48,2048]{2,1,0:T(8,128)} %get-tuple-element.19), channel_id=1, source_target_pairs={{0,256},{128,384},{256,0},{384,128},{1,257},{129,385},{257,1},{385... | collective-permute-start | bytes 2359304 | tf_op jit(solution)/shard_map/ppermute | solution.py:56
  239.2 0.1 reduce_sum.48
  239.3 0.1 copy.25
  239.4 0.1 copy.24
  239.5 0.1 copy.26
  239.6 3.8 %fusion.3 = (bf16[128,768]{1,0:T(8,128)(2,1)S(1)}, bf16[128,768]{1,0:T(8,128)(2,1)S(1)}, bf16[128,768]{1,0:T(8,128)(2,1)S(1)}, bf16[128,768]{1,0:T(8,128)(2,1)S(1)}) fusion(s32[768]{0:T(1024)S(1)} %get-tuple-element.26, f32[128,8]{1,0:T(8,128)S(1)} %copy.25, s32[128,8]{1,0:T(8,128)S(1)} %copy.24, s32[768]{0:T(1024)S(1)} %get-tuple-element.27, ...), kind=kLoop, calls=%fused_computation.11 | loop fusion | flops 7471104 | bytes 804864 | tf_op jit(solution)/shard_map/reduce_sum | solution.py:109
  243.5 14.1 %collective-permute-done.3 = f32[2,48,2048]{2,1,0:T(8,128)S(1)} collective-permute-done((f32[2,48,2048]{2,1,0:T(8,128)}, f32[2,48,2048]{2,1,0:T(8,128)S(1)}, u32[]{:S(2)}, u32[]{:S(2)}) %collective-permute-start.3) | collective-permute-done | bytes 786464 | tf_op jit(solution)/shard_map/ppermute | solution.py:56
  257.5 2.8 fusion.55
  260.3 2.5 convolution_add_fusion.2
  262.9 52.4 %all-to-all-done.3 = bf16[32,24,2048]{2,1,0:T(8,128)(2,1)} async-done(((bf16[32,24,2048]{2,1,0:T(8,128)(2,1)}), bf16[32,24,2048]{2,1,0:T(8,128)(2,1)}, u32[]{:S(2)}, u32[]{:S(2)}) %all-to-all-start.3) | async-done | bytes 3145760 | tf_op jit(solution)/shard_map/all_to_all | solution.py:104
  315.3 2.5 convolution_add_fusion.1
  317.7 0.0 copy-start.2
  317.8 3.4 %fusion.9 = bf16[128,2048]{1,0:T(8,128)(2,1)} fusion(f32[128,2048]{1,0:T(8,128)S(1)} %convolution_add_fusion.1, bf16[768,2048]{1,0:T(8,128)(2,1)} %bitcast.14, bf16[128,768]{1,0:T(8,128)(2,1)S(1)} %get-tuple-element.17), kind=kOutput, calls=%fused_computation.20 | convolution fusion | flops 403177472 | bytes 4915200 | tf_op jit(solution)/shard_map/dot_general | solution.py:110
  321.1 0.9 copy.35
  (23 shorter events, 0.1 us)
Async XLA Ops:
  7.2 17.0 %copy-start = (bf16[128,8,768]{2,1,0:T(8,128)(2,1)S(1)}, bf16[128,8,768]{2,1,0:T(8,128)(2,1)}, u32[]{:S(2)}) copy-start(bf16[128,8,768]{2,1,0:T(8,128)(2,1)} %param.7) | copy-start | bytes 4718596
  7.2 16.3 %copy-start.4 = (s32[128,8]{0,1:T(8,128)S(1)}, s32[128,8]{0,1:T(8,128)}, u32[]{:S(2)}) copy-start(s32[128,8]{0,1:T(8,128)} %param.8) | copy-start | bytes 12292
  11.1 29.0 %collective-permute-start = (bf16[48,2048]{1,0:T(8,128)(2,1)}, bf16[48,2048]{1,0:T(8,128)(2,1)S(1)}, u32[]{:S(2)}, u32[]{:S(2)}) collective-permute-start(bf16[48,2048]{1,0:T(8,128)(2,1)} %get-tuple-element.22), channel_id=1, source_target_pairs={{0,96},{32,0},{64,32},{96,64},{1,97},{33,1},{65,33},{97,65},{2,98}... | collective-permute-start | bytes 589832 | tf_op jit(solution)/shard_map/ppermute | solution.py:87
  19.0 21.8 %collective-permute-start.1 = (bf16[48,2048]{1,0:T(8,128)(2,1)}, bf16[48,2048]{1,0:T(8,128)(2,1)S(1)}, u32[]{:S(2)}, u32[]{:S(2)}) collective-permute-start(bf16[48,2048]{1,0:T(8,128)(2,1)} %get-tuple-element.22), channel_id=1, source_target_pairs={{0,64},{32,96},{64,0},{96,32},{1,65},{33,97},{65,1},{97,33},{2,66}... | collective-permute-start | bytes 589832 | tf_op jit(solution)/shard_map/ppermute | solution.py:87
  20.9 20.6 %collective-permute-start.2 = (bf16[48,2048]{1,0:T(8,128)(2,1)}, bf16[48,2048]{1,0:T(8,128)(2,1)}, u32[]{:S(2)}, u32[]{:S(2)}) collective-permute-start(bf16[48,2048]{1,0:T(8,128)(2,1)} %get-tuple-element.22), channel_id=1, source_target_pairs={{0,32},{32,64},{64,96},{96,0},{1,33},{33,65},{65,97},{97,1},{2,34}... | collective-permute-start | bytes 589832 | tf_op jit(solution)/shard_map/ppermute | solution.py:87
  24.2 2.5 copy-start.6
  26.7 45.7 %all-to-all-start = ((bf16[32,24,768]{2,1,0:T(8,128)(2,1)}), bf16[32,24,768]{2,1,0:T(8,128)(2,1)S(1)}, u32[]{:S(2)}, u32[]{:S(2)}) async-start(bf16[32,24,768]{2,1,0:T(8,128)(2,1)} %bitcast.47), calls=%async_computation | async-start | bytes 2359296 | tf_op jit(solution)/shard_map/all_to_all | solution.py:73
  40.1 85.7 %all-gather.3.cloned.1.call-start = ((), (), s32[]{:S(2)}) async-start(), calls=%async_computation.4 | async-start | bytes 3932160 | tf_op jit(solution)/shard_map/all_gather | solution.py:95
  43.9 28.5 %copy-start.7 = (s32[1024]{0:T(1024)S(1)}, s32[1024]{0:T(1024)}, u32[]{:S(2)}) copy-start(s32[1024]{0:T(1024)} %copy-done.6) | copy-start | bytes 12292
  72.4 10.3 %copy-start.3 = (bf16[48,2048]{1,0:T(8,128)(2,1)S(1)}, bf16[48,2048]{1,0:T(8,128)(2,1)}, u32[]{:S(2)}) copy-start(bf16[48,2048]{1,0:T(8,128)(2,1)} %get-tuple-element.9) | copy-start | bytes 589828
  74.9 56.7 %all-to-all-start.2 = ((bf16[32,24,768]{2,1,0:T(8,128)(2,1)}), bf16[32,24,768]{2,1,0:T(8,128)(2,1)}, u32[]{:S(2)}, u32[]{:S(2)}) async-start(bf16[32,24,768]{2,1,0:T(8,128)(2,1)} %bitcast.48), calls=%async_computation.2 | async-start | bytes 2359296 | tf_op jit(solution)/shard_map/all_to_all | solution.py:73
  131.6 93.4 %all-to-all-start.1 = ((bf16[32,24,2048]{2,1,0:T(8,128)(2,1)}), bf16[32,24,2048]{2,1,0:T(8,128)(2,1)}, u32[]{:S(2)}, u32[]{:S(2)}) async-start(bf16[32,24,2048]{2,1,0:T(8,128)(2,1)} %bitcast.44), calls=%async_computation.1 | async-start | bytes 6291456 | tf_op jit(solution)/shard_map/all_to_all | solution.py:104
  143.2 48.3 %all-gather.5.cloned.1.call-start = ((), (), s32[]{:S(2)}) async-start(), calls=%async_computation.5 | async-start | bytes 3932160 | tf_op jit(solution)/shard_map/all_gather | solution.py:95
  225.0 14.2 %copy-start.5 = (s32[128,8]{0,1:T(8,128)S(1)}, s32[128,8]{0,1:T(8,128)}, u32[]{:S(2)}) copy-start(s32[128,8]{0,1:T(8,128)} %param.9) | copy-start | bytes 12292
  225.0 90.2 %all-to-all-start.3 = ((bf16[32,24,2048]{2,1,0:T(8,128)(2,1)}), bf16[32,24,2048]{2,1,0:T(8,128)(2,1)}, u32[]{:S(2)}, u32[]{:S(2)}) async-start(bf16[32,24,2048]{2,1,0:T(8,128)(2,1)} %bitcast.43), calls=%async_computation.3 | async-start | bytes 6291456 | tf_op jit(solution)/shard_map/all_to_all | solution.py:104
  234.3 23.2 %collective-permute-start.3 = (f32[2,48,2048]{2,1,0:T(8,128)}, f32[2,48,2048]{2,1,0:T(8,128)S(1)}, u32[]{:S(2)}, u32[]{:S(2)}) collective-permute-start(f32[2,48,2048]{2,1,0:T(8,128)} %get-tuple-element.19), channel_id=1, source_target_pairs={{0,256},{128,384},{256,0},{384,128},{1,257},{129,385},{257,1},{385... | collective-permute-start | bytes 2359304 | tf_op jit(solution)/shard_map/ppermute | solution.py:56
  257.5 2.8 copy-start.1
  317.7 3.4 %copy-start.2 = (f32[2,48,2048]{2,1,0:T(8,128)S(1)}, f32[2,48,2048]{2,1,0:T(8,128)}, u32[]{:S(2)}) copy-start(f32[2,48,2048]{2,1,0:T(8,128)} %copy-done.1) | copy-start | bytes 2359300
Sparse Core Ops, SparseCore 0:
  72.6 43.1 all-gather.2
  146.1 45.2 all-gather.4

commit v13 on v12

--- a/solution.py
+++ b/solution.py
@@ -89,9 +89,8 @@
             ordered = jnp.stack([received[(-k) % inner] for k in range(inner)], axis=0)
             rows = jnp.roll(ordered, here, axis=0).reshape(inner * own.shape[0], width)
         first_stage.append(rows)
-        rows, tie = lax.optimization_barrier((rows, gathered[-1] if gathered else arrived[0]))
-        if not gathered:
-            arrived[0] = tie
+        if gathered:
+            rows, _ = lax.optimization_barrier((rows, gathered[-1]))
         gathered.append(lax.all_gather(rows, "grp_0", axis=0, tiled=True))
 
     mixed = jnp.zeros((tok_count, width), jnp.float32)

time: 330 us -> 347 us (1.052)
  waiting for transfers between devices: 165 us -> 183 us
    ppermute x3, waiting for transfers between devices: 0.01 us -> 11.8 us  [body(): lax.ppermute(own, 'grp_1', [(s, (s + k) % inner) for s in range(inner)])]
    all_to_all x2, waiting for transfers between devices: 23.4 us -> 29.8 us  [body(): lax.all_to_all(outgoing.reshape(ranks, capacity, hidden_width), 'ep', spl...]
  transfers between devices with their start and end apart: 10 -> 10, of which waited for: 5 -> 7; matrix products, arithmetic and copies ran while one was open for 11% -> 8% of each run, Pallas kernels for 0% -> 0%
where the time goes in v13:
time: 347 us; the launch traced here: 346 us
  waiting for transfers between devices  183 us (53%)
  starting transfers between devices  57.7 us (17%)
  blocking collectives  43.8 us (13%)
  matrix products  28.5 us (8%)
  between operations  14.3 us (4%)
  local copies, waits for them, and re-layouts  10.3 us (3%)
  other arithmetic  7.52 us (2%)
    all_to_all x2, waiting for transfers between devices, body(): lax.all_to_all(results.reshape(ranks, capacity, width), 'ep', split_axis=...  79.7 us
    all_gather x2, waiting for transfers between devices, body(): gathered.append(lax.all_gather(rows, 'grp_0', axis=0, tiled=True))  47.7 us
    all_gather x1, blocking collectives, body(): rows = lax.all_gather(own, 'grp_1', axis=0, tiled=True)  43.8 us
    all_to_all x2, waiting for transfers between devices, body(): lax.all_to_all(outgoing.reshape(ranks, capacity, hidden_width), 'ep', spl...  29.8 us
    all_to_all x2, starting transfers between devices, body(): lax.all_to_all(outgoing.reshape(ranks, capacity, hidden_width), 'ep', spl...  20.5 us
    all_to_all x2, starting transfers between devices, body(): lax.all_to_all(results.reshape(ranks, capacity, width), 'ep', split_axis=...  19.7 us
    ppermute x1, waiting for transfers between devices, body(): lax.ppermute(step_dir, 'grp_0', [(s, (s + shift) % outer) for s in range(...  13.7 us
    dot_general x2, matrix products, body(): jnp.dot(arrived[local].reshape(chunk, hidden_width), gathered[local], pre...  12.4 us
  transfers between devices with their start and end apart: 10, of which 7 were waited for; matrix products, arithmetic and copies ran while one was open for 8% of the time, Pallas kernels for 0%

profile of v13, /device:TPU:56, one launch (start us, length us, event | category | flops | bytes accessed | tf_op | source)
XLA Modules:
  0.0 345.5 jit_solution(671909987195876483)
XLA Ops:
  7.2 0.0 all-gather.3.cloned.1.call-start
  7.2 3.1 subtract_convert_fusion
  10.4 0.7 slice_bitcast_fusion.1
  11.1 7.9 %collective-permute-start = (bf16[48,2048]{1,0:T(8,128)(2,1)S(1)}, bf16[48,2048]{1,0:T(8,128)(2,1)S(1)}, u32[]{:S(2)}, u32[]{:S(2)}) collective-permute-start(bf16[48,2048]{1,0:T(8,128)(2,1)S(1)} %get-tuple-element.18), channel_id=1, source_target_pairs={{0,96},{32,0},{64,32},{96,64},{1,97},{33,1},{65,33},{97,65},{2,98}... | collective-permute-start | bytes 589832 | tf_op jit(solution)/shard_map/ppermute | solution.py:87
  19.0 1.9 collective-permute-start.1
  20.9 2.5 collective-permute-start.2
  23.4 0.1 copy.22
  23.5 0.1 eq.36
  23.6 0.7 collective-permute-done
  24.3 0.7 bitcast_dynamic-update-slice_fusion.4
  25.0 11.1 %collective-permute-done.1 = bf16[48,2048]{1,0:T(8,128)(2,1)S(1)} collective-permute-done((bf16[48,2048]{1,0:T(8,128)(2,1)S(1)}, bf16[48,2048]{1,0:T(8,128)(2,1)S(1)}, u32[]{:S(2)}, u32[]{:S(2)}) %collective-permute-start.1) | collective-permute-done | bytes 196640 | tf_op jit(solution)/shard_map/ppermute | solution.py:87
  36.1 0.7 bitcast_dynamic-update-slice_fusion.2
  36.8 0.7 bitcast_dynamic-update-slice_fusion
  37.5 0.7 slice_bitcast_fusion
  38.2 0.7 bitcast_dynamic-update-slice_fusion.5
  38.9 0.7 bitcast_dynamic-update-slice_fusion.3
  39.6 0.7 bitcast_dynamic-update-slice_fusion.1
  40.3 2.1 constant_dynamic-slice_fusion
  42.4 0.0 all-gather.3.cloned.1.call-update
  42.4 0.5 convert_reduce_fusion
  43.0 2.5 fusion.16
  45.4 12.8 %all-to-all-start = ((bf16[32,24,768]{2,1,0:T(8,128)(2,1)}), bf16[32,24,768]{2,1,0:T(8,128)(2,1)S(1)}, u32[]{:S(2)}, u32[]{:S(2)}) async-start(bf16[32,24,768]{2,1,0:T(8,128)(2,1)} %bitcast.49), calls=%async_computation | async-start | bytes 2359296 | tf_op jit(solution)/shard_map/all_to_all | solution.py:73
  58.3 2.5 fusion.21
  60.7 29.8 %all-to-all-done = bf16[32,24,768]{2,1,0:T(8,128)(2,1)S(1)} async-done(((bf16[32,24,768]{2,1,0:T(8,128)(2,1)}), bf16[32,24,768]{2,1,0:T(8,128)(2,1)S(1)}, u32[]{:S(2)}, u32[]{:S(2)}) %all-to-all-start) | async-done | bytes 1179680 | tf_op jit(solution)/shard_map/all_to_all | solution.py:73
  90.6 1.1 copy-done.1
  91.7 7.7 %all-to-all-start.2 = ((bf16[32,24,768]{2,1,0:T(8,128)(2,1)}), bf16[32,24,768]{2,1,0:T(8,128)(2,1)S(1)}, u32[]{:S(2)}, u32[]{:S(2)}) async-start(bf16[32,24,768]{2,1,0:T(8,128)(2,1)} %bitcast.48), calls=%async_computation.2 | async-start | bytes 2359296 | tf_op jit(solution)/shard_map/all_to_all | solution.py:73
  99.4 43.8 %all_gather.10 = bf16[192,2048]{1,0:T(8,128)(2,1)} all-gather(bf16[48,2048]{1,0:T(8,128)(2,1)S(1)} %get-tuple-element.5), channel_id=1, replica_groups=mesh['grp_0'=4,'grp_1'=4,'ep'=32] {'grp_1'}, dimensions={0}, use_global_device_ids=true | all-gather | bytes 983040 | tf_op jit(solution)/shard_map/all_gather | solution.py:85
  143.2 6.5 %multiply_convert_fusion.1 = bf16[768,2048]{1,0:T(8,128)(2,1)} fusion(bf16[768,768]{1,0:T(8,128)(2,1)} %bitcast.47, bf16[768,2048]{1,0:T(8,128)(2,1)} %all-gather.3.cloned.1.call-done), kind=kOutput, calls=%fused_computation.1 | convolution fusion | flops 2419064832 | bytes 7471104 | tf_op jit(solution)/shard_map/dot_general | solution.py:98
  149.7 10.4 %all-to-all-start.1 = ((bf16[32,24,2048]{2,1,0:T(8,128)(2,1)}), bf16[32,24,2048]{2,1,0:T(8,128)(2,1)}, u32[]{:S(2)}, u32[]{:S(2)}) async-start(bf16[32,24,2048]{2,1,0:T(8,128)(2,1)} %bitcast.44), calls=%async_computation.1 | async-start | bytes 6291456 | tf_op jit(solution)/shard_map/all_to_all | solution.py:103
  160.1 0.0 all-gather.5.cloned.1.call-start
  160.1 0.7 all-gather.5.cloned.1.call-update
  160.9 47.7 %all-gather.5.cloned.1.call-done = bf16[768,2048]{1,0:T(8,128)(2,1)} async-done(((bf16[192,2048]{1,0:T(8,128)(2,1)}), bf16[768,2048]{1,0:T(8,128)(2,1)}) %all-gather.5.cloned.1.call-update) | async-done | bytes 3145744 | tf_op jit(solution)/shard_map/all_gather | solution.py:94
  208.5 5.9 %multiply_convert_fusion = bf16[768,2048]{1,0:T(8,128)(2,1)} fusion(bf16[768,768]{1,0:T(8,128)(2,1)S(1)} %bitcast.46, bf16[768,2048]{1,0:T(8,128)(2,1)} %all-gather.5.cloned.1.call-done), kind=kOutput, calls=%fused_computation | convolution fusion | flops 2419064832 | bytes 7471104 | tf_op jit(solution)/shard_map/dot_general | solution.py:98
  214.5 27.4 %all-to-all-done.1 = bf16[32,24,2048]{2,1,0:T(8,128)(2,1)} async-done(((bf16[32,24,2048]{2,1,0:T(8,128)(2,1)}), bf16[32,24,2048]{2,1,0:T(8,128)(2,1)}, u32[]{:S(2)}, u32[]{:S(2)}) %all-to-all-start.1) | async-done | bytes 3145760 | tf_op jit(solution)/shard_map/all_to_all | solution.py:103
  241.9 9.3 %all-to-all-start.3 = ((bf16[32,24,2048]{2,1,0:T(8,128)(2,1)}), bf16[32,24,2048]{2,1,0:T(8,128)(2,1)}, u32[]{:S(2)}, u32[]{:S(2)}) async-start(bf16[32,24,2048]{2,1,0:T(8,128)(2,1)} %bitcast.43), calls=%async_computation.3 | async-start | bytes 6291456 | tf_op jit(solution)/shard_map/all_to_all | solution.py:103
  251.2 5.2 %collective-permute-start.3 = (f32[2,48,2048]{2,1,0:T(8,128)}, f32[2,48,2048]{2,1,0:T(8,128)S(1)}, u32[]{:S(2)}, u32[]{:S(2)}) collective-permute-start(f32[2,48,2048]{2,1,0:T(8,128)} %get-tuple-element.15), channel_id=1, source_target_pairs={{0,256},{128,384},{256,0},{384,128},{1,257},{129,385},{257,1},{385... | collective-permute-start | bytes 2359304 | tf_op jit(solution)/shard_map/ppermute | solution.py:56
  256.3 0.1 reduce_sum.48
  256.5 0.1 copy.25
  256.6 0.1 copy.24
  256.7 0.1 copy.26
  256.8 3.8 %fusion.3 = (bf16[128,768]{1,0:T(8,128)(2,1)S(1)}, bf16[128,768]{1,0:T(8,128)(2,1)S(1)}, bf16[128,768]{1,0:T(8,128)(2,1)S(1)}, bf16[128,768]{1,0:T(8,128)(2,1)S(1)}) fusion(s32[768]{0:T(1024)S(1)} %get-tuple-element.22, f32[128,8]{1,0:T(8,128)S(1)} %copy.25, s32[128,8]{1,0:T(8,128)S(1)} %copy.24, s32[768]{0:T(1024)S(1)} %get-tuple-element.23, ...), kind=kLoop, calls=%fused_computation.11 | loop fusion | flops 7471104 | bytes 804864 | tf_op jit(solution)/shard_map/reduce_sum | solution.py:108
  260.7 13.7 %collective-permute-done.3 = f32[2,48,2048]{2,1,0:T(8,128)S(1)} collective-permute-done((f32[2,48,2048]{2,1,0:T(8,128)}, f32[2,48,2048]{2,1,0:T(8,128)S(1)}, u32[]{:S(2)}, u32[]{:S(2)}) %collective-permute-start.3) | collective-permute-done | bytes 786464 | tf_op jit(solution)/shard_map/ppermute | solution.py:56
  274.4 2.8 fusion.55
  277.2 2.5 convolution_add_fusion.2
  279.7 52.3 %all-to-all-done.3 = bf16[32,24,2048]{2,1,0:T(8,128)(2,1)} async-done(((bf16[32,24,2048]{2,1,0:T(8,128)(2,1)}), bf16[32,24,2048]{2,1,0:T(8,128)(2,1)}, u32[]{:S(2)}, u32[]{:S(2)}) %all-to-all-start.3) | async-done | bytes 3145760 | tf_op jit(solution)/shard_map/all_to_all | solution.py:103
  332.0 2.5 convolution_add_fusion.1
  334.5 3.4 fusion.9
  337.8 0.9 copy.35
  (19 shorter events, 0.1 us)
Async XLA Ops:
  7.2 35.8 %copy-start = (bf16[128,8,768]{2,1,0:T(8,128)(2,1)S(1)}, bf16[128,8,768]{2,1,0:T(8,128)(2,1)}, u32[]{:S(2)}) copy-start(bf16[128,8,768]{2,1,0:T(8,128)(2,1)} %param.7) | copy-start | bytes 4718596
  7.2 16.2 %copy-start.4 = (s32[128,8]{0,1:T(8,128)S(1)}, s32[128,8]{0,1:T(8,128)}, u32[]{:S(2)}) copy-start(s32[128,8]{0,1:T(8,128)} %param.8) | copy-start | bytes 12292
  7.2 136.0 %all-gather.3.cloned.1.call-start = ((), (), s32[]{:S(2)}) async-start(), calls=%async_computation.4 | async-start | bytes 3932160 | tf_op jit(solution)/shard_map/all_gather | solution.py:94
  11.1 13.2 %collective-permute-start = (bf16[48,2048]{1,0:T(8,128)(2,1)S(1)}, bf16[48,2048]{1,0:T(8,128)(2,1)S(1)}, u32[]{:S(2)}, u32[]{:S(2)}) collective-permute-start(bf16[48,2048]{1,0:T(8,128)(2,1)S(1)} %get-tuple-element.18), channel_id=1, source_target_pairs={{0,96},{32,0},{64,32},{96,64},{1,97},{33,1},{65,33},{97,65},{2,98}... | collective-permute-start | bytes 589832 | tf_op jit(solution)/shard_map/ppermute | solution.py:87
  19.0 17.1 %collective-permute-start.1 = (bf16[48,2048]{1,0:T(8,128)(2,1)S(1)}, bf16[48,2048]{1,0:T(8,128)(2,1)S(1)}, u32[]{:S(2)}, u32[]{:S(2)}) collective-permute-start(bf16[48,2048]{1,0:T(8,128)(2,1)S(1)} %get-tuple-element.18), channel_id=1, source_target_pairs={{0,64},{32,96},{64,0},{96,32},{1,65},{33,97},{65,1},{97,33},{2,66}... | collective-permute-start | bytes 589832 | tf_op jit(solution)/shard_map/ppermute | solution.py:87
  20.9 15.9 %collective-permute-start.2 = (bf16[48,2048]{1,0:T(8,128)(2,1)S(1)}, bf16[48,2048]{1,0:T(8,128)(2,1)S(1)}, u32[]{:S(2)}, u32[]{:S(2)}) collective-permute-start(bf16[48,2048]{1,0:T(8,128)(2,1)S(1)} %get-tuple-element.18), channel_id=1, source_target_pairs={{0,32},{32,64},{64,96},{96,0},{1,33},{33,65},{65,97},{97,1},{2,34}... | collective-permute-start | bytes 589832 | tf_op jit(solution)/shard_map/ppermute | solution.py:87
  45.4 45.1 %all-to-all-start = ((bf16[32,24,768]{2,1,0:T(8,128)(2,1)}), bf16[32,24,768]{2,1,0:T(8,128)(2,1)S(1)}, u32[]{:S(2)}, u32[]{:S(2)}) async-start(bf16[32,24,768]{2,1,0:T(8,128)(2,1)} %bitcast.49), calls=%async_computation | async-start | bytes 2359296 | tf_op jit(solution)/shard_map/all_to_all | solution.py:73
  90.6 1.1 copy-start.1
  91.7 58.0 %all-to-all-start.2 = ((bf16[32,24,768]{2,1,0:T(8,128)(2,1)}), bf16[32,24,768]{2,1,0:T(8,128)(2,1)S(1)}, u32[]{:S(2)}, u32[]{:S(2)}) async-start(bf16[32,24,768]{2,1,0:T(8,128)(2,1)} %bitcast.48), calls=%async_computation.2 | async-start | bytes 2359296 | tf_op jit(solution)/shard_map/all_to_all | solution.py:73
  149.7 92.2 %all-to-all-start.1 = ((bf16[32,24,2048]{2,1,0:T(8,128)(2,1)}), bf16[32,24,2048]{2,1,0:T(8,128)(2,1)}, u32[]{:S(2)}, u32[]{:S(2)}) async-start(bf16[32,24,2048]{2,1,0:T(8,128)(2,1)} %bitcast.44), calls=%async_computation.1 | async-start | bytes 6291456 | tf_op jit(solution)/shard_map/all_to_all | solution.py:103
  160.1 48.4 %all-gather.5.cloned.1.call-start = ((), (), s32[]{:S(2)}) async-start(), calls=%async_computation.5 | async-start | bytes 3932160 | tf_op jit(solution)/shard_map/all_gather | solution.py:94
  241.9 14.6 %copy-start.5 = (s32[128,8]{0,1:T(8,128)S(1)}, s32[128,8]{0,1:T(8,128)}, u32[]{:S(2)}) copy-start(s32[128,8]{0,1:T(8,128)} %param.9) | copy-start | bytes 12292
  241.9 90.1 %all-to-all-start.3 = ((bf16[32,24,2048]{2,1,0:T(8,128)(2,1)}), bf16[32,24,2048]{2,1,0:T(8,128)(2,1)}, u32[]{:S(2)}, u32[]{:S(2)}) async-start(bf16[32,24,2048]{2,1,0:T(8,128)(2,1)} %bitcast.43), calls=%async_computation.3 | async-start | bytes 6291456 | tf_op jit(solution)/shard_map/all_to_all | solution.py:103
  251.2 23.2 %collective-permute-start.3 = (f32[2,48,2048]{2,1,0:T(8,128)}, f32[2,48,2048]{2,1,0:T(8,128)S(1)}, u32[]{:S(2)}, u32[]{:S(2)}) collective-permute-start(f32[2,48,2048]{2,1,0:T(8,128)} %get-tuple-element.15), channel_id=1, source_target_pairs={{0,256},{128,384},{256,0},{384,128},{1,257},{129,385},{257,1},{385... | collective-permute-start | bytes 2359304 | tf_op jit(solution)/shard_map/ppermute | solution.py:56
  274.4 2.8 copy-start.2
  334.4 3.4 copy-start.3
Sparse Core Ops, SparseCore 0:
  42.5 46.1 all-gather.2
  163.0 45.4 all-gather.4

commit v14 on v12

--- a/solution.py
+++ b/solution.py
@@ -82,12 +82,12 @@
         if first_stage:
             own, _ = lax.optimization_barrier((own, arrived[0]))
         if first_stage:
-            rows = lax.all_gather(own, "grp_1", axis=0, tiled=True)
-        else:
             received = [own] + [lax.ppermute(own, "grp_1", [(s, (s + k) % inner) for s in range(inner)])
                                 for k in range(1, inner)]
             ordered = jnp.stack([received[(-k) % inner] for k in range(inner)], axis=0)
             rows = jnp.roll(ordered, here, axis=0).reshape(inner * own.shape[0], width)
+        else:
+            rows = lax.all_gather(own, "grp_1", axis=0, tiled=True)
         first_stage.append(rows)
         rows, tie = lax.optimization_barrier((rows, gathered[-1] if gathered else arrived[0]))
         if not gathered:

time: 330 us -> 335 us (1.015)
  waiting for transfers between devices: 165 us -> 178 us
  local copies, waits for them, and re-layouts: 11.2 us -> 3.51 us
    ppermute x3, waiting for transfers between devices: 0.01 us -> 36.1 us  [body(): lax.ppermute(own, 'grp_1', [(s, (s + k) % inner) for s in range(inner)])]
    all_to_all x2, waiting for transfers between devices: 23.4 us -> 0.01 us  [body(): lax.all_to_all(outgoing.reshape(ranks, capacity, hidden_width), 'ep', spl...]
    all_to_all x2, starting transfers between devices: 21.1 us -> 25.7 us  [body(): lax.all_to_all(outgoing.reshape(ranks, capacity, hidden_width), 'ep', spl...]
    ppermute x3, starting transfers between devices: 12.3 us -> 8.58 us  [body(): lax.ppermute(own, 'grp_1', [(s, (s + k) % inner) for s in range(inner)])]
    unnamed x23 -> x21, local copies, waits for them, and re-layouts: 5.39 us -> 1.92 us
  transfers between devices with their start and end apart: 10 -> 10, of which waited for: 5 -> 6; matrix products, arithmetic and copies ran while one was open for 11% -> 9% of each run, Pallas kernels for 0% -> 0%
where the time goes in v14:
time: 335 us; the launch traced here: 332 us
  waiting for transfers between devices  178 us (53%)
  starting transfers between devices  59.4 us (18%)
  blocking collectives  41.2 us (12%)
  matrix products  28.5 us (9%)
  between operations  14.3 us (4%)
  other arithmetic  7.17 us (2%)
  local copies, waits for them, and re-layouts  3.51 us (1%)
    all_to_all x2, waiting for transfers between devices, body(): lax.all_to_all(results.reshape(ranks, capacity, width), 'ep', split_axis=...  79.6 us
    all_gather x2, waiting for transfers between devices, body(): gathered.append(lax.all_gather(rows, 'grp_0', axis=0, tiled=True))  48.2 us
    all_gather x1, blocking collectives, body(): rows = lax.all_gather(own, 'grp_1', axis=0, tiled=True)  41.2 us
    ppermute x3, waiting for transfers between devices, body(): lax.ppermute(own, 'grp_1', [(s, (s + k) % inner) for s in range(inner)])  36.1 us
    all_to_all x2, starting transfers between devices, body(): lax.all_to_all(outgoing.reshape(ranks, capacity, hidden_width), 'ep', spl...  25.7 us
    all_to_all x2, starting transfers between devices, body(): lax.all_to_all(results.reshape(ranks, capacity, width), 'ep', split_axis=...  19.7 us
    ppermute x1, waiting for transfers between devices, body(): lax.ppermute(step_dir, 'grp_0', [(s, (s + shift) % outer) for s in range(...  13.5 us
    dot_general x2, matrix products, body(): jnp.dot(arrived[local].reshape(chunk, hidden_width), gathered[local], pre...  12.4 us
  transfers between devices with their start and end apart: 10, of which 6 were waited for; matrix products, arithmetic and copies ran while one was open for 9% of the time, Pallas kernels for 0%

profile of v14, /device:TPU:56, one launch (start us, length us, event | category | flops | bytes accessed | tf_op | source)
XLA Modules:
  0.0 332.3 jit_solution(10292871052462293012)
XLA Ops:
  7.2 0.0 copy-start
  7.2 0.9 copy.22
  8.1 0.1 eq.36
  8.2 0.5 convert_reduce_fusion
  8.7 0.0 copy-done
  8.7 0.0 copy-start.3
  8.7 2.5 fusion.16
  11.2 15.5 %all-to-all-start = ((bf16[32,24,768]{2,1,0:T(8,128)(2,1)}), bf16[32,24,768]{2,1,0:T(8,128)(2,1)S(1)}, u32[]{:S(2)}, u32[]{:S(2)}) async-start(bf16[32,24,768]{2,1,0:T(8,128)(2,1)} %bitcast.51), calls=%async_computation | async-start | bytes 2359296 | tf_op jit(solution)/shard_map/all_to_all | solution.py:73
  26.8 0.0 all-gather.4.cloned.1.call-start
  26.8 0.0 copy-done.3
  26.8 2.8 subtract_convert_fusion
  29.7 41.2 %all-gather = bf16[1,192,2048]{2,1,0:T(8,128)(2,1)} all-gather(bf16[1,48,2048]{2,1,0:T(8,128)(2,1)S(1)} %get-tuple-element.21), channel_id=2, replica_groups=mesh['grp_0'=4,'grp_1'=4,'ep'=32] {'grp_1'}, dimensions={1}, use_global_device_ids=true | all-gather | bytes 983040 | tf_op jit(solution)/shard_map/all_gather | solution.py:90
  70.8 0.0 all-to-all-done
  70.8 0.0 all-gather.4.cloned.1.call-update
  70.9 2.5 fusion.21
  73.3 10.1 %all-to-all-start.2 = ((bf16[32,24,768]{2,1,0:T(8,128)(2,1)}), bf16[32,24,768]{2,1,0:T(8,128)(2,1)}, u32[]{:S(2)}, u32[]{:S(2)}) async-start(bf16[32,24,768]{2,1,0:T(8,128)(2,1)} %bitcast.50), calls=%async_computation.2 | async-start | bytes 2359296 | tf_op jit(solution)/shard_map/all_to_all | solution.py:73
  83.5 3.7 %collective-permute-start = (bf16[48,2048]{1,0:T(8,128)(2,1)S(1)}, bf16[48,2048]{1,0:T(8,128)(2,1)S(1)}, u32[]{:S(2)}, u32[]{:S(2)}) collective-permute-start(bf16[48,2048]{1,0:T(8,128)(2,1)S(1)} %get-tuple-element.9), channel_id=1, source_target_pairs={{0,96},{32,0},{64,32},{96,64},{1,97},{33,1},{65,33},{97,65},{2,98}... | collective-permute-start | bytes 589832 | tf_op jit(solution)/shard_map/ppermute | solution.py:85
  87.3 1.9 collective-permute-start.1
  89.2 2.9 collective-permute-start.2
  92.1 23.9 %collective-permute-done = bf16[48,2048]{1,0:T(8,128)(2,1)S(1)} collective-permute-done((bf16[48,2048]{1,0:T(8,128)(2,1)S(1)}, bf16[48,2048]{1,0:T(8,128)(2,1)S(1)}, u32[]{:S(2)}, u32[]{:S(2)}) %collective-permute-start) | collective-permute-done | bytes 196640 | tf_op jit(solution)/shard_map/ppermute | solution.py:85
  116.1 12.2 %collective-permute-done.1 = bf16[48,2048]{1,0:T(8,128)(2,1)S(1)} collective-permute-done((bf16[48,2048]{1,0:T(8,128)(2,1)S(1)}, bf16[48,2048]{1,0:T(8,128)(2,1)S(1)}, u32[]{:S(2)}, u32[]{:S(2)}) %collective-permute-start.1) | collective-permute-done | bytes 196640 | tf_op jit(solution)/shard_map/ppermute | solution.py:85
  128.3 0.0 collective-permute-done.2
  128.4 1.0 constant_dynamic-slice_fusion
  129.4 5.8 %multiply_convert_fusion.1 = bf16[768,2048]{1,0:T(8,128)(2,1)} fusion(bf16[768,768]{1,0:T(8,128)(2,1)S(1)} %bitcast.49, bf16[768,2048]{1,0:T(8,128)(2,1)} %all-gather.4.cloned.1.call-done), kind=kOutput, calls=%fused_computation.1 | convolution fusion | flops 2419064832 | bytes 7471104 | tf_op jit(solution)/shard_map/dot_general | solution.py:99
  135.2 0.0 all-to-all-done.2
  135.2 10.4 %all-to-all-start.1 = ((bf16[32,24,2048]{2,1,0:T(8,128)(2,1)}), bf16[32,24,2048]{2,1,0:T(8,128)(2,1)}, u32[]{:S(2)}, u32[]{:S(2)}) async-start(bf16[32,24,2048]{2,1,0:T(8,128)(2,1)} %bitcast.46), calls=%async_computation.1 | async-start | bytes 6291456 | tf_op jit(solution)/shard_map/all_to_all | solution.py:104
  145.7 0.0 all-gather.6.cloned.1.call-start
  145.7 0.7 all-gather.6.cloned.1.call-update
  146.4 48.2 %all-gather.6.cloned.1.call-done = bf16[768,2048]{1,0:T(8,128)(2,1)} async-done(((bf16[192,2048]{1,0:T(8,128)(2,1)}), bf16[768,2048]{1,0:T(8,128)(2,1)}) %all-gather.6.cloned.1.call-update) | async-done | bytes 3145744 | tf_op jit(solution)/shard_map/all_gather | solution.py:95
  194.6 6.6 %multiply_convert_fusion = bf16[768,2048]{1,0:T(8,128)(2,1)} fusion(bf16[768,768]{1,0:T(8,128)(2,1)} %bitcast.13, bf16[768,2048]{1,0:T(8,128)(2,1)} %all-gather.6.cloned.1.call-done), kind=kOutput, calls=%fused_computation | convolution fusion | flops 2419064832 | bytes 7471104 | tf_op jit(solution)/shard_map/dot_general | solution.py:99
  201.2 25.7 %all-to-all-done.1 = bf16[32,24,2048]{2,1,0:T(8,128)(2,1)} async-done(((bf16[32,24,2048]{2,1,0:T(8,128)(2,1)}), bf16[32,24,2048]{2,1,0:T(8,128)(2,1)}, u32[]{:S(2)}, u32[]{:S(2)}) %all-to-all-start.1) | async-done | bytes 3145760 | tf_op jit(solution)/shard_map/all_to_all | solution.py:104
  226.9 9.3 %all-to-all-start.3 = ((bf16[32,24,2048]{2,1,0:T(8,128)(2,1)}), bf16[32,24,2048]{2,1,0:T(8,128)(2,1)}, u32[]{:S(2)}, u32[]{:S(2)}) async-start(bf16[32,24,2048]{2,1,0:T(8,128)(2,1)} %bitcast.45), calls=%async_computation.3 | async-start | bytes 6291456 | tf_op jit(solution)/shard_map/all_to_all | solution.py:104
  236.2 5.4 %collective-permute-start.3 = (f32[2,48,2048]{2,1,0:T(8,128)}, f32[2,48,2048]{2,1,0:T(8,128)S(1)}, u32[]{:S(2)}, u32[]{:S(2)}) collective-permute-start(f32[2,48,2048]{2,1,0:T(8,128)} %get-tuple-element.19), channel_id=1, source_target_pairs={{0,256},{128,384},{256,0},{384,128},{1,257},{129,385},{257,1},{385... | collective-permute-start | bytes 2359304 | tf_op jit(solution)/shard_map/ppermute | solution.py:56
  241.6 0.1 reduce_sum.48
  241.7 0.0 copy-done.5
  241.7 0.1 copy.25
  241.8 0.0 copy-done.4
  241.8 0.1 copy.24
  242.0 0.1 copy.26
  242.1 3.8 %fusion.3 = (bf16[128,768]{1,0:T(8,128)(2,1)S(1)}, bf16[128,768]{1,0:T(8,128)(2,1)S(1)}, bf16[128,768]{1,0:T(8,128)(2,1)S(1)}, bf16[128,768]{1,0:T(8,128)(2,1)S(1)}) fusion(s32[768]{0:T(1024)S(1)} %get-tuple-element.24, f32[128,8]{1,0:T(8,128)S(1)} %copy.25, s32[128,8]{1,0:T(8,128)S(1)} %copy.24, s32[768]{0:T(1024)S(1)} %get-tuple-element.25, ...), kind=kLoop, calls=%fused_computation.11 | loop fusion | flops 7471104 | bytes 804864 | tf_op jit(solution)/shard_map/reduce_sum | solution.py:109
  245.9 13.5 %collective-permute-done.3 = f32[2,48,2048]{2,1,0:T(8,128)S(1)} collective-permute-done((f32[2,48,2048]{2,1,0:T(8,128)}, f32[2,48,2048]{2,1,0:T(8,128)S(1)}, u32[]{:S(2)}, u32[]{:S(2)}) %collective-permute-start.3) | collective-permute-done | bytes 786464 | tf_op jit(solution)/shard_map/ppermute | solution.py:56
  259.4 2.8 fusion.55
  262.2 2.5 convolution_add_fusion.2
  264.8 53.9 %all-to-all-done.3 = bf16[32,24,2048]{2,1,0:T(8,128)(2,1)} async-done(((bf16[32,24,2048]{2,1,0:T(8,128)(2,1)}), bf16[32,24,2048]{2,1,0:T(8,128)(2,1)}, u32[]{:S(2)}, u32[]{:S(2)}) %all-to-all-start.3) | async-done | bytes 3145760 | tf_op jit(solution)/shard_map/all_to_all | solution.py:104
  318.7 2.5 convolution_add_fusion.1
  321.2 0.0 copy-start.2
  321.2 3.4 %fusion.9 = bf16[128,2048]{1,0:T(8,128)(2,1)} fusion(f32[128,2048]{1,0:T(8,128)S(1)} %convolution_add_fusion.1, bf16[768,2048]{1,0:T(8,128)(2,1)} %bitcast.15, bf16[128,768]{1,0:T(8,128)(2,1)S(1)} %get-tuple-element.17), kind=kOutput, calls=%fused_computation.20 | convolution fusion | flops 403177472 | bytes 4915200 | tf_op jit(solution)/shard_map/dot_general | solution.py:110
  324.6 0.9 copy.35
  (20 shorter events, 0.2 us)
Async XLA Ops:
  7.2 1.6 copy-start
  8.7 18.1 %copy-start.3 = (f32[2,48,2048]{2,1,0:T(8,128)S(1)}, f32[2,48,2048]{2,1,0:T(8,128)}, u32[]{:S(2)}) copy-start(f32[2,48,2048]{2,1,0:T(8,128)} %param.10) | copy-start | bytes 2359300
  11.2 59.6 %all-to-all-start = ((bf16[32,24,768]{2,1,0:T(8,128)(2,1)}), bf16[32,24,768]{2,1,0:T(8,128)(2,1)S(1)}, u32[]{:S(2)}, u32[]{:S(2)}) async-start(bf16[32,24,768]{2,1,0:T(8,128)(2,1)} %bitcast.51), calls=%async_computation | async-start | bytes 2359296 | tf_op jit(solution)/shard_map/all_to_all | solution.py:73
  26.8 102.6 %all-gather.4.cloned.1.call-start = ((), (), s32[]{:S(2)}) async-start(), calls=%async_computation.4 | async-start | bytes 3932160 | tf_op jit(solution)/shard_map/all_gather | solution.py:95
  73.3 61.9 %all-to-all-start.2 = ((bf16[32,24,768]{2,1,0:T(8,128)(2,1)}), bf16[32,24,768]{2,1,0:T(8,128)(2,1)}, u32[]{:S(2)}, u32[]{:S(2)}) async-start(bf16[32,24,768]{2,1,0:T(8,128)(2,1)} %bitcast.50), calls=%async_computation.2 | async-start | bytes 2359296 | tf_op jit(solution)/shard_map/all_to_all | solution.py:73
  83.5 32.5 %collective-permute-start = (bf16[48,2048]{1,0:T(8,128)(2,1)S(1)}, bf16[48,2048]{1,0:T(8,128)(2,1)S(1)}, u32[]{:S(2)}, u32[]{:S(2)}) collective-permute-start(bf16[48,2048]{1,0:T(8,128)(2,1)S(1)} %get-tuple-element.9), channel_id=1, source_target_pairs={{0,96},{32,0},{64,32},{96,64},{1,97},{33,1},{65,33},{97,65},{2,98}... | collective-permute-start | bytes 589832 | tf_op jit(solution)/shard_map/ppermute | solution.py:85
  87.3 40.9 %collective-permute-start.1 = (bf16[48,2048]{1,0:T(8,128)(2,1)S(1)}, bf16[48,2048]{1,0:T(8,128)(2,1)S(1)}, u32[]{:S(2)}, u32[]{:S(2)}) collective-permute-start(bf16[48,2048]{1,0:T(8,128)(2,1)S(1)} %get-tuple-element.9), channel_id=1, source_target_pairs={{0,64},{32,96},{64,0},{96,32},{1,65},{33,97},{65,1},{97,33},{2,66}... | collective-permute-start | bytes 589832 | tf_op jit(solution)/shard_map/ppermute | solution.py:85
  89.2 39.0 %collective-permute-start.2 = (bf16[48,2048]{1,0:T(8,128)(2,1)S(1)}, bf16[48,2048]{1,0:T(8,128)(2,1)S(1)}, u32[]{:S(2)}, u32[]{:S(2)}) collective-permute-start(bf16[48,2048]{1,0:T(8,128)(2,1)S(1)} %get-tuple-element.9), channel_id=1, source_target_pairs={{0,32},{32,64},{64,96},{96,0},{1,33},{33,65},{65,97},{97,1},{2,34}... | collective-permute-start | bytes 589832 | tf_op jit(solution)/shard_map/ppermute | solution.py:85
  135.2 91.7 %all-to-all-start.1 = ((bf16[32,24,2048]{2,1,0:T(8,128)(2,1)}), bf16[32,24,2048]{2,1,0:T(8,128)(2,1)}, u32[]{:S(2)}, u32[]{:S(2)}) async-start(bf16[32,24,2048]{2,1,0:T(8,128)(2,1)} %bitcast.46), calls=%async_computation.1 | async-start | bytes 6291456 | tf_op jit(solution)/shard_map/all_to_all | solution.py:104
  145.7 48.9 %all-gather.6.cloned.1.call-start = ((), (), s32[]{:S(2)}) async-start(), calls=%async_computation.5 | async-start | bytes 3932160 | tf_op jit(solution)/shard_map/all_gather | solution.py:95
  226.9 14.8 %copy-start.5 = (s32[128,8]{0,1:T(8,128)S(1)}, s32[128,8]{0,1:T(8,128)}, u32[]{:S(2)}) copy-start(s32[128,8]{0,1:T(8,128)} %param.9) | copy-start | bytes 12292
  226.9 14.9 %copy-start.4 = (s32[128,8]{0,1:T(8,128)S(1)}, s32[128,8]{0,1:T(8,128)}, u32[]{:S(2)}) copy-start(s32[128,8]{0,1:T(8,128)} %param.8) | copy-start | bytes 12292
  226.9 91.8 %all-to-all-start.3 = ((bf16[32,24,2048]{2,1,0:T(8,128)(2,1)}), bf16[32,24,2048]{2,1,0:T(8,128)(2,1)}, u32[]{:S(2)}, u32[]{:S(2)}) async-start(bf16[32,24,2048]{2,1,0:T(8,128)(2,1)} %bitcast.45), calls=%async_computation.3 | async-start | bytes 6291456 | tf_op jit(solution)/shard_map/all_to_all | solution.py:104
  236.2 23.2 %collective-permute-start.3 = (f32[2,48,2048]{2,1,0:T(8,128)}, f32[2,48,2048]{2,1,0:T(8,128)S(1)}, u32[]{:S(2)}, u32[]{:S(2)}) collective-permute-start(f32[2,48,2048]{2,1,0:T(8,128)} %get-tuple-element.19), channel_id=1, source_target_pairs={{0,256},{128,384},{256,0},{384,128},{1,257},{129,385},{257,1},{385... | collective-permute-start | bytes 2359304 | tf_op jit(solution)/shard_map/ppermute | solution.py:56
  259.4 2.8 copy-start.1
  321.2 3.4 %copy-start.2 = (f32[2,48,2048]{2,1,0:T(8,128)S(1)}, f32[2,48,2048]{2,1,0:T(8,128)}, u32[]{:S(2)}) copy-start(f32[2,48,2048]{2,1,0:T(8,128)} %copy-done.1) | copy-start | bytes 2359300
Sparse Core Ops, SparseCore 0:
  71.0 43.4 all-gather.3
  148.6 45.9 all-gather.5

commit v15 on v11

--- a/solution.py
+++ b/solution.py
@@ -97,9 +97,10 @@
                                   split_axis=0, concat_axis=0, tiled=True)
         returned = returned.reshape(chunk, width)
         hit = token_pos[:, :, None] == slot_of[local][None, None, :]
-        for part in (high, low):
-            weight = jnp.sum(jnp.where(hit, part[:, :, None], 0.0), axis=1).astype(jnp.bfloat16)
-            mixed = mixed + jnp.dot(weight, returned, preferred_element_type=jnp.float32)
+        weight = jnp.concatenate(
+            [jnp.sum(jnp.where(hit, part[:, :, None], 0.0), axis=1) for part in (high, low)], axis=0)
+        both = jnp.dot(weight.astype(jnp.bfloat16), returned, preferred_element_type=jnp.float32)
+        mixed = mixed + both[:tok_count] + both[tok_count:]
     return (mixed.astype(jnp.bfloat16), backup)
 
 

time: 328 us -> 327 us (level)
  matrix products: 28.5 us -> 24.7 us
    dot_general x4 -> x2, matrix products: 11.1 us -> 7.24 us  [body(): jnp.dot(weight.astype(jnp.bfloat16), returned, preferred_element_type=jnp...]
  transfers between devices with their start and end apart: 7 -> 7, of which waited for: 4 -> 4; matrix products, arithmetic and copies ran while one was open for 8% -> 9% of each run, Pallas kernels for 0% -> 0%
where the time goes in v15:
time: 327 us; the launch traced here: 325 us
  waiting for transfers between devices  139 us (43%)
  blocking collectives  84.3 us (26%)
  starting transfers between devices  49.1 us (15%)
  matrix products  24.7 us (8%)
  between operations  14.2 us (4%)
  other arithmetic  9.01 us (3%)
  local copies, waits for them, and re-layouts  4.26 us (1%)
    all_gather x2, blocking collectives, body(): rows = lax.all_gather(own, 'grp_1', axis=0, tiled=True)  84.3 us
    all_to_all x2, waiting for transfers between devices, body(): lax.all_to_all(results.reshape(ranks, capacity, width), 'ep', split_axis=...  80 us
    all_gather x2, waiting for transfers between devices, body(): gathered.append(lax.all_gather(rows, 'grp_0', axis=0, tiled=True))  47.7 us
    all_to_all x2, starting transfers between devices, body(): lax.all_to_all(outgoing.reshape(ranks, capacity, hidden_width), 'ep', spl...  25.7 us
    all_to_all x2, starting transfers between devices, body(): lax.all_to_all(results.reshape(ranks, capacity, width), 'ep', split_axis=...  18.3 us
    dot_general x2, matrix products, body(): jnp.dot(arrived[local].reshape(chunk, hidden_width), gathered[local], pre...  12.5 us
    ppermute x1, waiting for transfers between devices, body(): lax.ppermute(step_dir, 'grp_0', [(s, (s + shift) % outer) for s in range(...  11 us
    dot_general x2, matrix products, body(): jnp.dot(weight.astype(jnp.bfloat16), returned, preferred_element_type=jnp...  7.24 us
  transfers between devices with their start and end apart: 7, of which 4 were waited for; matrix products, arithmetic and copies ran while one was open for 9% of the time, Pallas kernels for 0%

profile of v15, /device:TPU:56, one launch (start us, length us, event | category | flops | bytes accessed | tf_op | source)
XLA Modules:
  0.0 324.9 jit_solution(854978757086746772)
XLA Ops:
  7.2 0.0 copy-start
  7.2 0.9 copy.22
  8.1 0.1 eq.33
  8.2 0.5 convert_reduce_fusion
  8.7 0.0 copy-done
  8.7 0.0 copy-start.2
  8.7 2.5 fusion.15
  11.2 15.5 %all-to-all-start = ((bf16[32,24,768]{2,1,0:T(8,128)(2,1)}), bf16[32,24,768]{2,1,0:T(8,128)(2,1)S(1)}, u32[]{:S(2)}, u32[]{:S(2)}) async-start(bf16[32,24,768]{2,1,0:T(8,128)(2,1)} %bitcast.31), calls=%async_computation | async-start | bytes 2359296 | tf_op jit(solution)/shard_map/all_to_all | solution.py:73
  26.8 0.0 all-gather.4.cloned.1.call-start
  26.8 0.0 copy-done.2
  26.8 2.8 subtract_convert_fusion
  29.7 41.2 %all-gather = bf16[1,192,2048]{2,1,0:T(8,128)(2,1)} all-gather(bf16[1,48,2048]{2,1,0:T(8,128)(2,1)S(1)} %get-tuple-element.20), channel_id=2, replica_groups=mesh['grp_0'=4,'grp_1'=4,'ep'=32] {'grp_1'}, dimensions={1}, use_global_device_ids=true | all-gather | bytes 983040 | tf_op jit(solution)/shard_map/all_gather | solution.py:82
  70.8 0.0 all-to-all-done
  70.8 0.0 all-gather.4.cloned.1.call-update
  70.8 2.5 fusion.20
  73.3 10.1 %all-to-all-start.2 = ((bf16[32,24,768]{2,1,0:T(8,128)(2,1)}), bf16[32,24,768]{2,1,0:T(8,128)(2,1)}, u32[]{:S(2)}, u32[]{:S(2)}) async-start(bf16[32,24,768]{2,1,0:T(8,128)(2,1)} %bitcast.30), calls=%async_computation.2 | async-start | bytes 2359296 | tf_op jit(solution)/shard_map/all_to_all | solution.py:73
  83.5 43.1 %all_gather.14 = bf16[192,2048]{1,0:T(8,128)(2,1)} all-gather(bf16[48,2048]{1,0:T(8,128)(2,1)S(1)} %get-tuple-element.9), channel_id=1, replica_groups=mesh['grp_0'=4,'grp_1'=4,'ep'=32] {'grp_1'}, dimensions={0}, use_global_device_ids=true | all-gather | bytes 983040 | tf_op jit(solution)/shard_map/all_gather | solution.py:82
  126.6 0.0 all-gather.4.cloned.1.call-done
  126.6 5.9 %multiply_convert_fusion.1 = bf16[768,2048]{1,0:T(8,128)(2,1)} fusion(bf16[768,768]{1,0:T(8,128)(2,1)S(1)} %bitcast.29, bf16[768,2048]{1,0:T(8,128)(2,1)} %all-gather.4.cloned.1.call-done), kind=kOutput, calls=%fused_computation.1 | convolution fusion | flops 2419064832 | bytes 7471104 | tf_op jit(solution)/shard_map/dot_general | solution.py:91
  132.5 0.0 all-to-all-done.2
  132.5 9.0 %all-to-all-start.1 = ((bf16[32,24,2048]{2,1,0:T(8,128)(2,1)}), bf16[32,24,2048]{2,1,0:T(8,128)(2,1)}, u32[]{:S(2)}, u32[]{:S(2)}) async-start(bf16[32,24,2048]{2,1,0:T(8,128)(2,1)} %bitcast.27), calls=%async_computation.1 | async-start | bytes 6291456 | tf_op jit(solution)/shard_map/all_to_all | solution.py:96
  141.6 0.0 all-gather.6.cloned.1.call-start
  141.6 0.7 all-gather.6.cloned.1.call-update
  142.3 47.7 %all-gather.6.cloned.1.call-done = bf16[768,2048]{1,0:T(8,128)(2,1)} async-done(((bf16[192,2048]{1,0:T(8,128)(2,1)}), bf16[768,2048]{1,0:T(8,128)(2,1)}) %all-gather.6.cloned.1.call-update) | async-done | bytes 3145744 | tf_op jit(solution)/shard_map/all_gather | solution.py:87
  190.0 6.5 %multiply_convert_fusion = bf16[768,2048]{1,0:T(8,128)(2,1)} fusion(bf16[768,768]{1,0:T(8,128)(2,1)} %bitcast.8, bf16[768,2048]{1,0:T(8,128)(2,1)} %all-gather.6.cloned.1.call-done), kind=kOutput, calls=%fused_computation | convolution fusion | flops 2419064832 | bytes 7471104 | tf_op jit(solution)/shard_map/dot_general | solution.py:91
  196.6 26.7 %all-to-all-done.1 = bf16[32,24,2048]{2,1,0:T(8,128)(2,1)} async-done(((bf16[32,24,2048]{2,1,0:T(8,128)(2,1)}), bf16[32,24,2048]{2,1,0:T(8,128)(2,1)}, u32[]{:S(2)}, u32[]{:S(2)}) %all-to-all-start.1) | async-done | bytes 3145760 | tf_op jit(solution)/shard_map/all_to_all | solution.py:96
  223.3 0.0 copy-start.3
  223.3 0.0 copy-start.4
  223.3 0.0 copy-start.5
  223.3 9.3 %all-to-all-start.3 = ((bf16[32,24,2048]{2,1,0:T(8,128)(2,1)}), bf16[32,24,2048]{2,1,0:T(8,128)(2,1)}, u32[]{:S(2)}, u32[]{:S(2)}) async-start(bf16[32,24,2048]{2,1,0:T(8,128)(2,1)} %bitcast.26), calls=%async_computation.3 | async-start | bytes 6291456 | tf_op jit(solution)/shard_map/all_to_all | solution.py:96
  232.6 0.0 copy-done.3
  232.6 5.0 %collective-permute-start = (f32[2,48,2048]{2,1,0:T(8,128)S(1)}, f32[2,48,2048]{2,1,0:T(8,128)S(1)}, u32[]{:S(2)}, u32[]{:S(2)}) collective-permute-start(f32[2,48,2048]{2,1,0:T(8,128)S(1)} %copy-done.3), channel_id=1, source_target_pairs={{0,256},{128,384},{256,0},{384,128},{1,257},{129,385},{257,1},{385... | collective-permute-start | bytes 2359304 | tf_op jit(solution)/shard_map/ppermute | solution.py:56
  237.6 0.1 reduce_sum.48
  237.8 0.0 copy-done.4
  237.8 0.8 copy.24
  238.5 0.0 copy-done.5
  238.6 0.7 copy.25
  239.3 0.7 copy.26
  240.0 4.6 %fusion.2 = (bf16[128,768]{1,0:T(8,128)(2,1)S(1)}, bf16[128,768]{1,0:T(8,128)(2,1)S(1)}, bf16[128,768]{1,0:T(8,128)(2,1)S(1)}, bf16[128,768]{1,0:T(8,128)(2,1)S(1)}) fusion(f32[128,8]{1,0:T(8,128)} %copy.26, s32[768]{0:T(1024)S(1)} %get-tuple-element.25, s32[128,8]{1,0:T(8,128)} %copy.24, s32[768]{0:T(1024)S(1)} %get-tuple-element.24, f32[128,8]{1,0:T(8,128)} %copy.25), kind=kLoop, calls=%fused_computation.10 | loop fusion | flops 7471104 | bytes 804864 | tf_op jit(solution)/shard_map/reduce_sum | solution.py:101
  244.6 11.0 %collective-permute-done = f32[2,48,2048]{2,1,0:T(8,128)S(1)} collective-permute-done((f32[2,48,2048]{2,1,0:T(8,128)S(1)}, f32[2,48,2048]{2,1,0:T(8,128)S(1)}, u32[]{:S(2)}, u32[]{:S(2)}) %collective-permute-start) | collective-permute-done | bytes 786464 | tf_op jit(solution)/shard_map/ppermute | solution.py:56
  255.6 4.2 %fusion.34 = f32[256,2048]{1,0:T(8,128)} fusion(bf16[768,2048]{1,0:T(8,128)(2,1)} %bitcast.6, bf16[128,768]{1,0:T(8,128)(2,1)S(1)} %get-tuple-element.14, bf16[128,768]{1,0:T(8,128)(2,1)S(1)} %get-tuple-element.17), kind=kOutput, calls=%fused_computation.40 | convolution fusion | flops 806092800 | bytes 5636096 | tf_op jit(solution)/shard_map/dot_general | solution.py:102
  259.9 53.3 %all-to-all-done.3 = bf16[32,24,2048]{2,1,0:T(8,128)(2,1)} async-done(((bf16[32,24,2048]{2,1,0:T(8,128)(2,1)}), bf16[32,24,2048]{2,1,0:T(8,128)(2,1)}, u32[]{:S(2)}, u32[]{:S(2)}) %all-to-all-start.3) | async-done | bytes 3145760 | tf_op jit(solution)/shard_map/all_to_all | solution.py:96
  313.1 0.0 copy-start.1
  313.1 3.0 fusion.38
  316.2 0.0 copy-done.1
  316.2 1.0 fusion.25
  317.2 0.9 copy.28
  (6 shorter events, 0.1 us)
Async XLA Ops:
  7.2 1.6 copy-start
  8.7 18.1 %copy-start.2 = (f32[2,48,2048]{2,1,0:T(8,128)S(1)}, f32[2,48,2048]{2,1,0:T(8,128)}, u32[]{:S(2)}) copy-start(f32[2,48,2048]{2,1,0:T(8,128)} %param.10) | copy-start | bytes 2359300
  11.2 59.6 %all-to-all-start = ((bf16[32,24,768]{2,1,0:T(8,128)(2,1)}), bf16[32,24,768]{2,1,0:T(8,128)(2,1)S(1)}, u32[]{:S(2)}, u32[]{:S(2)}) async-start(bf16[32,24,768]{2,1,0:T(8,128)(2,1)} %bitcast.31), calls=%async_computation | async-start | bytes 2359296 | tf_op jit(solution)/shard_map/all_to_all | solution.py:73
  26.8 99.8 %all-gather.4.cloned.1.call-start = ((), (), s32[]{:S(2)}) async-start(), calls=%async_computation.4 | async-start | bytes 3932160 | tf_op jit(solution)/shard_map/all_gather | solution.py:87
  73.3 59.2 %all-to-all-start.2 = ((bf16[32,24,768]{2,1,0:T(8,128)(2,1)}), bf16[32,24,768]{2,1,0:T(8,128)(2,1)}, u32[]{:S(2)}, u32[]{:S(2)}) async-start(bf16[32,24,768]{2,1,0:T(8,128)(2,1)} %bitcast.30), calls=%async_computation.2 | async-start | bytes 2359296 | tf_op jit(solution)/shard_map/all_to_all | solution.py:73
  132.5 90.8 %all-to-all-start.1 = ((bf16[32,24,2048]{2,1,0:T(8,128)(2,1)}), bf16[32,24,2048]{2,1,0:T(8,128)(2,1)}, u32[]{:S(2)}, u32[]{:S(2)}) async-start(bf16[32,24,2048]{2,1,0:T(8,128)(2,1)} %bitcast.27), calls=%async_computation.1 | async-start | bytes 6291456 | tf_op jit(solution)/shard_map/all_to_all | solution.py:96
  141.6 48.5 %all-gather.6.cloned.1.call-start = ((), (), s32[]{:S(2)}) async-start(), calls=%async_computation.5 | async-start | bytes 3932160 | tf_op jit(solution)/shard_map/all_gather | solution.py:87
  223.3 9.3 %copy-start.3 = (f32[2,48,2048]{2,1,0:T(8,128)S(1)}, f32[2,48,2048]{2,1,0:T(8,128)}, u32[]{:S(2)}) copy-start(f32[2,48,2048]{2,1,0:T(8,128)} %get-tuple-element.19) | copy-start | bytes 2359300
  223.3 14.5 %copy-start.4 = (s32[128,8]{0,1:T(8,128)S(1)}, s32[128,8]{0,1:T(8,128)}, u32[]{:S(2)}) copy-start(s32[128,8]{0,1:T(8,128)} %param.8) | copy-start | bytes 12292
  223.3 15.2 %copy-start.5 = (s32[128,8]{0,1:T(8,128)S(1)}, s32[128,8]{0,1:T(8,128)}, u32[]{:S(2)}) copy-start(s32[128,8]{0,1:T(8,128)} %param.9) | copy-start | bytes 12292
  223.3 89.8 %all-to-all-start.3 = ((bf16[32,24,2048]{2,1,0:T(8,128)(2,1)}), bf16[32,24,2048]{2,1,0:T(8,128)(2,1)}, u32[]{:S(2)}, u32[]{:S(2)}) async-start(bf16[32,24,2048]{2,1,0:T(8,128)(2,1)} %bitcast.26), calls=%async_computation.3 | async-start | bytes 6291456 | tf_op jit(solution)/shard_map/all_to_all | solution.py:96
  232.6 23.0 %collective-permute-start = (f32[2,48,2048]{2,1,0:T(8,128)S(1)}, f32[2,48,2048]{2,1,0:T(8,128)S(1)}, u32[]{:S(2)}, u32[]{:S(2)}) collective-permute-start(f32[2,48,2048]{2,1,0:T(8,128)S(1)} %copy-done.3), channel_id=1, source_target_pairs={{0,256},{128,384},{256,0},{384,128},{1,257},{129,385},{257,1},{385... | collective-permute-start | bytes 2359304 | tf_op jit(solution)/shard_map/ppermute | solution.py:56
  313.1 3.0 copy-start.1
Sparse Core Ops, SparseCore 0:
  71.0 43.4 all-gather.3
  144.5 45.4 all-gather.5
